TPU v7x, 32 devices: a whole 2x2x4 slice. The times are simulated.
32 devices in a mesh: seq: 8 (over y, x, core), fsdp: 4 (over z).
Axes of the slice: x: 2, y: 2, z: 4, core: 2. Of those that a mesh axis runs over, the one named last changes fastest.
Arguments:
- query_states: bfloat16 [2048, 4096], P('seq', 'fsdp'), may hold values from -24 to 24
- key_states: bfloat16 [2048, 4096], P('seq', 'fsdp'), may hold values from -6 to 6
- value_states: bfloat16 [2048, 4096], P('seq', 'fsdp'), may hold values from -6 to 6
- positions: int32 [2048], P('seq'), may hold values from 0 to 2047, as said below
- out_weight: bfloat16 [4096, 5120], P('fsdp', 'seq'), may hold values from -1 to 1
- cotangent: bfloat16 [2048, 5120], P('seq', 'fsdp'), may hold values from -0.59765625 to 0.59765625
Outputs:
- attn_output: float32 [2048, 5120], P('seq', 'fsdp')
- grad_queries: float32 [2048, 4096], P('seq', 'fsdp')
- grad_keys: float32 [2048, 4096], P('seq', 'fsdp')
- grad_values: float32 [2048, 4096], P('seq', 'fsdp')
- grad_weight: float32 [4096, 5120], P('fsdp', 'seq')
Inputs may be any that keep to these rules, and one draw needn't show every extreme that they name: A permutation of 0 to 2047; each aligned block of 256 rows holds, in increasing order, the positions of one residue class modulo 2048 // 256.
All inputs are finite; a program needn't handle non-finite values.
Results may differ from a plain program's by a relative error of at most 0.02.
Values may be sent and summed in bfloat16 or wider, within the bound.
No kernel may reach another device: no remote copies, remote signals or barrier semaphores. Data moves between devices by JAX's collectives and lax.ppermute only.
A program may use at most 128 MiB of HBM per device.

v0:
```python
import jax
import jax.numpy as jnp
from jax import lax
from jax.sharding import PartitionSpec as P

HEAD_DIM = 128


blocked = -1e30


def shifted(block, axis, distance):
    devices = range(lax.axis_size(axis))
    route = [((i - distance) % len(devices), i) for i in devices]
    return lax.ppermute(block, axis, route)


def split_heads(matrix):
    return matrix.reshape(matrix.shape[0], -1, HEAD_DIM)


def masked_scores(query_rows, key_rows, query_pos, key_pos):
    raw = jnp.einsum(
        "qhd,khd->hqk", query_rows, key_rows, preferred_element_type=jnp.float32
    ) * HEAD_DIM ** (-0.5)
    visible = key_pos[None, None, :] <= query_pos[None, :, None]
    return jnp.where(visible, raw, blocked)


def tile_grads(
    query_rows, grad_rows, log_total, row_delta, query_pos, key_rows, value_rows, key_pos
):
    scores = masked_scores(query_rows, key_rows, query_pos, key_pos)
    probs = jnp.exp(scores - log_total[:, :, None])
    grad_probs = jnp.einsum(
        "qhd,khd->hqk", grad_rows, value_rows, preferred_element_type=jnp.float32
    )
    grad_scores = (probs * (grad_probs - row_delta[:, :, None])).astype(jnp.bfloat16)
    grad_query = jnp.einsum(
        "hqk,khd->qhd", grad_scores, key_rows, preferred_element_type=jnp.float32
    )
    grad_key = jnp.einsum(
        "hqk,qhd->khd", grad_scores, query_rows, preferred_element_type=jnp.float32
    )
    grad_value = jnp.einsum(
        "hqk,qhd->khd", probs.astype(jnp.bfloat16), grad_rows, preferred_element_type=jnp.float32
    )
    return (grad_query, grad_key, grad_value)


def shards(query_states, key_states, value_states, positions, out_weight, cotangent):
    local_tokens = query_states.shape[0]
    query_heads = split_heads(query_states)
    key_heads = split_heads(key_states)
    value_heads = split_heads(value_states)
    local_heads = query_heads.shape[1]
    row_max = jnp.full((local_heads, local_tokens), blocked, jnp.float32)
    piece_keys = lax.all_gather(key_states, "seq", axis=0, tiled=True)
    piece_pos = lax.all_gather(positions, "seq", axis=0, tiled=True)
    scores = masked_scores(query_heads, split_heads(piece_keys), positions, piece_pos)
    new_max = jnp.maximum(row_max, jnp.max(scores, axis=2))
    new_total = jnp.sum(jnp.exp(scores - new_max[:, :, None]), axis=2)
    log_total = new_max + jnp.log(new_total)
    zero_heads = jnp.zeros((local_tokens, local_heads, HEAD_DIM), jnp.float32)
    piece_keys = lax.all_gather(key_states, "seq", axis=0, tiled=True)
    piece_values = lax.all_gather(value_states, "seq", axis=0, tiled=True)
    piece_pos = lax.all_gather(positions, "seq", axis=0, tiled=True)
    scores = masked_scores(query_heads, split_heads(piece_keys), positions, piece_pos)
    weights = jnp.exp(scores - log_total[:, :, None]).astype(jnp.bfloat16)
    attended = jnp.einsum(
        "hqk,khd->qhd", weights, split_heads(piece_values), preferred_element_type=jnp.float32
    )
    attended_heads = attended.astype(jnp.bfloat16)
    attended_flat = attended_heads.reshape(local_tokens, local_heads * HEAD_DIM)
    weight_full = lax.all_gather(out_weight, "seq", axis=1, tiled=True)
    partial_sum = jnp.dot(attended_flat, weight_full, preferred_element_type=jnp.float32).astype(
        jnp.bfloat16
    )
    attn_output = lax.psum_scatter(partial_sum, "fsdp", scatter_dimension=1, tiled=True).astype(
        jnp.float32
    )
    cotangent_full = lax.all_gather(cotangent, "fsdp", axis=1, tiled=True)
    grad_attended = jnp.einsum(
        "td,hd->th", cotangent_full, weight_full, preferred_element_type=jnp.float32
    ).astype(jnp.bfloat16)
    weight_term = jnp.einsum(
        "th,td->hd", attended_flat, cotangent_full, preferred_element_type=jnp.float32
    )
    grad_weight = lax.psum_scatter(weight_term, "seq", scatter_dimension=1, tiled=True)
    grad_heads = split_heads(grad_attended)
    row_delta = jnp.sum(
        grad_heads.astype(jnp.float32) * attended_heads.astype(jnp.float32), axis=2
    ).T
    cycle_length = lax.axis_size("seq")

    def key_step(cycle_step, state_tuple):
        key_block, value_block, key_pos, key_grad, value_grad, query_grad = state_tuple
        grad_query, grad_key, grad_value = tile_grads(
            query_heads,
            grad_heads,
            log_total,
            row_delta,
            positions,
            key_block,
            value_block,
            key_pos,
        )
        key_block, value_block, key_pos = shifted((key_block, value_block, key_pos), "seq", 1)
        key_grad, value_grad = shifted((key_grad + grad_key, value_grad + grad_value), "seq", 1)
        return (key_block, value_block, key_pos, key_grad, value_grad, query_grad + grad_query)

    final_state = lax.fori_loop(
        0,
        cycle_length,
        key_step,
        (key_heads, value_heads, positions, zero_heads, zero_heads, zero_heads),
    )
    query_sum, key_sum, value_sum = (final_state[5], final_state[3], final_state[4])
    score_scale = HEAD_DIM ** (-0.5)
    grad_queries = (query_sum * score_scale).reshape(local_tokens, local_heads * HEAD_DIM)
    grad_keys = (key_sum * score_scale).reshape(local_tokens, local_heads * HEAD_DIM)
    grad_values = value_sum.reshape(local_tokens, local_heads * HEAD_DIM)
    return (attn_output, grad_queries, grad_keys, grad_values, grad_weight)


def solution(mesh):
    in_specs = (
        P("seq", "fsdp"),
        P("seq", "fsdp"),
        P("seq", "fsdp"),
        P("seq"),
        P("fsdp", "seq"),
        P("seq", "fsdp"),
    )
    out_specs = (
        P("seq", "fsdp"),
        P("seq", "fsdp"),
        P("seq", "fsdp"),
        P("seq", "fsdp"),
        P("fsdp", "seq"),
    )
    return jax.shard_map(shards, mesh=mesh, in_specs=in_specs, out_specs=out_specs, check_vma=False)
```

profile of v0, /device:TPU:0, one launch (start us, length us, event | category | flops | bytes accessed | tf_op | source)
XLA Modules:
  0.0 683.8 jit_solution(8055189785752940412)
XLA Ops:
  11.6 10.4 %all-gather = s32[8,1,256]{2,1,0:T(1,128)S(1)} all-gather(s32[1,1,256]{2,1,0:T(1,128)S(1)} %bitcast.97), channel_id=1, replica_groups=mesh['seq'=8,'fsdp'=4] {'seq'}, dimensions={0}, use_global_device_ids=true | all-gather | bytes 9216 | tf_op jit(solution)/shard_map/all_gather | solution.py:67
  22.4 26.8 %all-gather.8.cloned.1.call-done = bf16[2048,1024]{1,0:T(8,128)(2,1)} async-done(((bf16[256,1024]{1,0:T(8,128)(2,1)}), bf16[2048,1024]{1,0:T(8,128)(2,1)}) %all-gather.8.cloned.1.call-update) | async-done | bytes 4194320 | tf_op jit(solution)/shard_map/all_gather | solution.py:66
  49.2 6.5 copy.42
  55.7 33.3 %all-gather.6.cloned.1.call-done = bf16[2048,1024]{0,1:T(8,128)(2,1)} async-done(((bf16[256,1024]{0,1:T(8,128)(2,1)}), bf16[2048,1024]{0,1:T(8,128)(2,1)}) %all-gather.6.cloned.1.call-update) | async-done | bytes 4194320 | tf_op jit(solution)/shard_map/all_gather | solution.py:65
  89.0 5.3 fusion.4
  94.3 4.5 exponential_reduce_fusion
  100.5 44.9 %all-gather.12.cloned.1.call-done = bf16[256,5120]{1,0:T(8,128)(2,1)} async-done(((bf16[256,1280]{1,0:T(8,128)(2,1)}), bf16[256,5120]{1,0:T(8,128)(2,1)}) %all-gather.12.cloned.1.call-update) | async-done | bytes 2621456 | tf_op jit(solution)/shard_map/all_gather | solution.py:82
  145.4 63.5 %all-gather.10.cloned.1.call-done = bf16[1024,5120]{1,0:T(8,128)(2,1)} async-done(((bf16[1024,640]{1,0:T(8,128)(2,1)}), bf16[1024,5120]{1,0:T(8,128)(2,1)}) %all-gather.10.cloned.1.call-update) | async-done | bytes 10485776 | tf_op jit(solution)/shard_map/all_gather | solution.py:75
  208.9 8.5 %convolution_convert_fusion.1 = bf16[256,1024]{1,0:T(8,128)(2,1)} fusion(bf16[256,5120]{1,0:T(8,128)(2,1)} %all-gather.12.cloned.1.call-done, bf16[1024,5120]{1,0:T(8,128)(2,1)} %all-gather.10.cloned.1.call-done), kind=kOutput, calls=%fused_computation.18 | convolution fusion | flops 2684616704 | bytes 13631488 | tf_op jit(solution)/shard_map/td,hd->th/dot_general | solution.py:83
  219.6 9.9 %multiply_reduce_fusion = (f32[256,8]{0,1:T(8,128)S(1)}, bf16[8,256,128]{1,2,0:T(8,128)(2,1)S(1)}) fusion(bf16[256,1024]{0,1:T(8,128)(2,1)} %copy.45, bf16[2048,8,128]{0,2,1:T(8,128)(2,1)} %bitcast.89, f32[8,256,2048]{2,1,0:T(8,128)} %copy-done, f32[8,256]{1,0:T(8,128)S(1)} %log_add_fusion, pred[256,2048]{1,0:T(8,128)(4,1)S(1)} %broadcast_compare_fusion.1), kind=kOutput, calls=%fused_computation.24 | convolution fusion | flops 1091827712 | bytes 22560768 | tf_op jit(solution)/shard_map/hqk,khd->qhd/dot_general | solution.py:70
  230.3 4.3 convolution_convert_fusion
  236.3 9.8 %fusion.10 = f32[1024,5120]{1,0:T(8,128)} fusion(bf16[256,1024]{0,1:T(8,128)(2,1)} %bitcast.91, bf16[256,5120]{1,0:T(8,128)(2,1)S(1)} %copy-done.3), kind=kOutput, calls=%fused_computation.30 | convolution fusion | flops 2684354560 | bytes 24117248 | tf_op jit(solution)/shard_map/th,td->hd/dot_general | solution.py:86
  251.9 416.6 %while.21 = (s32[]{:T(128)}, bf16[256,8,128]{2,0,1:T(8,128)(2,1)}, bf16[256,8,128]{2,0,1:T(8,128)(2,1)}, s32[256]{0:T(256)S(1)}, f32[256,8,128]{2,0,1:T(8,128)},...) while((s32[]{:T(128)}, bf16[256,8,128]{2,0,1:T(8,128)(2,1)}, ...), condition=%wide.region_5.6_spmd.clone, body=%wide.region_4.5_spmd.clone.sunk | while | flops 675872768 | bytes 34234708 | solution.py:112
  265.4 30.6 %collective-permute-done.2 = s32[256]{0:T(256)S(1)} collective-permute-done((s32[256]{0:T(256)S(1)}, s32[256]{0:T(256)S(1)}, u32[]{:S(2)}, u32[]{:S(2)}) %collective-permute-start.2) | collective-permute-done | bytes 1056 | tf_op jit(solution)/shard_map/while/body/eval_jaxpr/ppermute | solution.py:15
  311.4 43.0 %collective-permute-done.2 = s32[256]{0:T(256)S(1)} collective-permute-done((s32[256]{0:T(256)S(1)}, s32[256]{0:T(256)S(1)}, u32[]{:S(2)}, u32[]{:S(2)}) %collective-permute-start.2) | collective-permute-done | bytes 1056 | tf_op jit(solution)/shard_map/while/body/eval_jaxpr/ppermute | solution.py:15
  371.1 75.8 %collective-permute-done.2 = s32[256]{0:T(256)S(1)} collective-permute-done((s32[256]{0:T(256)S(1)}, s32[256]{0:T(256)S(1)}, u32[]{:S(2)}, u32[]{:S(2)}) %collective-permute-start.2) | collective-permute-done | bytes 1056 | tf_op jit(solution)/shard_map/while/body/eval_jaxpr/ppermute | solution.py:15
  463.6 28.4 %collective-permute-done.2 = s32[256]{0:T(256)S(1)} collective-permute-done((s32[256]{0:T(256)S(1)}, s32[256]{0:T(256)S(1)}, u32[]{:S(2)}, u32[]{:S(2)}) %collective-permute-start.2) | collective-permute-done | bytes 1056 | tf_op jit(solution)/shard_map/while/body/eval_jaxpr/ppermute | solution.py:15
  501.6 3.5 collective-permute-start.1
  507.7 28.4 %collective-permute-done.2 = s32[256]{0:T(256)S(1)} collective-permute-done((s32[256]{0:T(256)S(1)}, s32[256]{0:T(256)S(1)}, u32[]{:S(2)}, u32[]{:S(2)}) %collective-permute-start.2) | collective-permute-done | bytes 1056 | tf_op jit(solution)/shard_map/while/body/eval_jaxpr/ppermute | solution.py:15
  545.7 3.4 collective-permute-start.1
  551.8 28.4 %collective-permute-done.2 = s32[256]{0:T(256)S(1)} collective-permute-done((s32[256]{0:T(256)S(1)}, s32[256]{0:T(256)S(1)}, u32[]{:S(2)}, u32[]{:S(2)}) %collective-permute-start.2) | collective-permute-done | bytes 1056 | tf_op jit(solution)/shard_map/while/body/eval_jaxpr/ppermute | solution.py:15
  595.9 28.4 %collective-permute-done.2 = s32[256]{0:T(256)S(1)} collective-permute-done((s32[256]{0:T(256)S(1)}, s32[256]{0:T(256)S(1)}, u32[]{:S(2)}, u32[]{:S(2)}) %collective-permute-start.2) | collective-permute-done | bytes 1056 | tf_op jit(solution)/shard_map/while/body/eval_jaxpr/ppermute | solution.py:15
  633.9 3.4 collective-permute-start.1
  640.0 28.4 %collective-permute-done.2 = s32[256]{0:T(256)S(1)} collective-permute-done((s32[256]{0:T(256)S(1)}, s32[256]{0:T(256)S(1)}, u32[]{:S(2)}, u32[]{:S(2)}) %collective-permute-start.2) | collective-permute-done | bytes 1056 | tf_op jit(solution)/shard_map/while/body/eval_jaxpr/ppermute | solution.py:15
  (198 shorter events, 139.5 us)
Async XLA Ops:
  7.2 42.0 %all-gather.8.cloned.1.call-start = ((), (), s32[]{:S(2)}) async-start(), calls=%async_computation.3 | async-start | bytes 4718592 | tf_op jit(solution)/shard_map/all_gather | solution.py:66
  7.9 81.1 %all-gather.6.cloned.1.call-start = ((), (), s32[]{:S(2)}) async-start(), calls=%async_computation.2 | async-start | bytes 4718592 | tf_op jit(solution)/shard_map/all_gather | solution.py:65
  10.0 135.4 %all-gather.12.cloned.1.call-start = ((), (), s32[]{:S(2)}) async-start(), calls=%async_computation.6 | async-start | bytes 3276800 | tf_op jit(solution)/shard_map/all_gather | solution.py:82
  10.8 198.2 %all-gather.10.cloned.1.call-start = ((), (), s32[]{:S(2)}) async-start(), calls=%async_computation.4 | async-start | bytes 11796480 | tf_op jit(solution)/shard_map/all_gather | solution.py:75
  11.3 663.4 %reduce-scatter.3.cloned.1.call-start = ((), (), s32[]{:S(2)}) async-start(), calls=%async_computation.5 | async-start | bytes 3276800 | tf_op jit(solution)/shard_map/reduce_scatter | solution.py:79
  234.6 442.4 %reduce-scatter.5.cloned.1.call-start = ((), (), s32[]{:S(2)}) async-start(), calls=%async_computation.7 | async-start | bytes 23592960 | tf_op jit(solution)/shard_map/reduce_scatter | solution.py:89
  258.1 37.9 %collective-permute-start.3 = (f32[256,8,128]{2,0,1:T(8,128)}, f32[256,8,128]{2,0,1:T(8,128)}, u32[]{:S(2)}, u32[]{:S(2)}) collective-permute-start(f32[256,8,128]{2,0,1:T(8,128)} %fusion.53), channel_id=1, source_target_pairs={{28,0},{0,4},{4,8},{8,12},{12,16},{16,20},{20,24},{24,28},{29,1},{... | collective-permute-start | bytes 3145736 | tf_op jit(solution)/shard_map/while/body/eval_jaxpr/ppermute | solution.py:15
  302.4 52.0 %collective-permute-start.3 = (f32[256,8,128]{2,0,1:T(8,128)}, f32[256,8,128]{2,0,1:T(8,128)}, u32[]{:S(2)}, u32[]{:S(2)}) collective-permute-start(f32[256,8,128]{2,0,1:T(8,128)} %fusion.53), channel_id=1, source_target_pairs={{28,0},{0,4},{4,8},{8,12},{12,16},{16,20},{20,24},{24,28},{29,1},{... | collective-permute-start | bytes 3145736 | tf_op jit(solution)/shard_map/while/body/eval_jaxpr/ppermute | solution.py:15
  305.4 49.0 %collective-permute-start.4 = (f32[256,8,128]{2,0,1:T(8,128)}, f32[256,8,128]{2,0,1:T(8,128)}, u32[]{:S(2)}, u32[]{:S(2)}) collective-permute-start(f32[256,8,128]{2,0,1:T(8,128)} %fusion.54), channel_id=1, source_target_pairs={{28,0},{0,4},{4,8},{8,12},{12,16},{16,20},{20,24},{24,28},{29,1},{... | collective-permute-start | bytes 3145736 | tf_op jit(solution)/shard_map/while/body/eval_jaxpr/ppermute | solution.py:15
  306.3 48.0 %collective-permute-start = (bf16[256,8,128]{2,0,1:T(8,128)(2,1)S(1)}, bf16[256,8,128]{2,0,1:T(8,128)(2,1)}, u32[]{:S(2)}, u32[]{:S(2)}) collective-permute-start(bf16[256,8,128]{2,0,1:T(8,128)(2,1)S(1)} %copy.73), channel_id=1, source_target_pairs={{28,0},{0,4},{4,8},{8,12},{12,16},{16,20},{20,24},{24,28},{29,1},{... | collective-permute-start | bytes 1572872 | tf_op jit(solution)/shard_map/while/body/eval_jaxpr/ppermute | solution.py:15
  306.4 48.0 %collective-permute-start.1 = (bf16[256,8,128]{2,0,1:T(8,128)(2,1)S(1)}, bf16[256,8,128]{2,0,1:T(8,128)(2,1)}, u32[]{:S(2)}, u32[]{:S(2)}) collective-permute-start(bf16[256,8,128]{2,0,1:T(8,128)(2,1)S(1)} %copy.74), channel_id=1, source_target_pairs={{28,0},{0,4},{4,8},{8,12},{12,16},{16,20},{20,24},{24,28},{29,1},{... | collective-permute-start | bytes 1572872 | tf_op jit(solution)/shard_map/while/body/eval_jaxpr/ppermute | solution.py:15
  308.5 45.9 %collective-permute-start.2 = (s32[256]{0:T(256)S(1)}, s32[256]{0:T(256)S(1)}, u32[]{:S(2)}, u32[]{:S(2)}) collective-permute-start(s32[256]{0:T(256)S(1)} %copy.75), channel_id=1, source_target_pairs={{28,0},{0,4},{4,8},{8,12},{12,16},{16,20},{20,24},{24,28},{29,1},{... | collective-permute-start | bytes 3080 | tf_op jit(solution)/shard_map/while/body/eval_jaxpr/ppermute | solution.py:15
  360.7 86.3 %collective-permute-start.3 = (f32[256,8,128]{2,0,1:T(8,128)}, f32[256,8,128]{2,0,1:T(8,128)}, u32[]{:S(2)}, u32[]{:S(2)}) collective-permute-start(f32[256,8,128]{2,0,1:T(8,128)} %fusion.53), channel_id=1, source_target_pairs={{28,0},{0,4},{4,8},{8,12},{12,16},{16,20},{20,24},{24,28},{29,1},{... | collective-permute-start | bytes 3145736 | tf_op jit(solution)/shard_map/while/body/eval_jaxpr/ppermute | solution.py:15
  363.4 83.6 %collective-permute-start.4 = (f32[256,8,128]{2,0,1:T(8,128)}, f32[256,8,128]{2,0,1:T(8,128)}, u32[]{:S(2)}, u32[]{:S(2)}) collective-permute-start(f32[256,8,128]{2,0,1:T(8,128)} %fusion.54), channel_id=1, source_target_pairs={{28,0},{0,4},{4,8},{8,12},{12,16},{16,20},{20,24},{24,28},{29,1},{... | collective-permute-start | bytes 3145736 | tf_op jit(solution)/shard_map/while/body/eval_jaxpr/ppermute | solution.py:15
  364.7 82.3 %collective-permute-start = (bf16[256,8,128]{2,0,1:T(8,128)(2,1)S(1)}, bf16[256,8,128]{2,0,1:T(8,128)(2,1)}, u32[]{:S(2)}, u32[]{:S(2)}) collective-permute-start(bf16[256,8,128]{2,0,1:T(8,128)(2,1)S(1)} %copy.73), channel_id=1, source_target_pairs={{28,0},{0,4},{4,8},{8,12},{12,16},{16,20},{20,24},{24,28},{29,1},{... | collective-permute-start | bytes 1572872 | tf_op jit(solution)/shard_map/while/body/eval_jaxpr/ppermute | solution.py:15
  365.1 81.9 %collective-permute-start.1 = (bf16[256,8,128]{2,0,1:T(8,128)(2,1)S(1)}, bf16[256,8,128]{2,0,1:T(8,128)(2,1)}, u32[]{:S(2)}, u32[]{:S(2)}) collective-permute-start(bf16[256,8,128]{2,0,1:T(8,128)(2,1)S(1)} %copy.74), channel_id=1, source_target_pairs={{28,0},{0,4},{4,8},{8,12},{12,16},{16,20},{20,24},{24,28},{29,1},{... | collective-permute-start | bytes 1572872 | tf_op jit(solution)/shard_map/while/body/eval_jaxpr/ppermute | solution.py:15
  368.5 78.5 %collective-permute-start.2 = (s32[256]{0:T(256)S(1)}, s32[256]{0:T(256)S(1)}, u32[]{:S(2)}, u32[]{:S(2)}) collective-permute-start(s32[256]{0:T(256)S(1)} %copy.75), channel_id=1, source_target_pairs={{28,0},{0,4},{4,8},{8,12},{12,16},{16,20},{20,24},{24,28},{29,1},{... | collective-permute-start | bytes 3080 | tf_op jit(solution)/shard_map/while/body/eval_jaxpr/ppermute | solution.py:15
  453.2 38.9 %collective-permute-start.3 = (f32[256,8,128]{2,0,1:T(8,128)}, f32[256,8,128]{2,0,1:T(8,128)}, u32[]{:S(2)}, u32[]{:S(2)}) collective-permute-start(f32[256,8,128]{2,0,1:T(8,128)} %fusion.53), channel_id=1, source_target_pairs={{28,0},{0,4},{4,8},{8,12},{12,16},{16,20},{20,24},{24,28},{29,1},{... | collective-permute-start | bytes 3145736 | tf_op jit(solution)/shard_map/while/body/eval_jaxpr/ppermute | solution.py:15
  455.9 36.2 %collective-permute-start.4 = (f32[256,8,128]{2,0,1:T(8,128)}, f32[256,8,128]{2,0,1:T(8,128)}, u32[]{:S(2)}, u32[]{:S(2)}) collective-permute-start(f32[256,8,128]{2,0,1:T(8,128)} %fusion.54), channel_id=1, source_target_pairs={{28,0},{0,4},{4,8},{8,12},{12,16},{16,20},{20,24},{24,28},{29,1},{... | collective-permute-start | bytes 3145736 | tf_op jit(solution)/shard_map/while/body/eval_jaxpr/ppermute | solution.py:15
  498.2 37.9 %collective-permute-start.3 = (f32[256,8,128]{2,0,1:T(8,128)}, f32[256,8,128]{2,0,1:T(8,128)}, u32[]{:S(2)}, u32[]{:S(2)}) collective-permute-start(f32[256,8,128]{2,0,1:T(8,128)} %fusion.53), channel_id=1, source_target_pairs={{28,0},{0,4},{4,8},{8,12},{12,16},{16,20},{20,24},{24,28},{29,1},{... | collective-permute-start | bytes 3145736 | tf_op jit(solution)/shard_map/while/body/eval_jaxpr/ppermute | solution.py:15
  542.3 37.9 %collective-permute-start.3 = (f32[256,8,128]{2,0,1:T(8,128)}, f32[256,8,128]{2,0,1:T(8,128)}, u32[]{:S(2)}, u32[]{:S(2)}) collective-permute-start(f32[256,8,128]{2,0,1:T(8,128)} %fusion.53), channel_id=1, source_target_pairs={{28,0},{0,4},{4,8},{8,12},{12,16},{16,20},{20,24},{24,28},{29,1},{... | collective-permute-start | bytes 3145736 | tf_op jit(solution)/shard_map/while/body/eval_jaxpr/ppermute | solution.py:15
  586.4 37.9 %collective-permute-start.3 = (f32[256,8,128]{2,0,1:T(8,128)}, f32[256,8,128]{2,0,1:T(8,128)}, u32[]{:S(2)}, u32[]{:S(2)}) collective-permute-start(f32[256,8,128]{2,0,1:T(8,128)} %fusion.53), channel_id=1, source_target_pairs={{28,0},{0,4},{4,8},{8,12},{12,16},{16,20},{20,24},{24,28},{29,1},{... | collective-permute-start | bytes 3145736 | tf_op jit(solution)/shard_map/while/body/eval_jaxpr/ppermute | solution.py:15
  589.2 35.2 %collective-permute-start.4 = (f32[256,8,128]{2,0,1:T(8,128)}, f32[256,8,128]{2,0,1:T(8,128)}, u32[]{:S(2)}, u32[]{:S(2)}) collective-permute-start(f32[256,8,128]{2,0,1:T(8,128)} %fusion.54), channel_id=1, source_target_pairs={{28,0},{0,4},{4,8},{8,12},{12,16},{16,20},{20,24},{24,28},{29,1},{... | collective-permute-start | bytes 3145736 | tf_op jit(solution)/shard_map/while/body/eval_jaxpr/ppermute | solution.py:15
  630.5 37.9 %collective-permute-start.3 = (f32[256,8,128]{2,0,1:T(8,128)}, f32[256,8,128]{2,0,1:T(8,128)}, u32[]{:S(2)}, u32[]{:S(2)}) collective-permute-start(f32[256,8,128]{2,0,1:T(8,128)} %fusion.53), channel_id=1, source_target_pairs={{28,0},{0,4},{4,8},{8,12},{12,16},{16,20},{20,24},{24,28},{29,1},{... | collective-permute-start | bytes 3145736 | tf_op jit(solution)/shard_map/while/body/eval_jaxpr/ppermute | solution.py:15
  (33 other events, 800.6 us)
Sparse Core Ops, SparseCore 0:
  9.9 39.2 all-gather.7
  51.7 37.3 all-gather.5
  90.6 54.7 all-gather.11
  147.2 61.7 all-gather.9
  234.7 52.2 reduce-scatter.2
  291.1 169.2 reduce-scatter.4
where the time goes:
time: 686 us; the launch traced here: 684 us
  waiting for transfers between devices  462 us (67%)
  matrix products  111 us (16%)
  local copies, waits for them, and re-layouts  41.9 us (6%)
  starting transfers between devices  33.5 us (5%)
  between operations  14.3 us (2%)
  blocking collectives  10.4 us (2%)
  other arithmetic  9.66 us (1%)
    ppermute x40, waiting for transfers between devices, shifted(): return lax.ppermute(block, axis, route)  292 us
    all_gather x1, waiting for transfers between devices, shards(): weight_full = lax.all_gather(out_weight, 'seq', axis=1, tiled=True)  63.5 us
    all_gather x1, waiting for transfers between devices, shards(): cotangent_full = lax.all_gather(cotangent, 'fsdp', axis=1, tiled=True)  44.9 us
    all_gather x1, waiting for transfers between devices, shards(): piece_keys = lax.all_gather(key_states, 'seq', axis=0, tiled=True)  33.3 us
    ppermute x40, starting transfers between devices, shifted(): return lax.ppermute(block, axis, route)  33.1 us
    all_gather x1, waiting for transfers between devices, shards(): piece_values = lax.all_gather(value_states, 'seq', axis=0, tiled=True)  26.8 us
    dot_general x8, matrix products, tile_grads(): jnp.einsum('hqk,qhd->khd', probs.astype(jnp.bfloat16), grad_rows, preferr...  22 us
    dot_general x8, matrix products, tile_grads(): jnp.einsum('hqk,qhd->khd', grad_scores, query_rows, preferred_element_typ...  21.7 us
  transfers between devices with their start and end apart: 46, of which 12 were waited for; matrix products, arithmetic and copies ran while one was open for 20% of the time, Pallas kernels for 0%

commit v1 on v0

v1 whole, which is shorter than its diff:
```python
import jax
import jax.numpy as jnp
from jax import lax
from jax.sharding import PartitionSpec as P

HEAD_DIM = 128


blocked = -1e30


def split_heads(matrix):
    return matrix.reshape(matrix.shape[0], -1, HEAD_DIM)


def masked_scores(query_rows, key_rows, query_pos, key_pos):
    raw = jnp.einsum(
        "qhd,khd->hqk", query_rows, key_rows, preferred_element_type=jnp.float32
    ) * HEAD_DIM ** (-0.5)
    visible = key_pos[None, None, :] <= query_pos[None, :, None]
    return jnp.where(visible, raw, blocked)


def shards(query_states, key_states, value_states, positions, out_weight, cotangent):
    local_tokens = query_states.shape[0]
    query_heads = split_heads(query_states)
    local_heads = query_heads.shape[1]
    all_keys = lax.all_gather(key_states, "seq", axis=0, tiled=True)
    all_values = lax.all_gather(value_states, "seq", axis=0, tiled=True)
    all_pos = lax.all_gather(positions, "seq", axis=0, tiled=True)
    key_heads = split_heads(all_keys)
    value_heads = split_heads(all_values)
    scores = masked_scores(query_heads, key_heads, positions, all_pos)
    row_max = jnp.max(scores, axis=2)
    log_total = row_max + jnp.log(jnp.sum(jnp.exp(scores - row_max[:, :, None]), axis=2))
    probs = jnp.exp(scores - log_total[:, :, None])
    weights = probs.astype(jnp.bfloat16)
    attended = jnp.einsum(
        "hqk,khd->qhd", weights, value_heads, preferred_element_type=jnp.float32
    )
    attended_heads = attended.astype(jnp.bfloat16)
    attended_flat = attended_heads.reshape(local_tokens, local_heads * HEAD_DIM)
    weight_full = lax.all_gather(out_weight, "seq", axis=1, tiled=True)
    partial_sum = jnp.dot(attended_flat, weight_full, preferred_element_type=jnp.float32).astype(
        jnp.bfloat16
    )
    attn_output = lax.psum_scatter(partial_sum, "fsdp", scatter_dimension=1, tiled=True).astype(
        jnp.float32
    )
    cotangent_full = lax.all_gather(cotangent, "fsdp", axis=1, tiled=True)
    grad_attended = jnp.einsum(
        "td,hd->th", cotangent_full, weight_full, preferred_element_type=jnp.float32
    ).astype(jnp.bfloat16)
    all_attended = lax.all_gather(attended_flat, "seq", axis=0, tiled=True)
    cotangent_cols = lax.all_to_all(cotangent_full, "seq", 1, 0, tiled=True)
    grad_weight = jnp.einsum(
        "th,td->hd", all_attended, cotangent_cols, preferred_element_type=jnp.float32
    )
    grad_heads = split_heads(grad_attended)
    row_delta = jnp.sum(
        grad_heads.astype(jnp.float32) * attended_heads.astype(jnp.float32), axis=2
    ).T
    grad_probs = jnp.einsum(
        "qhd,khd->hqk", grad_heads, value_heads, preferred_element_type=jnp.float32
    )
    grad_scores = (probs * (grad_probs - row_delta[:, :, None])).astype(jnp.bfloat16)
    query_sum = jnp.einsum(
        "hqk,khd->qhd", grad_scores, key_heads, preferred_element_type=jnp.float32
    )
    key_part = jnp.einsum(
        "hqk,qhd->khd", grad_scores, query_heads, preferred_element_type=jnp.float32
    )
    value_part = jnp.einsum(
        "hqk,qhd->khd", weights, grad_heads, preferred_element_type=jnp.float32
    )
    key_sum = lax.psum_scatter(key_part, "seq", scatter_dimension=0, tiled=True)
    value_sum = lax.psum_scatter(value_part, "seq", scatter_dimension=0, tiled=True)
    score_scale = HEAD_DIM ** (-0.5)
    grad_queries = (query_sum * score_scale).reshape(local_tokens, local_heads * HEAD_DIM)
    grad_keys = (key_sum * score_scale).reshape(local_tokens, local_heads * HEAD_DIM)
    grad_values = value_sum.reshape(local_tokens, local_heads * HEAD_DIM)
    return (attn_output, grad_queries, grad_keys, grad_values, grad_weight)


def solution(mesh):
    in_specs = (
        P("seq", "fsdp"),
        P("seq", "fsdp"),
        P("seq", "fsdp"),
        P("seq"),
        P("fsdp", "seq"),
        P("seq", "fsdp"),
    )
    out_specs = (
        P("seq", "fsdp"),
        P("seq", "fsdp"),
        P("seq", "fsdp"),
        P("seq", "fsdp"),
        P("fsdp", "seq"),
    )
    return jax.shard_map(shards, mesh=mesh, in_specs=in_specs, out_specs=out_specs, check_vma=False)
```

time: 686 us -> 489 us (0.71)
  waiting for transfers between devices: 462 us -> 316 us
  blocking collectives: 10.4 us -> 48.6 us
  matrix products: 111 us -> 74.1 us
  starting transfers between devices: 33.5 us -> 0.5 us
  local copies, waits for them, and re-layouts: 41.9 us -> 25.2 us
    ppermute x40 -> x0, waiting for transfers between devices: 292 us -> none  [shifted(): return lax.ppermute(block, axis, route)]
    reduce_scatter x1 -> x2, waiting for transfers between devices: 0.01 us -> 140 us  [the longest x1 71.8 us: shards(): lax.psum_scatter(value_part, 'seq', scatter_dimension=0, tiled=True)]
    all_to_all x0 -> x1, blocking collectives: none -> 38.1 us  [shards(): cotangent_cols = lax.all_to_all(cotangent_full, 'seq', 1, 0, tiled=True)]
    dot_general x34 -> x6, matrix products: 87 us -> 52.7 us  [the longest x1 11.1 us: shards(): jnp.einsum('qhd,khd->hqk', grad_heads, value_heads, preferred_element_typ...]
    ppermute x40 -> x0, starting transfers between devices: 33.1 us -> none  [shifted(): return lax.ppermute(block, axis, route)]
    while x24 -> x0, local copies, waits for them, and re-layouts: 16.8 us -> none
    unnamed x30 -> x15, local copies, waits for them, and re-layouts: 9.72 us -> 15.5 us
    all_gather x2 -> x3, waiting for transfers between devices: 60.2 us -> 65.7 us  [the longest x1 33.3 us: shards(): all_keys = lax.all_gather(key_states, 'seq', axis=0, tiled=True)]
  transfers between devices with their start and end apart: 46 -> 8, of which waited for: 12 -> 7; matrix products, arithmetic and copies ran while one was open for 20% -> 15% of each run, Pallas kernels for 0% -> 0%
where the time goes in v1:
time: 489 us; the launch traced here: 488 us
  waiting for transfers between devices  316 us (65%)
  matrix products  74.1 us (15%)
  blocking collectives  48.6 us (10%)
  local copies, waits for them, and re-layouts  25.2 us (5%)
  between operations  14.2 us (3%)
  other arithmetic  9.09 us (2%)
    reduce_scatter x1, waiting for transfers between devices, shards(): lax.psum_scatter(value_part, 'seq', scatter_dimension=0, tiled=True)  71.8 us
    reduce_scatter x1, waiting for transfers between devices, shards(): key_sum = lax.psum_scatter(key_part, 'seq', scatter_dimension=0, tiled=True)  67.8 us
    all_gather x1, waiting for transfers between devices, shards(): weight_full = lax.all_gather(out_weight, 'seq', axis=1, tiled=True)  63.5 us
    all_gather x1, waiting for transfers between devices, shards(): cotangent_full = lax.all_gather(cotangent, 'fsdp', axis=1, tiled=True)  45.4 us
    all_to_all x1, blocking collectives, shards(): cotangent_cols = lax.all_to_all(cotangent_full, 'seq', 1, 0, tiled=True)  38.1 us
    all_gather x1, waiting for transfers between devices, shards(): all_keys = lax.all_gather(key_states, 'seq', axis=0, tiled=True)  33.3 us
    all_gather x1, waiting for transfers between devices, shards(): all_values = lax.all_gather(value_states, 'seq', axis=0, tiled=True)  24.7 us
    unnamed x15, local copies, waits for them, and re-layouts  15.5 us
  transfers between devices with their start and end apart: 8, of which 7 were waited for; matrix products, arithmetic and copies ran while one was open for 15% of the time, Pallas kernels for 0%

profile of v1, /device:TPU:0, one launch (start us, length us, event | category | flops | bytes accessed | tf_op | source)
XLA Modules:
  0.0 487.9 jit_solution(822385104639132643)
XLA Ops:
  12.9 10.6 %all-gather = s32[8,1,256]{2,1,0:T(1,128)S(1)} all-gather(s32[1,1,256]{2,1,0:T(1,128)} %bitcast.66), channel_id=1, replica_groups=mesh['seq'=8,'fsdp'=4] {'seq'}, dimensions={0}, use_global_device_ids=true | all-gather | bytes 9216 | tf_op jit(solution)/shard_map/all_gather | solution.py:30
  24.5 24.7 %all-gather.9.cloned.1.call-done = bf16[2048,1024]{1,0:T(8,128)(2,1)} async-done(((bf16[256,1024]{1,0:T(8,128)(2,1)}), bf16[2048,1024]{1,0:T(8,128)(2,1)}) %all-gather.9.cloned.1.call-update) | async-done | bytes 4194320 | tf_op jit(solution)/shard_map/all_gather | solution.py:29
  49.2 6.5 %copy.52 = bf16[2048,1024]{0,1:T(8,128)(2,1)} copy(bf16[2048,1024]{1,0:T(8,128)(2,1)} %all-gather.9.cloned.1.call-done) | data formatting | bytes 8388608 | tf_op jit(solution)/shard_map/all_gather | solution.py:29
  55.8 33.3 %all-gather.7.cloned.1.call-done = bf16[2048,1024]{0,1:T(8,128)(2,1)} async-done(((bf16[256,1024]{0,1:T(8,128)(2,1)}), bf16[2048,1024]{0,1:T(8,128)(2,1)}) %all-gather.7.cloned.1.call-update) | async-done | bytes 4194320 | tf_op jit(solution)/shard_map/all_gather | solution.py:28
  89.0 5.3 %fusion.1 = (f32[8,256]{1,0:T(8,128)S(1)}, f32[8,256,2048]{2,1,0:T(8,128)S(1)}) fusion(pred[256,2048]{1,0:T(8,128)(4,1)S(1)} %broadcast_compare_fusion, bf16[2048,8,128]{0,2,1:T(8,128)(2,1)} %bitcast.51, bf16[256,1024]{1,0:T(8,128)(2,1)S(1)} %copy-done), kind=kOutput, calls=%fused_computation.5 | convolution fusion | flops 1086322688 | bytes 22028288 | tf_op jit(solution)/shard_map/qhd,khd->hqk/dot_general | solution.py:17
  94.3 4.5 exponential_reduce_fusion
  100.5 45.4 %all-gather.13.cloned.1.call-done = bf16[256,5120]{0,1:T(8,128)(2,1)} async-done(((bf16[256,1280]{0,1:T(8,128)(2,1)}), bf16[256,5120]{0,1:T(8,128)(2,1)}) %all-gather.13.cloned.1.call-update) | async-done | bytes 2621456 | tf_op jit(solution)/shard_map/all_gather | solution.py:50
  146.0 63.5 %all-gather.11.cloned.1.call-done = bf16[1024,5120]{1,0:T(8,128)(2,1)} async-done(((bf16[1024,640]{1,0:T(8,128)(2,1)}), bf16[1024,5120]{1,0:T(8,128)(2,1)}) %all-gather.11.cloned.1.call-update) | async-done | bytes 10485776 | tf_op jit(solution)/shard_map/all_gather | solution.py:43
  209.5 7.7 %convolution_convert_fusion.1 = bf16[256,1024]{1,0:T(8,128)(2,1)S(1)} fusion(bf16[256,5120]{0,1:T(8,128)(2,1)} %all-gather.13.cloned.1.call-done, bf16[1024,5120]{1,0:T(8,128)(2,1)} %all-gather.11.cloned.1.call-done), kind=kOutput, calls=%fused_computation.10 | convolution fusion | flops 2684616704 | bytes 13631488 | tf_op jit(solution)/shard_map/td,hd->th/dot_general | solution.py:51
  217.4 9.7 %multiply_reduce_fusion = (f32[256,8]{0,1:T(8,128)S(1)}, bf16[8,256,128]{1,2,0:T(8,128)(2,1)S(1)}) fusion(bf16[256,1024]{0,1:T(8,128)(2,1)S(1)} %copy.54, bf16[2048,8,128]{0,2,1:T(8,128)(2,1)} %bitcast.54, f32[8,256,2048]{2,1,0:T(8,128)} %copy-done.1, f32[8,256]{1,0:T(8,128)S(1)} %log_add_fusion, pred[256,2048]{1,0:T(8,128)(4,1)S(1)} %broadcast_compare_fusion), kind=kOutput, calls=%fused_computation.12 | convolution fusion | flops 1091827712 | bytes 22560768 | tf_op jit(solution)/shard_map/hqk,khd->qhd/dot_general | solution.py:38
  227.1 8.4 %convolution_convert_fusion = bf16[256,5120]{1,0:T(8,128)(2,1)} fusion(bf16[256,1024]{0,1:T(8,128)(2,1)S(1)} %bitcast.57, bf16[1024,5120]{1,0:T(8,128)(2,1)} %all-gather.11.cloned.1.call-done), kind=kOutput, calls=%fused_computation.6 | convolution fusion | flops 2685665280 | bytes 13631488 | tf_op jit(solution)/shard_map/dot_general | solution.py:44
  236.4 11.1 %multiply_convert_fusion = bf16[8,256,2048]{2,1,0:T(8,128)(2,1)S(1)} fusion(f32[8,256,2048]{2,1,0:T(8,128)} %copy-done.1, f32[8,256]{1,0:T(8,128)S(1)} %bitcast.67, f32[8,256]{1,0:T(8,128)S(1)} %log_add_fusion, pred[256,2048]{1,0:T(8,128)(4,1)S(1)} %broadcast_compare_fusion, bf16[256,8,128]{0,2,1:T(8,128)(2,1)S(1)} %bitcast.61, bf16[2048,8,128]{0,2,1:T(8,128)(2,1)} %bitcast.55), kind=kOutput, calls=%fused_computation | convolution fusion | flops 1098907648 | bytes 30425088 | tf_op jit(solution)/shard_map/qhd,khd->hqk/dot_general | solution.py:63
  247.5 3.2 copy-done.2
  250.7 6.0 %convolution_bitcast_fusion.1 = f32[2048,8,128]{2,0,1:T(8,128)} fusion(bf16[8,256,2048]{2,1,0:T(8,128)(2,1)S(1)} %multiply_convert_fusion, bf16[256,1024]{1,0:T(8,128)(2,1)S(1)} %copy-done), kind=kOutput, calls=%fused_computation.8 | convolution fusion | flops 1073741824 | bytes 17301504 | tf_op jit(solution)/shard_map/hqk,qhd->khd/dot_general | solution.py:70
  256.8 10.3 %convolution_bitcast_fusion = f32[2048,8,128]{0,2,1:T(8,128)} fusion(bf16[256,8,128]{0,2,1:T(8,128)(2,1)S(1)} %bitcast.62, f32[8,256,2048]{2,1,0:T(8,128)} %copy-done.1, f32[8,256]{1,0:T(8,128)S(1)} %log_add_fusion, pred[256,2048]{1,0:T(8,128)(4,1)S(1)} %broadcast_compare_fusion), kind=kOutput, calls=%fused_computation.7 | convolution fusion | flops 1090519040 | bytes 26222592 | tf_op jit(solution)/shard_map/hqk,qhd->khd/dot_general | solution.py:73
  267.0 38.1 %all_to_all.19 = bf16[256,8,640]{0,2,1:T(8,128)(2,1)S(1)} all-to-all(bf16[256,8,640]{0,2,1:T(8,128)(2,1)} %bitcast.59), channel_id=1, replica_groups=mesh['seq'=8,'fsdp'=4] {'seq'}, dimensions={1} | all-to-all | bytes 5242880 | tf_op jit(solution)/shard_map/all_to_all | solution.py:55
  305.1 2.6 copy.60
  307.7 8.6 %convolution_multiply_fusion = f32[8,256,128]{1,2,0:T(8,128)} fusion(bf16[8,256,2048]{2,1,0:T(8,128)(2,1)} %copy-done.2, bf16[2048,8,128]{0,2,1:T(8,128)(2,1)} %bitcast.52), kind=kOutput, calls=%fused_computation.9 | convolution fusion | flops 1074003968 | bytes 13631488 | tf_op jit(solution)/shard_map/hqk,khd->qhd/dot_general | solution.py:67
  316.3 2.5 copy.61
  321.1 7.7 %all-gather.15.cloned.1.call-done = bf16[2048,1024]{0,1:T(8,128)(2,1)} async-done(((bf16[256,1024]{0,1:T(8,128)(2,1)}), bf16[2048,1024]{0,1:T(8,128)(2,1)}) %all-gather.15.cloned.1.call-update) | async-done | bytes 4194320 | tf_op jit(solution)/shard_map/all_gather | solution.py:54
  328.8 7.1 %fusion.9 = f32[1024,640]{1,0:T(8,128)} fusion(bf16[2048,1024]{0,1:T(8,128)(2,1)} %all-gather.15.cloned.1.call-done, bf16[2048,640]{1,0:T(8,128)(2,1)S(1)} %bitcast.60), kind=kOutput, calls=%fused_computation.21 | convolution fusion | flops 2684354560 | bytes 9437184 | tf_op jit(solution)/shard_map/th,td->hd/dot_general | solution.py:56
  335.9 67.8 %reduce-scatter.6.cloned.1.call-done = f32[256,8,128]{2,0,1:T(8,128)} async-done(((f32[2048,8,128]{2,0,1:T(8,128)}), f32[256,8,128]{2,0,1:T(8,128)}) %reduce-scatter.6.cloned.1.call-update) | async-done | bytes 1048592 | tf_op jit(solution)/shard_map/reduce_scatter | solution.py:76
  406.7 71.8 %reduce-scatter.8.cloned.1.call-done = f32[256,8,128]{0,2,1:T(8,128)} async-done(((f32[2048,8,128]{0,2,1:T(8,128)}), f32[256,8,128]{0,2,1:T(8,128)}) %reduce-scatter.8.cloned.1.call-update) | async-done | bytes 1048592 | tf_op jit(solution)/shard_map/reduce_scatter | solution.py:77
  478.5 2.5 copy.63
  (35 shorter events, 14.7 us)
Async XLA Ops:
  7.2 81.9 %copy-start = (bf16[256,1024]{1,0:T(8,128)(2,1)S(1)}, bf16[256,1024]{1,0:T(8,128)(2,1)}, u32[]{:S(2)}) copy-start(bf16[256,1024]{1,0:T(8,128)(2,1)} %param.6) | copy-start | bytes 1572868
  7.2 42.0 %all-gather.9.cloned.1.call-start = ((), (), s32[]{:S(2)}) async-start(), calls=%async_computation.5 | async-start | bytes 4718592 | tf_op jit(solution)/shard_map/all_gather | solution.py:29
  7.9 81.1 %all-gather.7.cloned.1.call-start = ((), (), s32[]{:S(2)}) async-start(), calls=%async_computation.4 | async-start | bytes 4718592 | tf_op jit(solution)/shard_map/all_gather | solution.py:28
  10.0 135.9 %all-gather.13.cloned.1.call-start = ((), (), s32[]{:S(2)}) async-start(), calls=%async_computation.8 | async-start | bytes 3276800 | tf_op jit(solution)/shard_map/all_gather | solution.py:50
  12.3 197.2 %all-gather.11.cloned.1.call-start = ((), (), s32[]{:S(2)}) async-start(), calls=%async_computation.6 | async-start | bytes 11796480 | tf_op jit(solution)/shard_map/all_gather | solution.py:43
  12.8 306.0 %reduce-scatter.4.cloned.1.call-start = ((), (), s32[]{:S(2)}) async-start(), calls=%async_computation.7 | async-start | bytes 3276800 | tf_op jit(solution)/shard_map/reduce_scatter | solution.py:47
  94.3 6.2 %copy-start.1 = (f32[8,256,2048]{2,1,0:T(8,128)}, f32[8,256,2048]{2,1,0:T(8,128)S(1)}, u32[]{:S(2)}) copy-start(f32[8,256,2048]{2,1,0:T(8,128)S(1)} %get-tuple-element.26) | copy-start | bytes 50331652
  227.1 8.4 %copy-start.3 = (bf16[8,256,128]{1,2,0:T(8,128)(2,1)}, bf16[8,256,128]{1,2,0:T(8,128)(2,1)S(1)}, u32[]{:S(2)}) copy-start(bf16[8,256,128]{1,2,0:T(8,128)(2,1)S(1)} %get-tuple-element.28) | copy-start | bytes 1572868
  235.6 93.2 %all-gather.15.cloned.1.call-start = ((), (), s32[]{:S(2)}) async-start(), calls=%async_computation.11 | async-start | bytes 4718592 | tf_op jit(solution)/shard_map/all_gather | solution.py:54
  236.1 167.6 %reduce-scatter.6.cloned.1.call-start = ((), (), s32[]{:S(2)}) async-start(), calls=%async_computation.9 | async-start | bytes 9437184 | tf_op jit(solution)/shard_map/reduce_scatter | solution.py:76
  247.5 3.2 copy-start.2
  256.7 221.8 %reduce-scatter.8.cloned.1.call-start = ((), (), s32[]{:S(2)}) async-start(), calls=%async_computation.10 | async-start | bytes 9437184 | tf_op jit(solution)/shard_map/reduce_scatter | solution.py:77
  307.7 21.1 %copy-start.4 = (bf16[8,256,640]{2,1,0:T(8,128)(2,1)S(1)}, bf16[8,256,640]{2,1,0:T(8,128)(2,1)}, u32[]{:S(2)}) copy-start(bf16[8,256,640]{2,1,0:T(8,128)(2,1)} %copy.60) | copy-start | bytes 7864324
Sparse Core Ops, SparseCore 0:
  9.9 39.2 all-gather.8
  51.7 37.3 all-gather.6
  91.2 54.7 all-gather.12
  147.7 61.7 all-gather.10
  235.7 52.2 reduce-scatter.3
  290.3 38.4 all-gather.14
  332.3 71.3 reduce-scatter.5
  407.2 71.2 reduce-scatter.7

commit v2 on v1

--- a/solution.py
+++ b/solution.py
@@ -73,8 +73,12 @@
     value_part = jnp.einsum(
         "hqk,qhd->khd", weights, grad_heads, preferred_element_type=jnp.float32
     )
-    key_sum = lax.psum_scatter(key_part, "seq", scatter_dimension=0, tiled=True)
-    value_sum = lax.psum_scatter(value_part, "seq", scatter_dimension=0, tiled=True)
+    both_parts = jnp.concatenate([key_part, value_part], axis=1).astype(jnp.bfloat16)
+    both_sums = lax.psum_scatter(both_parts, "seq", scatter_dimension=0, tiled=True).astype(
+        jnp.float32
+    )
+    key_sum = both_sums[:, :local_heads]
+    value_sum = both_sums[:, local_heads:]
     score_scale = HEAD_DIM ** (-0.5)
     grad_queries = (query_sum * score_scale).reshape(local_tokens, local_heads * HEAD_DIM)
     grad_keys = (key_sum * score_scale).reshape(local_tokens, local_heads * HEAD_DIM)

time: 489 us -> 427 us (0.87)
  waiting for transfers between devices: 316 us -> 240 us
  other arithmetic: 9.09 us -> 16.7 us
    reduce_scatter x2 -> x1, waiting for transfers between devices: 140 us -> 67.9 us  [shards(): lax.psum_scatter(both_parts, 'seq', scatter_dimension=0, tiled=True)]
    concatenate x0 -> x1, other arithmetic: none -> 7.46 us  [shards(): jnp.concatenate([key_part, value_part], axis=1).astype(jnp.bfloat16)]
    unnamed x15 -> x17, local copies, waits for them, and re-layouts: 15.5 us -> 14.3 us
  transfers between devices with their start and end apart: 8 -> 7, of which waited for: 7 -> 6; matrix products, arithmetic and copies ran while one was open for 15% -> 19% of each run, Pallas kernels for 0% -> 0%
where the time goes in v2:
time: 427 us; the launch traced here: 426 us
  waiting for transfers between devices  240 us (56%)
  matrix products  77 us (18%)
  blocking collectives  51.9 us (12%)
  local copies, waits for them, and re-layouts  25.4 us (6%)
  other arithmetic  16.7 us (4%)
  between operations  14.3 us (3%)
    reduce_scatter x1, waiting for transfers between devices, shards(): lax.psum_scatter(both_parts, 'seq', scatter_dimension=0, tiled=True)  67.9 us
    all_gather x1, waiting for transfers between devices, shards(): weight_full = lax.all_gather(out_weight, 'seq', axis=1, tiled=True)  63.5 us
    all_gather x1, waiting for transfers between devices, shards(): cotangent_full = lax.all_gather(cotangent, 'fsdp', axis=1, tiled=True)  45.4 us
    all_to_all x1, blocking collectives, shards(): cotangent_cols = lax.all_to_all(cotangent_full, 'seq', 1, 0, tiled=True)  41.3 us
    all_gather x1, waiting for transfers between devices, shards(): all_keys = lax.all_gather(key_states, 'seq', axis=0, tiled=True)  33.3 us
    all_gather x1, waiting for transfers between devices, shards(): all_values = lax.all_gather(value_states, 'seq', axis=0, tiled=True)  24.7 us
    unnamed x17, local copies, waits for them, and re-layouts  14.3 us
    dot_general x1, matrix products, shards(): jnp.einsum('hqk,qhd->khd', weights, grad_heads, preferred_element_type=jn...  13.2 us
  transfers between devices with their start and end apart: 7, of which 6 were waited for; matrix products, arithmetic and copies ran while one was open for 19% of the time, Pallas kernels for 0%

profile of v2, /device:TPU:0, one launch (start us, length us, event | category | flops | bytes accessed | tf_op | source)
XLA Modules:
  0.0 426.0 jit_solution(16855897893419601684)
XLA Ops:
  12.9 10.6 %all-gather = s32[8,1,256]{2,1,0:T(1,128)S(1)} all-gather(s32[1,1,256]{2,1,0:T(1,128)} %bitcast.66), channel_id=1, replica_groups=mesh['seq'=8,'fsdp'=4] {'seq'}, dimensions={0}, use_global_device_ids=true | all-gather | bytes 9216 | tf_op jit(solution)/shard_map/all_gather | solution.py:30
  24.5 24.7 %all-gather.9.cloned.1.call-done = bf16[2048,1024]{1,0:T(8,128)(2,1)} async-done(((bf16[256,1024]{1,0:T(8,128)(2,1)}), bf16[2048,1024]{1,0:T(8,128)(2,1)}) %all-gather.9.cloned.1.call-update) | async-done | bytes 4194320 | tf_op jit(solution)/shard_map/all_gather | solution.py:29
  49.2 6.5 %copy.56 = bf16[2048,1024]{0,1:T(8,128)(2,1)} copy(bf16[2048,1024]{1,0:T(8,128)(2,1)} %all-gather.9.cloned.1.call-done) | data formatting | bytes 8388608 | tf_op jit(solution)/shard_map/all_gather | solution.py:29
  55.7 33.3 %all-gather.7.cloned.1.call-done = bf16[2048,1024]{0,1:T(8,128)(2,1)} async-done(((bf16[256,1024]{0,1:T(8,128)(2,1)}), bf16[2048,1024]{0,1:T(8,128)(2,1)}) %all-gather.7.cloned.1.call-update) | async-done | bytes 4194320 | tf_op jit(solution)/shard_map/all_gather | solution.py:28
  89.0 5.3 %fusion.1 = (f32[8,256]{1,0:T(8,128)S(1)}, f32[8,256,2048]{2,1,0:T(8,128)S(1)}) fusion(pred[256,2048]{1,0:T(8,128)(4,1)S(1)} %broadcast_compare_fusion, bf16[2048,8,128]{0,2,1:T(8,128)(2,1)} %bitcast.51, bf16[256,1024]{1,0:T(8,128)(2,1)S(1)} %copy-done), kind=kOutput, calls=%fused_computation.5 | convolution fusion | flops 1086322688 | bytes 22028288 | tf_op jit(solution)/shard_map/qhd,khd->hqk/dot_general | solution.py:17
  94.3 4.5 %exponential_reduce_fusion = f32[8,256]{1,0:T(8,128)S(1)} fusion(f32[8,256,2048]{2,1,0:T(8,128)S(1)} %get-tuple-element.26, f32[8,256]{1,0:T(8,128)S(1)} %get-tuple-element.25, pred[256,2048]{1,0:T(8,128)(4,1)S(1)} %broadcast_compare_fusion), kind=kLoop, calls=%fused_computation.2 | loop fusion | flops 16775168 | bytes 17317888 | tf_op jit(solution)/shard_map/reduce_sum | solution.py:35
  100.5 45.4 %all-gather.13.cloned.1.call-done = bf16[256,5120]{0,1:T(8,128)(2,1)} async-done(((bf16[256,1280]{0,1:T(8,128)(2,1)}), bf16[256,5120]{0,1:T(8,128)(2,1)}) %all-gather.13.cloned.1.call-update) | async-done | bytes 2621456 | tf_op jit(solution)/shard_map/all_gather | solution.py:50
  146.0 63.5 %all-gather.11.cloned.1.call-done = bf16[1024,5120]{1,0:T(8,128)(2,1)} async-done(((bf16[1024,640]{1,0:T(8,128)(2,1)}), bf16[1024,5120]{1,0:T(8,128)(2,1)}) %all-gather.11.cloned.1.call-update) | async-done | bytes 10485776 | tf_op jit(solution)/shard_map/all_gather | solution.py:43
  209.5 7.7 %convolution_convert_fusion.1 = bf16[256,1024]{1,0:T(8,128)(2,1)S(1)} fusion(bf16[256,5120]{0,1:T(8,128)(2,1)} %all-gather.13.cloned.1.call-done, bf16[1024,5120]{1,0:T(8,128)(2,1)} %all-gather.11.cloned.1.call-done), kind=kOutput, calls=%fused_computation.11 | convolution fusion | flops 2684616704 | bytes 13631488 | tf_op jit(solution)/shard_map/td,hd->th/dot_general | solution.py:51
  217.4 9.9 %multiply_reduce_fusion = (f32[256,8]{0,1:T(8,128)S(1)}, bf16[8,256,128]{1,2,0:T(8,128)(2,1)S(1)}) fusion(bf16[256,1024]{0,1:T(8,128)(2,1)S(1)} %copy.58, bf16[2048,8,128]{0,2,1:T(8,128)(2,1)} %bitcast.54, f32[8,256,2048]{2,1,0:T(8,128)} %copy-done.1, f32[8,256]{1,0:T(8,128)S(1)} %log_add_fusion, pred[256,2048]{1,0:T(8,128)(4,1)S(1)} %broadcast_compare_fusion), kind=kOutput, calls=%fused_computation.14 | convolution fusion | flops 1091827712 | bytes 22560768 | tf_op jit(solution)/shard_map/hqk,khd->qhd/dot_general | solution.py:38
  227.3 8.4 %convolution_convert_fusion = bf16[256,5120]{1,0:T(8,128)(2,1)} fusion(bf16[256,1024]{0,1:T(8,128)(2,1)S(1)} %bitcast.58, bf16[1024,5120]{1,0:T(8,128)(2,1)} %all-gather.11.cloned.1.call-done), kind=kOutput, calls=%fused_computation.7 | convolution fusion | flops 2685665280 | bytes 13631488 | tf_op jit(solution)/shard_map/dot_general | solution.py:44
  236.6 11.2 %multiply_convert_fusion = bf16[8,256,2048]{2,1,0:T(8,128)(2,1)S(1)} fusion(f32[8,256,2048]{2,1,0:T(8,128)} %copy-done.1, f32[8,256]{1,0:T(8,128)S(1)} %bitcast.67, f32[8,256]{1,0:T(8,128)S(1)} %log_add_fusion, pred[256,2048]{1,0:T(8,128)(4,1)S(1)} %broadcast_compare_fusion, bf16[256,8,128]{0,2,1:T(8,128)(2,1)} %bitcast.63, bf16[2048,8,128]{0,2,1:T(8,128)(2,1)} %bitcast.55), kind=kOutput, calls=%fused_computation | convolution fusion | flops 1098907648 | bytes 30425088 | tf_op jit(solution)/shard_map/qhd,khd->hqk/dot_general | solution.py:63
  247.8 3.2 copy-done.2
  251.0 4.9 %convert_bitcast_fusion.1 = bf16[2048,8,128]{2,0,1:T(8,128)(2,1)} fusion(bf16[8,256,2048]{2,1,0:T(8,128)(2,1)S(1)} %multiply_convert_fusion, bf16[256,1024]{1,0:T(8,128)(2,1)S(1)} %copy-done), kind=kOutput, calls=%fused_computation.9 | convolution fusion | flops 1075838976 | bytes 13107200 | tf_op jit(solution)/shard_map/hqk,qhd->khd/dot_general | solution.py:70
  255.9 13.2 %convert_bitcast_fusion = bf16[2048,8,128]{2,0,1:T(8,128)(2,1)} fusion(bf16[256,8,128]{0,2,1:T(8,128)(2,1)} %bitcast.64, f32[8,256,2048]{2,1,0:T(8,128)} %copy-done.1, f32[8,256]{1,0:T(8,128)S(1)} %log_add_fusion, pred[256,2048]{1,0:T(8,128)(4,1)S(1)} %broadcast_compare_fusion), kind=kOutput, calls=%fused_computation.8 | convolution fusion | flops 1092616192 | bytes 22028288 | tf_op jit(solution)/shard_map/hqk,qhd->khd/dot_general | solution.py:73
  269.1 7.5 %pad_maximum_fusion = bf16[2048,16,128]{2,0,1:T(8,128)(2,1)} fusion(bf16[2048,8,128]{2,0,1:T(8,128)(2,1)} %convert_bitcast_fusion, bf16[2048,8,128]{2,0,1:T(8,128)(2,1)} %convert_bitcast_fusion.1), kind=kLoop, calls=%fused_computation.6 | loop fusion | flops 4194304 | bytes 16777216 | tf_op jit(solution)/shard_map/concatenate | solution.py:76
  276.6 41.3 %all_to_all.19 = bf16[256,8,640]{0,2,1:T(8,128)(2,1)S(1)} all-to-all(bf16[256,8,640]{0,2,1:T(8,128)(2,1)} %bitcast.60), channel_id=1, replica_groups=mesh['seq'=8,'fsdp'=4] {'seq'}, dimensions={1} | all-to-all | bytes 5242880 | tf_op jit(solution)/shard_map/all_to_all | solution.py:55
  318.0 2.6 copy.66
  320.6 9.3 %convolution_multiply_fusion = f32[8,256,128]{1,2,0:T(8,128)} fusion(bf16[8,256,2048]{2,1,0:T(8,128)(2,1)} %copy-done.2, bf16[2048,8,128]{0,2,1:T(8,128)(2,1)} %bitcast.52), kind=kOutput, calls=%fused_computation.10 | convolution fusion | flops 1074003968 | bytes 13631488 | tf_op jit(solution)/shard_map/hqk,khd->qhd/dot_general | solution.py:67
  329.9 2.5 copy.67
  332.5 2.2 convert_element_type.35
  334.7 3.6 all-gather.15.cloned.1.call-done
  338.3 7.1 %fusion.9 = f32[1024,640]{1,0:T(8,128)} fusion(bf16[2048,1024]{0,1:T(8,128)(2,1)} %all-gather.15.cloned.1.call-done, bf16[2048,640]{1,0:T(8,128)(2,1)S(1)} %bitcast.61), kind=kOutput, calls=%fused_computation.22 | convolution fusion | flops 2684354560 | bytes 9437184 | tf_op jit(solution)/shard_map/th,td->hd/dot_general | solution.py:56
  345.3 67.9 %reduce-scatter.5.cloned.1.call-done = bf16[256,16,128]{2,0,1:T(8,128)(2,1)} async-done(((bf16[2048,16,128]{2,0,1:T(8,128)(2,1)}), bf16[256,16,128]{2,0,1:T(8,128)(2,1)}) %reduce-scatter.5.cloned.1.call-update) | async-done | bytes 1048592 | tf_op jit(solution)/shard_map/reduce_scatter | solution.py:77
  (38 shorter events, 15.3 us)
Async XLA Ops:
  7.2 81.9 %copy-start = (bf16[256,1024]{1,0:T(8,128)(2,1)S(1)}, bf16[256,1024]{1,0:T(8,128)(2,1)}, u32[]{:S(2)}) copy-start(bf16[256,1024]{1,0:T(8,128)(2,1)} %param.6) | copy-start | bytes 1572868
  7.2 42.0 %all-gather.9.cloned.1.call-start = ((), (), s32[]{:S(2)}) async-start(), calls=%async_computation.4 | async-start | bytes 4718592 | tf_op jit(solution)/shard_map/all_gather | solution.py:29
  7.9 81.1 %all-gather.7.cloned.1.call-start = ((), (), s32[]{:S(2)}) async-start(), calls=%async_computation.3 | async-start | bytes 4718592 | tf_op jit(solution)/shard_map/all_gather | solution.py:28
  10.0 135.9 %all-gather.13.cloned.1.call-start = ((), (), s32[]{:S(2)}) async-start(), calls=%async_computation.7 | async-start | bytes 3276800 | tf_op jit(solution)/shard_map/all_gather | solution.py:50
  12.3 197.2 %all-gather.11.cloned.1.call-start = ((), (), s32[]{:S(2)}) async-start(), calls=%async_computation.5 | async-start | bytes 11796480 | tf_op jit(solution)/shard_map/all_gather | solution.py:43
  12.8 319.6 %reduce-scatter.3.cloned.1.call-start = ((), (), s32[]{:S(2)}) async-start(), calls=%async_computation.6 | async-start | bytes 3276800 | tf_op jit(solution)/shard_map/reduce_scatter | solution.py:47
  94.3 6.2 %copy-start.1 = (f32[8,256,2048]{2,1,0:T(8,128)}, f32[8,256,2048]{2,1,0:T(8,128)S(1)}, u32[]{:S(2)}) copy-start(f32[8,256,2048]{2,1,0:T(8,128)S(1)} %get-tuple-element.26) | copy-start | bytes 50331652
  217.4 9.9 %copy-start.5 = (bf16[256,1024]{0,1:T(8,128)(2,1)}, bf16[256,1024]{0,1:T(8,128)(2,1)S(1)}, u32[]{:S(2)}) copy-start(bf16[256,1024]{0,1:T(8,128)(2,1)S(1)} %copy.58) | copy-start | bytes 1572868
  227.3 8.4 %copy-start.3 = (bf16[8,256,128]{1,2,0:T(8,128)(2,1)}, bf16[8,256,128]{1,2,0:T(8,128)(2,1)S(1)}, u32[]{:S(2)}) copy-start(bf16[8,256,128]{1,2,0:T(8,128)(2,1)S(1)} %get-tuple-element.28) | copy-start | bytes 1572868
  235.8 102.5 %all-gather.15.cloned.1.call-start = ((), (), s32[]{:S(2)}) async-start(), calls=%async_computation.9 | async-start | bytes 4718592 | tf_op jit(solution)/shard_map/all_gather | solution.py:54
  236.4 176.9 %reduce-scatter.5.cloned.1.call-start = ((), (), s32[]{:S(2)}) async-start(), calls=%async_computation.8 | async-start | bytes 9437184 | tf_op jit(solution)/shard_map/reduce_scatter | solution.py:77
  247.8 3.2 copy-start.2
  320.6 17.7 %copy-start.4 = (bf16[8,256,640]{2,1,0:T(8,128)(2,1)S(1)}, bf16[8,256,640]{2,1,0:T(8,128)(2,1)}, u32[]{:S(2)}) copy-start(bf16[8,256,640]{2,1,0:T(8,128)(2,1)} %copy.66) | copy-start | bytes 7864324
Sparse Core Ops, SparseCore 0:
  9.9 39.2 all-gather.8
  51.7 37.3 all-gather.6
  91.2 54.7 all-gather.12
  147.7 61.7 all-gather.10
  235.9 52.2 reduce-scatter.2
  290.5 47.7 all-gather.14
  341.7 71.4 reduce-scatter.4

commit v3 on v2

--- a/solution.py
+++ b/solution.py
@@ -19,6 +19,41 @@
     ) * HEAD_DIM ** (-0.5)
     visible = key_pos[None, None, :] <= query_pos[None, :, None]
     return jnp.where(visible, raw, blocked)
+
+
+def shift_pieces(block, axis):
+    count = lax.axis_size(axis)
+    pieces = [block]
+    for distance in range(1, count):
+        route = [(i, (i + distance) % count) for i in range(count)]
+        pieces.append(lax.ppermute(block, axis, route))
+    return pieces
+
+
+def permute_gather(block, axis, dim):
+    count = lax.axis_size(axis)
+    me = lax.axis_index(axis)
+    width = block.shape[dim]
+    shape = list(block.shape)
+    shape[dim] = width * count
+    full = jnp.zeros(shape, block.dtype)
+    for distance, piece in enumerate(shift_pieces(block, axis)):
+        start = [0] * block.ndim
+        start[dim] = ((me - distance) % count) * width
+        full = lax.dynamic_update_slice(full, piece, start)
+    return full
+
+
+def permute_sum_scatter(block, axis, dim):
+    count = lax.axis_size(axis)
+    me = lax.axis_index(axis)
+    width = block.shape[dim] // count
+    total = lax.dynamic_slice_in_dim(block, me * width, width, dim).astype(jnp.float32)
+    for distance in range(1, count):
+        route = [(i, (i + distance) % count) for i in range(count)]
+        piece = lax.dynamic_slice_in_dim(block, ((me + distance) % count) * width, width, dim)
+        total = total + lax.ppermute(piece, axis, route).astype(jnp.float32)
+    return total
 
 
 def shards(query_states, key_states, value_states, positions, out_weight, cotangent):
@@ -44,10 +79,8 @@
     partial_sum = jnp.dot(attended_flat, weight_full, preferred_element_type=jnp.float32).astype(
         jnp.bfloat16
     )
-    attn_output = lax.psum_scatter(partial_sum, "fsdp", scatter_dimension=1, tiled=True).astype(
-        jnp.float32
-    )
-    cotangent_full = lax.all_gather(cotangent, "fsdp", axis=1, tiled=True)
+    attn_output = permute_sum_scatter(partial_sum, "fsdp", 1)
+    cotangent_full = permute_gather(cotangent, "fsdp", 1)
     grad_attended = jnp.einsum(
         "td,hd->th", cotangent_full, weight_full, preferred_element_type=jnp.float32
     ).astype(jnp.bfloat16)

time: 427 us -> 353 us (0.83)
  waiting for transfers between devices: 240 us -> 182 us
  blocking collectives: 51.9 us -> 9.29 us
  starting transfers between devices: 0.46 us -> 15.6 us
  local copies, waits for them, and re-layouts: 25.4 us -> 34.9 us
    ppermute x0 -> x6, waiting for transfers between devices: none -> 69.3 us  [the longest x3 41.6 us: permute_sum_scatter(): total = total + lax.ppermute(piece, axis, route).astype(jnp.float32)]
    reduce_scatter x1, waiting for transfers between devices: 67.9 us -> 0.01 us  [shards(): lax.psum_scatter(both_parts, 'seq', scatter_dimension=0, tiled=True)]
    all_gather x1 -> x0, waiting for transfers between devices: 45.4 us -> none  [shards(): cotangent_full = lax.all_gather(cotangent, 'fsdp', axis=1, tiled=True)]
    all_to_all x1 -> x0, blocking collectives: 41.3 us -> none  [shards(): cotangent_cols = lax.all_to_all(cotangent_full, 'seq', 1, 0, tiled=True)]
    all_to_all x0 -> x1, waiting for transfers between devices: none -> 40.1 us  [shards(): cotangent_cols = lax.all_to_all(cotangent_full, 'seq', 1, 0, tiled=True)]
    all_gather x1, waiting for transfers between devices: 24.7 us -> 0.02 us  [shards(): all_values = lax.all_gather(value_states, 'seq', axis=0, tiled=True)]
    all_gather x1, waiting for transfers between devices: 33.3 us -> 18.5 us  [shards(): all_keys = lax.all_gather(key_states, 'seq', axis=0, tiled=True)]
    ppermute x0 -> x6, starting transfers between devices: none -> 11.4 us  [the longest x3 6.99 us: shift_pieces(): pieces.append(lax.ppermute(block, axis, route))]
  transfers between devices with their start and end apart: 7 -> 12, of which waited for: 6 -> 7; matrix products, arithmetic and copies ran while one was open for 19% -> 28% of each run, Pallas kernels for 0% -> 0%
where the time goes in v3:
time: 353 us; the launch traced here: 352 us
  waiting for transfers between devices  182 us (52%)
  matrix products  77.3 us (22%)
  local copies, waits for them, and re-layouts  34.9 us (10%)
  other arithmetic  18.5 us (5%)
  starting transfers between devices  15.6 us (4%)
  between operations  14 us (4%)
  blocking collectives  9.29 us (3%)
    all_gather x1, waiting for transfers between devices, shards(): weight_full = lax.all_gather(out_weight, 'seq', axis=1, tiled=True)  52.7 us
    ppermute x3, waiting for transfers between devices, permute_sum_scatter(): total = total + lax.ppermute(piece, axis, route).astype(jnp.float32)  41.6 us
    all_to_all x1, waiting for transfers between devices, shards(): cotangent_cols = lax.all_to_all(cotangent_full, 'seq', 1, 0, tiled=True)  40.1 us
    ppermute x3, waiting for transfers between devices, shift_pieces(): pieces.append(lax.ppermute(block, axis, route))  27.7 us
    all_gather x1, waiting for transfers between devices, shards(): all_keys = lax.all_gather(key_states, 'seq', axis=0, tiled=True)  18.5 us
    unnamed x27, local copies, waits for them, and re-layouts  16.3 us
    dot_general x1, matrix products, shards(): jnp.einsum('hqk,qhd->khd', weights, grad_heads, preferred_element_type=jn...  13.9 us
    dot_general x1, matrix products, shards(): jnp.einsum('hqk,khd->qhd', weights, value_heads, preferred_element_type=j...  11.2 us
  transfers between devices with their start and end apart: 12, of which 7 were waited for; matrix products, arithmetic and copies ran while one was open for 28% of the time, Pallas kernels for 0%

profile of v3, /device:TPU:0, one launch (start us, length us, event | category | flops | bytes accessed | tf_op | source)
XLA Modules:
  0.0 351.5 jit_solution(9768460813269315612)
XLA Ops:
  13.0 3.1 collective-permute-start.3
  20.0 9.3 %all-gather = s32[8,1,256]{2,1,0:T(1,128)S(1)} all-gather(s32[1,1,256]{2,1,0:T(1,128)} %bitcast.66), channel_id=1, replica_groups=mesh['seq'=8,'fsdp'=4] {'seq'}, dimensions={0}, use_global_device_ids=true | all-gather | bytes 9216 | tf_op jit(solution)/shard_map/all_gather | solution.py:65
  35.3 26.0 %collective-permute-done.4 = bf16[256,1280]{0,1:T(8,128)(2,1)} collective-permute-done((bf16[256,1280]{0,1:T(8,128)(2,1)}, bf16[256,1280]{0,1:T(8,128)(2,1)}, u32[]{:S(2)}, u32[]{:S(2)}) %collective-permute-start.4) | collective-permute-done | bytes 655392 | tf_op jit(solution)/shard_map/ppermute | solution.py:29
  63.7 6.9 %copy.59 = bf16[2048,1024]{0,1:T(8,128)(2,1)} copy(bf16[2048,1024]{1,0:T(8,128)(2,1)} %all-gather.8.cloned.1.call-done) | data formatting | bytes 8388608 | tf_op jit(solution)/shard_map/all_gather | solution.py:64
  70.6 18.5 %all-gather.6.cloned.1.call-done = bf16[2048,1024]{0,1:T(8,128)(2,1)} async-done(((bf16[256,1024]{0,1:T(8,128)(2,1)}), bf16[2048,1024]{0,1:T(8,128)(2,1)}) %all-gather.6.cloned.1.call-update) | async-done | bytes 4194320 | tf_op jit(solution)/shard_map/all_gather | solution.py:63
  89.0 5.3 %fusion.1 = (f32[8,256]{1,0:T(8,128)S(1)}, f32[8,256,2048]{2,1,0:T(8,128)S(1)}) fusion(pred[256,2048]{1,0:T(8,128)(4,1)} %broadcast_compare_fusion, bf16[2048,8,128]{0,2,1:T(8,128)(2,1)} %bitcast.51, bf16[256,1024]{1,0:T(8,128)(2,1)S(1)} %copy-done), kind=kOutput, calls=%fused_computation.5 | convolution fusion | flops 1086322688 | bytes 22028288 | tf_op jit(solution)/shard_map/qhd,khd->hqk/dot_general | solution.py:17
  94.4 4.5 %exponential_reduce_fusion = f32[8,256]{1,0:T(8,128)S(1)} fusion(f32[8,256,2048]{2,1,0:T(8,128)S(1)} %get-tuple-element.29, f32[8,256]{1,0:T(8,128)S(1)} %get-tuple-element.28, pred[256,2048]{1,0:T(8,128)(4,1)S(1)} %copy-done.6), kind=kLoop, calls=%fused_computation.2 | loop fusion | flops 16775168 | bytes 17317888 | tf_op jit(solution)/shard_map/reduce_sum | solution.py:70
  101.3 52.7 %all-gather.10.cloned.1.call-done = bf16[1024,5120]{1,0:T(8,128)(2,1)} async-done(((bf16[1024,640]{1,0:T(8,128)(2,1)}), bf16[1024,5120]{1,0:T(8,128)(2,1)}) %all-gather.10.cloned.1.call-update) | async-done | bytes 10485776 | tf_op jit(solution)/shard_map/all_gather | solution.py:78
  154.0 7.7 %convolution_convert_fusion.1 = bf16[256,1024]{1,0:T(8,128)(2,1)} fusion(bf16[256,5120]{0,1:T(8,128)(2,1)S(1)} %constant_dynamic-update-slice_fusion, bf16[1024,5120]{1,0:T(8,128)(2,1)} %all-gather.10.cloned.1.call-done), kind=kOutput, calls=%fused_computation.12 | convolution fusion | flops 2684616704 | bytes 13631488 | tf_op jit(solution)/shard_map/td,hd->th/dot_general | solution.py:84
  163.0 11.2 %multiply_reduce_fusion = (f32[256,8]{0,1:T(8,128)S(1)}, bf16[8,256,128]{1,2,0:T(8,128)(2,1)}) fusion(bf16[256,1024]{0,1:T(8,128)(2,1)S(1)} %copy.64, bf16[2048,8,128]{0,2,1:T(8,128)(2,1)} %bitcast.55, f32[8,256,2048]{2,1,0:T(8,128)} %copy-done.2, f32[8,256]{1,0:T(8,128)S(1)} %log_add_fusion, pred[256,2048]{1,0:T(8,128)(4,1)} %broadcast_compare_fusion), kind=kOutput, calls=%fused_computation.15 | convolution fusion | flops 1091827712 | bytes 22560768 | tf_op jit(solution)/shard_map/hqk,khd->qhd/dot_general | solution.py:73
  174.5 11.2 %multiply_convert_fusion = bf16[8,256,2048]{2,1,0:T(8,128)(2,1)S(1)} fusion(f32[8,256,2048]{2,1,0:T(8,128)} %copy-done.2, f32[8,256]{1,0:T(8,128)S(1)} %bitcast.67, f32[8,256]{1,0:T(8,128)S(1)} %log_add_fusion, pred[256,2048]{1,0:T(8,128)(4,1)S(1)} %copy-done.7, bf16[256,8,128]{0,2,1:T(8,128)(2,1)} %bitcast.63, bf16[2048,8,128]{0,2,1:T(8,128)(2,1)} %bitcast.56), kind=kOutput, calls=%fused_computation | convolution fusion | flops 1098907648 | bytes 30425088 | tf_op jit(solution)/shard_map/qhd,khd->hqk/dot_general | solution.py:96
  185.7 3.3 copy-done.5
  189.0 4.8 %convert_bitcast_fusion.1 = bf16[2048,8,128]{2,0,1:T(8,128)(2,1)} fusion(bf16[8,256,2048]{2,1,0:T(8,128)(2,1)S(1)} %multiply_convert_fusion, bf16[256,1024]{1,0:T(8,128)(2,1)S(1)} %copy-done), kind=kOutput, calls=%fused_computation.9 | convolution fusion | flops 1075838976 | bytes 13107200 | tf_op jit(solution)/shard_map/hqk,qhd->khd/dot_general | solution.py:103
  193.8 13.9 %convert_bitcast_fusion = bf16[2048,8,128]{2,0,1:T(8,128)(2,1)} fusion(bf16[256,8,128]{0,2,1:T(8,128)(2,1)} %bitcast.64, f32[8,256,2048]{2,1,0:T(8,128)} %copy-done.2, f32[8,256]{1,0:T(8,128)S(1)} %log_add_fusion, pred[256,2048]{1,0:T(8,128)(4,1)S(1)} %copy-done.7), kind=kOutput, calls=%fused_computation.8 | convolution fusion | flops 1092616192 | bytes 22028288 | tf_op jit(solution)/shard_map/hqk,qhd->khd/dot_general | solution.py:106
  207.7 7.7 %pad_maximum_fusion = bf16[2048,16,128]{2,0,1:T(8,128)(2,1)} fusion(bf16[2048,8,128]{2,0,1:T(8,128)(2,1)} %convert_bitcast_fusion, bf16[2048,8,128]{2,0,1:T(8,128)(2,1)} %convert_bitcast_fusion.1), kind=kLoop, calls=%fused_computation.6 | loop fusion | flops 4194304 | bytes 16777216 | tf_op jit(solution)/shard_map/concatenate | solution.py:109
  215.5 3.8 %all-to-all-start = ((bf16[256,8,640]{0,2,1:T(8,128)(2,1)}), bf16[256,8,640]{0,2,1:T(8,128)(2,1)S(1)}, u32[]{:S(2)}, u32[]{:S(2)}) async-start(bf16[256,8,640]{0,2,1:T(8,128)(2,1)} %bitcast.54), calls=%async_computation.1 | async-start | bytes 5242880 | tf_op jit(solution)/shard_map/all_to_all | solution.py:88
  219.3 40.1 %all-to-all-done = bf16[256,8,640]{0,2,1:T(8,128)(2,1)S(1)} async-done(((bf16[256,8,640]{0,2,1:T(8,128)(2,1)}), bf16[256,8,640]{0,2,1:T(8,128)(2,1)S(1)}, u32[]{:S(2)}, u32[]{:S(2)}) %all-to-all-start) | async-done | bytes 2621472 | tf_op jit(solution)/shard_map/all_to_all | solution.py:88
  262.1 7.6 %convolution_convert_fusion = bf16[256,5120]{1,0:T(8,128)(2,1)S(1)} fusion(bf16[256,1024]{0,1:T(8,128)(2,1)S(1)} %bitcast.60, bf16[1024,5120]{1,0:T(8,128)(2,1)} %all-gather.10.cloned.1.call-done), kind=kOutput, calls=%fused_computation.7 | convolution fusion | flops 2685665280 | bytes 13631488 | tf_op jit(solution)/shard_map/dot_general | solution.py:79
  271.0 3.3 collective-permute-start.2
  275.5 7.5 %convolution_multiply_fusion = f32[8,256,128]{1,2,0:T(8,128)} fusion(bf16[8,256,2048]{2,1,0:T(8,128)(2,1)} %copy-done.5, bf16[2048,8,128]{0,2,1:T(8,128)(2,1)S(1)} %bitcast.52), kind=kOutput, calls=%fused_computation.10 | convolution fusion | flops 1074003968 | bytes 13631488 | tf_op jit(solution)/shard_map/hqk,khd->qhd/dot_general | solution.py:100
  285.5 4.3 %collective-permute-done.2 = bf16[256,1280]{1,0:T(8,128)(2,1)} collective-permute-done((bf16[256,1280]{1,0:T(8,128)(2,1)}, bf16[256,1280]{1,0:T(8,128)(2,1)}, u32[]{:S(2)}, u32[]{:S(2)}) %collective-permute-start.2) | collective-permute-done | bytes 655392 | tf_op jit(solution)/shard_map/ppermute | solution.py:55
  289.8 37.2 %collective-permute-done.1 = bf16[256,1280]{1,0:T(8,128)(2,1)} collective-permute-done((bf16[256,1280]{1,0:T(8,128)(2,1)}, bf16[256,1280]{1,0:T(8,128)(2,1)}, u32[]{:S(2)}, u32[]{:S(2)}) %collective-permute-start.1) | collective-permute-done | bytes 655392 | tf_op jit(solution)/shard_map/ppermute | solution.py:55
  327.0 2.8 convert_add_fusion
  329.9 7.9 %fusion.9 = f32[1024,640]{1,0:T(8,128)} fusion(bf16[2048,1024]{0,1:T(8,128)(2,1)} %all-gather.12.cloned.1.call-done, bf16[2048,640]{1,0:T(8,128)(2,1)} %bitcast.61), kind=kOutput, calls=%fused_computation.30 | convolution fusion | flops 2684354560 | bytes 9437184 | tf_op jit(solution)/shard_map/th,td->hd/dot_general | solution.py:89
  (61 shorter events, 36.7 us)
Async XLA Ops:
  7.2 81.9 %copy-start = (bf16[256,1024]{1,0:T(8,128)(2,1)S(1)}, bf16[256,1024]{1,0:T(8,128)(2,1)}, u32[]{:S(2)}) copy-start(bf16[256,1024]{1,0:T(8,128)(2,1)} %param.6) | copy-start | bytes 1572868
  7.2 56.5 %all-gather.8.cloned.1.call-start = ((), (), s32[]{:S(2)}) async-start(), calls=%async_computation.3 | async-start | bytes 4718592 | tf_op jit(solution)/shard_map/all_gather | solution.py:64
  7.9 81.1 %all-gather.6.cloned.1.call-start = ((), (), s32[]{:S(2)}) async-start(), calls=%async_computation.2 | async-start | bytes 4718592 | tf_op jit(solution)/shard_map/all_gather | solution.py:63
  10.0 144.0 %all-gather.10.cloned.1.call-start = ((), (), s32[]{:S(2)}) async-start(), calls=%async_computation.4 | async-start | bytes 11796480 | tf_op jit(solution)/shard_map/all_gather | solution.py:78
  10.8 319.1 %all-gather.12.cloned.1.call-start = ((), (), s32[]{:S(2)}) async-start(), calls=%async_computation.6 | async-start | bytes 4718592 | tf_op jit(solution)/shard_map/all_gather | solution.py:87
  13.0 21.1 %collective-permute-start.3 = (bf16[256,1280]{0,1:T(8,128)(2,1)}, bf16[256,1280]{0,1:T(8,128)(2,1)}, u32[]{:S(2)}, u32[]{:S(2)}) collective-permute-start(bf16[256,1280]{0,1:T(8,128)(2,1)} %copy.60), channel_id=1, source_target_pairs={{0,1},{1,2},{2,3},{3,0},{4,5},{5,6},{6,7},{7,4},{8,9},{9,10},{10,1... | collective-permute-start | bytes 1966088 | tf_op jit(solution)/shard_map/ppermute | solution.py:29
  16.0 45.3 %collective-permute-start.4 = (bf16[256,1280]{0,1:T(8,128)(2,1)}, bf16[256,1280]{0,1:T(8,128)(2,1)}, u32[]{:S(2)}, u32[]{:S(2)}) collective-permute-start(bf16[256,1280]{0,1:T(8,128)(2,1)} %copy.60), channel_id=1, source_target_pairs={{0,2},{1,3},{2,0},{3,1},{4,6},{5,7},{6,4},{7,5},{8,10},{9,11},{10,... | collective-permute-start | bytes 1966088 | tf_op jit(solution)/shard_map/ppermute | solution.py:29
  18.6 43.8 %collective-permute-start.5 = (bf16[256,1280]{0,1:T(8,128)(2,1)}, bf16[256,1280]{0,1:T(8,128)(2,1)}, u32[]{:S(2)}, u32[]{:S(2)}) collective-permute-start(bf16[256,1280]{0,1:T(8,128)(2,1)} %copy.60), channel_id=1, source_target_pairs={{0,3},{1,0},{2,1},{3,2},{4,7},{5,4},{6,5},{7,6},{8,11},{9,8},{10,9... | collective-permute-start | bytes 1966088 | tf_op jit(solution)/shard_map/ppermute | solution.py:29
  63.6 90.4 %copy-start.4 = (bf16[256,5120]{0,1:T(8,128)(2,1)}, bf16[256,5120]{0,1:T(8,128)(2,1)S(1)}, u32[]{:S(2)}) copy-start(bf16[256,5120]{0,1:T(8,128)(2,1)S(1)} %constant_dynamic-update-slice_fusion) | copy-start | bytes 7864324
  89.0 5.4 %copy-start.6 = (pred[256,2048]{1,0:T(8,128)(4,1)S(1)}, pred[256,2048]{1,0:T(8,128)(4,1)}, u32[]{:S(2)}) copy-start(pred[256,2048]{1,0:T(8,128)(4,1)} %broadcast_compare_fusion) | copy-start | bytes 1572868
  94.4 6.9 %copy-start.2 = (f32[8,256,2048]{2,1,0:T(8,128)}, f32[8,256,2048]{2,1,0:T(8,128)S(1)}, u32[]{:S(2)}) copy-start(f32[8,256,2048]{2,1,0:T(8,128)S(1)} %get-tuple-element.29) | copy-start | bytes 50331652
  162.9 11.3 %copy-start.10 = (bf16[256,1024]{0,1:T(8,128)(2,1)}, bf16[256,1024]{0,1:T(8,128)(2,1)S(1)}, u32[]{:S(2)}) copy-start(bf16[256,1024]{0,1:T(8,128)(2,1)S(1)} %copy.64) | copy-start | bytes 1572868
  163.0 11.5 %copy-start.7 = (pred[256,2048]{1,0:T(8,128)(4,1)S(1)}, pred[256,2048]{1,0:T(8,128)(4,1)}, u32[]{:S(2)}) copy-start(pred[256,2048]{1,0:T(8,128)(4,1)} %broadcast_compare_fusion) | copy-start | bytes 1572868
  174.2 163.6 %reduce-scatter.2.cloned.1.call-start = ((), (), s32[]{:S(2)}) async-start(), calls=%async_computation.5 | async-start | bytes 9437184 | tf_op jit(solution)/shard_map/reduce_scatter | solution.py:110
  185.7 3.3 copy-start.5
  215.5 46.6 %copy-start.9 = (bf16[8,256,128]{1,2,0:T(8,128)(2,1)S(1)}, bf16[8,256,128]{1,2,0:T(8,128)(2,1)}, u32[]{:S(2)}) copy-start(bf16[8,256,128]{1,2,0:T(8,128)(2,1)} %get-tuple-element.31) | copy-start | bytes 1572868
  215.5 43.9 %all-to-all-start = ((bf16[256,8,640]{0,2,1:T(8,128)(2,1)}), bf16[256,8,640]{0,2,1:T(8,128)(2,1)S(1)}, u32[]{:S(2)}, u32[]{:S(2)}) async-start(bf16[256,8,640]{0,2,1:T(8,128)(2,1)} %bitcast.54), calls=%async_computation.1 | async-start | bytes 5242880 | tf_op jit(solution)/shard_map/all_to_all | solution.py:88
  262.1 13.4 %copy-start.3 = (bf16[2048,1024]{0,1:T(8,128)(2,1)S(1)}, bf16[2048,1024]{0,1:T(8,128)(2,1)}, u32[]{:S(2)}) copy-start(bf16[2048,1024]{0,1:T(8,128)(2,1)} %all-gather.6.cloned.1.call-done) | copy-start | bytes 12582916
  271.0 18.8 %collective-permute-start.2 = (bf16[256,1280]{1,0:T(8,128)(2,1)}, bf16[256,1280]{1,0:T(8,128)(2,1)}, u32[]{:S(2)}, u32[]{:S(2)}) collective-permute-start(bf16[256,1280]{1,0:T(8,128)(2,1)} %get-tuple-element.26), channel_id=1, source_target_pairs={{0,3},{1,0},{2,1},{3,2},{4,7},{5,4},{6,5},{7,6},{8,11},{9,8},{10,9... | collective-permute-start | bytes 1966088 | tf_op jit(solution)/shard_map/ppermute | solution.py:55
  274.4 52.7 %collective-permute-start.1 = (bf16[256,1280]{1,0:T(8,128)(2,1)}, bf16[256,1280]{1,0:T(8,128)(2,1)}, u32[]{:S(2)}, u32[]{:S(2)}) collective-permute-start(bf16[256,1280]{1,0:T(8,128)(2,1)} %get-tuple-element.27), channel_id=1, source_target_pairs={{0,2},{1,3},{2,0},{3,1},{4,6},{5,7},{6,4},{7,5},{8,10},{9,11},{10,... | collective-permute-start | bytes 1966088 | tf_op jit(solution)/shard_map/ppermute | solution.py:55
  274.4 52.7 %collective-permute-start = (bf16[256,1280]{1,0:T(8,128)(2,1)}, bf16[256,1280]{1,0:T(8,128)(2,1)}, u32[]{:S(2)}, u32[]{:S(2)}) collective-permute-start(bf16[256,1280]{1,0:T(8,128)(2,1)} %get-tuple-element.25), channel_id=1, source_target_pairs={{0,1},{1,2},{2,3},{3,0},{4,5},{5,6},{6,7},{7,4},{8,9},{9,10},{10,1... | collective-permute-start | bytes 1966088 | tf_op jit(solution)/shard_map/ppermute | solution.py:55
  337.8 5.5 %copy-start.8 = (bf16[256,16,128]{2,0,1:T(8,128)(2,1)S(1)}, bf16[256,16,128]{2,0,1:T(8,128)(2,1)}, u32[]{:S(2)}) copy-start(bf16[256,16,128]{2,0,1:T(8,128)(2,1)} %reduce-scatter.2.cloned.1.call-done) | copy-start | bytes 3145732
  339.3 5.7 %copy-start.1 = (bf16[256,1024]{1,0:T(8,128)(2,1)S(1)}, bf16[256,1024]{1,0:T(8,128)(2,1)}, u32[]{:S(2)}) copy-start(bf16[256,1024]{1,0:T(8,128)(2,1)} %param.6) | copy-start | bytes 1572868
Sparse Core Ops, SparseCore 0:
  9.9 39.2 all-gather.7
  51.7 37.3 all-gather.5
  90.9 63.0 all-gather.9
  174.3 37.3 all-gather.11
  215.6 78.9 reduce-scatter.1

commit v4 on v3

--- a/solution.py
+++ b/solution.py
@@ -107,6 +107,7 @@
         "hqk,qhd->khd", weights, grad_heads, preferred_element_type=jnp.float32
     )
     both_parts = jnp.concatenate([key_part, value_part], axis=1).astype(jnp.bfloat16)
+    attn_output, both_parts = lax.optimization_barrier((attn_output, both_parts))
     both_sums = lax.psum_scatter(both_parts, "seq", scatter_dimension=0, tiled=True).astype(
         jnp.float32
     )

time: 353 us -> 339 us (0.960)
  waiting for transfers between devices: 182 us -> 127 us
  blocking collectives: 9.29 us -> 55.4 us
  starting transfers between devices: 15.6 us -> 10.9 us
    all_to_all x0 -> x1, blocking collectives: none -> 46.2 us  [shards(): cotangent_cols = lax.all_to_all(cotangent_full, 'seq', 1, 0, tiled=True)]
    all_to_all x1 -> x0, waiting for transfers between devices: 40.1 us -> none  [shards(): cotangent_cols = lax.all_to_all(cotangent_full, 'seq', 1, 0, tiled=True)]
    ppermute x3, waiting for transfers between devices: 41.6 us -> 17.5 us  [permute_sum_scatter(): total = total + lax.ppermute(piece, axis, route).astype(jnp.float32)]
    ppermute x3, waiting for transfers between devices: 27.7 us -> 41.8 us  [shift_pieces(): pieces.append(lax.ppermute(block, axis, route))]
    all_gather x1, waiting for transfers between devices: 18.5 us -> 5.43 us  [shards(): all_keys = lax.all_gather(key_states, 'seq', axis=0, tiled=True)]
    reduce_scatter x1, waiting for transfers between devices: 0.01 us -> 8.33 us  [shards(): lax.psum_scatter(both_parts, 'seq', scatter_dimension=0, tiled=True)]
    all_to_all x1 -> x0, starting transfers between devices: 3.77 us -> none  [shards(): cotangent_cols = lax.all_to_all(cotangent_full, 'seq', 1, 0, tiled=True)]
    unnamed x27 -> x23, local copies, waits for them, and re-layouts: 16.3 us -> 13.5 us
  transfers between devices with their start and end apart: 12 -> 11, of which waited for: 7 -> 6; matrix products, arithmetic and copies ran while one was open for 28% -> 30% of each run, Pallas kernels for 0% -> 0%
where the time goes in v4:
time: 339 us; the launch traced here: 338 us
  waiting for transfers between devices  127 us (37%)
  matrix products  79 us (23%)
  blocking collectives  55.4 us (16%)
  local copies, waits for them, and re-layouts  34.9 us (10%)
  other arithmetic  16.9 us (5%)
  between operations  14 us (4%)
  starting transfers between devices  10.9 us (3%)
    all_gather x1, waiting for transfers between devices, shards(): weight_full = lax.all_gather(out_weight, 'seq', axis=1, tiled=True)  52.7 us
    all_to_all x1, blocking collectives, shards(): cotangent_cols = lax.all_to_all(cotangent_full, 'seq', 1, 0, tiled=True)  46.2 us
    ppermute x3, waiting for transfers between devices, shift_pieces(): pieces.append(lax.ppermute(block, axis, route))  41.8 us
    ppermute x3, waiting for transfers between devices, permute_sum_scatter(): total = total + lax.ppermute(piece, axis, route).astype(jnp.float32)  17.5 us
    unnamed x23, local copies, waits for them, and re-layouts  13.5 us
    dot_general x1, matrix products, shards(): jnp.einsum('qhd,khd->hqk', grad_heads, value_heads, preferred_element_typ...  13 us
    dot_general x1, matrix products, shards(): jnp.einsum('hqk,khd->qhd', weights, value_heads, preferred_element_type=j...  10.7 us
    dot_general x1, matrix products, shards(): jnp.einsum('hqk,qhd->khd', weights, grad_heads, preferred_element_type=jn...  10.6 us
  transfers between devices with their start and end apart: 11, of which 6 were waited for; matrix products, arithmetic and copies ran while one was open for 30% of the time, Pallas kernels for 0%

profile of v4, /device:TPU:0, one launch (start us, length us, event | category | flops | bytes accessed | tf_op | source)
XLA Modules:
  0.0 338.3 jit_solution(13247313128857532095)
XLA Ops:
  13.0 5.1 %collective-permute-start.5 = (bf16[256,1280]{0,1:T(8,128)(2,1)}, bf16[256,1280]{0,1:T(8,128)(2,1)}, u32[]{:S(2)}, u32[]{:S(2)}) collective-permute-start(bf16[256,1280]{0,1:T(8,128)(2,1)} %copy.60), channel_id=1, source_target_pairs={{0,3},{1,0},{2,1},{3,2},{4,7},{5,4},{6,5},{7,6},{8,11},{9,8},{10,9... | collective-permute-start | bytes 1966088 | tf_op jit(solution)/shard_map/ppermute | solution.py:29
  19.1 9.2 %all-gather = s32[8,1,256]{2,1,0:T(1,128)S(1)} all-gather(s32[1,1,256]{2,1,0:T(1,128)} %bitcast.66), channel_id=1, replica_groups=mesh['seq'=8,'fsdp'=4] {'seq'}, dimensions={0}, use_global_device_ids=true | all-gather | bytes 9216 | tf_op jit(solution)/shard_map/all_gather | solution.py:65
  31.5 30.0 %collective-permute-done.3 = bf16[256,1280]{0,1:T(8,128)(2,1)} collective-permute-done((bf16[256,1280]{0,1:T(8,128)(2,1)}, bf16[256,1280]{0,1:T(8,128)(2,1)}, u32[]{:S(2)}, u32[]{:S(2)}) %collective-permute-start.3) | collective-permute-done | bytes 655392 | tf_op jit(solution)/shard_map/ppermute | solution.py:29
  62.6 11.8 %collective-permute-done.4 = bf16[256,1280]{0,1:T(8,128)(2,1)} collective-permute-done((bf16[256,1280]{0,1:T(8,128)(2,1)}, bf16[256,1280]{0,1:T(8,128)(2,1)}, u32[]{:S(2)}, u32[]{:S(2)}) %collective-permute-start.4) | collective-permute-done | bytes 655392 | tf_op jit(solution)/shard_map/ppermute | solution.py:29
  76.7 6.9 %copy.59 = bf16[2048,1024]{0,1:T(8,128)(2,1)} copy(bf16[2048,1024]{1,0:T(8,128)(2,1)} %all-gather.8.cloned.1.call-done) | data formatting | bytes 8388608 | tf_op jit(solution)/shard_map/all_gather | solution.py:64
  83.6 5.4 %all-gather.6.cloned.1.call-done = bf16[2048,1024]{0,1:T(8,128)(2,1)} async-done(((bf16[256,1024]{0,1:T(8,128)(2,1)}), bf16[2048,1024]{0,1:T(8,128)(2,1)}) %all-gather.6.cloned.1.call-update) | async-done | bytes 4194320 | tf_op jit(solution)/shard_map/all_gather | solution.py:63
  89.1 5.3 %fusion.1 = (f32[8,256]{1,0:T(8,128)S(1)}, f32[8,256,2048]{2,1,0:T(8,128)S(1)}) fusion(pred[256,2048]{1,0:T(8,128)(4,1)} %broadcast_compare_fusion, bf16[2048,8,128]{0,2,1:T(8,128)(2,1)} %bitcast.51, bf16[256,1024]{1,0:T(8,128)(2,1)S(1)} %copy-done), kind=kOutput, calls=%fused_computation.5 | convolution fusion | flops 1086322688 | bytes 22028288 | tf_op jit(solution)/shard_map/qhd,khd->hqk/dot_general | solution.py:17
  94.4 4.5 %exponential_reduce_fusion = f32[8,256]{1,0:T(8,128)S(1)} fusion(f32[8,256,2048]{2,1,0:T(8,128)S(1)} %get-tuple-element.33, f32[8,256]{1,0:T(8,128)S(1)} %get-tuple-element.32, pred[256,2048]{1,0:T(8,128)(4,1)S(1)} %copy-done.4), kind=kLoop, calls=%fused_computation.2 | loop fusion | flops 16775168 | bytes 17317888 | tf_op jit(solution)/shard_map/reduce_sum | solution.py:70
  101.3 52.7 %all-gather.10.cloned.1.call-done = bf16[1024,5120]{1,0:T(8,128)(2,1)} async-done(((bf16[1024,640]{1,0:T(8,128)(2,1)}), bf16[1024,5120]{1,0:T(8,128)(2,1)}) %all-gather.10.cloned.1.call-update) | async-done | bytes 10485776 | tf_op jit(solution)/shard_map/all_gather | solution.py:78
  154.0 7.7 %convolution_convert_fusion.1 = bf16[256,1024]{1,0:T(8,128)(2,1)} fusion(bf16[256,5120]{0,1:T(8,128)(2,1)S(1)} %constant_dynamic-update-slice_fusion, bf16[1024,5120]{1,0:T(8,128)(2,1)} %all-gather.10.cloned.1.call-done), kind=kOutput, calls=%fused_computation.12 | convolution fusion | flops 2684616704 | bytes 13631488 | tf_op jit(solution)/shard_map/td,hd->th/dot_general | solution.py:84
  163.0 10.7 %multiply_reduce_fusion = (f32[256,8]{0,1:T(8,128)S(1)}, bf16[8,256,128]{1,2,0:T(8,128)(2,1)}) fusion(bf16[256,1024]{0,1:T(8,128)(2,1)S(1)} %copy.64, bf16[2048,8,128]{0,2,1:T(8,128)(2,1)} %bitcast.55, f32[8,256,2048]{2,1,0:T(8,128)} %copy-done.1, f32[8,256]{1,0:T(8,128)S(1)} %log_add_fusion, pred[256,2048]{1,0:T(8,128)(4,1)} %broadcast_compare_fusion), kind=kOutput, calls=%fused_computation.15 | convolution fusion | flops 1091827712 | bytes 22560768 | tf_op jit(solution)/shard_map/hqk,khd->qhd/dot_general | solution.py:73
  174.0 7.2 %convolution_convert_fusion = bf16[256,5120]{1,0:T(8,128)(2,1)S(1)} fusion(bf16[256,1024]{0,1:T(8,128)(2,1)} %bitcast.60, bf16[1024,5120]{1,0:T(8,128)(2,1)} %all-gather.10.cloned.1.call-done), kind=kOutput, calls=%fused_computation.7 | convolution fusion | flops 2685665280 | bytes 13631488 | tf_op jit(solution)/shard_map/dot_general | solution.py:79
  186.9 10.6 %convert_bitcast_fusion = bf16[2048,8,128]{2,0,1:T(8,128)(2,1)} fusion(bf16[256,8,128]{0,2,1:T(8,128)(2,1)S(1)} %bitcast.63, f32[8,256,2048]{2,1,0:T(8,128)} %copy-done.1, f32[8,256]{1,0:T(8,128)S(1)} %log_add_fusion, pred[256,2048]{1,0:T(8,128)(4,1)S(1)} %copy-done.5), kind=kOutput, calls=%fused_computation.8 | convolution fusion | flops 1092616192 | bytes 22028288 | tf_op jit(solution)/shard_map/hqk,qhd->khd/dot_general | solution.py:106
  197.5 13.0 %multiply_convert_fusion = bf16[8,256,2048]{2,1,0:T(8,128)(2,1)} fusion(f32[8,256,2048]{2,1,0:T(8,128)} %copy-done.1, f32[8,256]{1,0:T(8,128)S(1)} %bitcast.67, f32[8,256]{1,0:T(8,128)S(1)} %log_add_fusion, pred[256,2048]{1,0:T(8,128)(4,1)S(1)} %copy-done.5, bf16[256,8,128]{0,2,1:T(8,128)(2,1)S(1)} %bitcast.64, bf16[2048,8,128]{0,2,1:T(8,128)(2,1)} %bitcast.56), kind=kOutput, calls=%fused_computation | convolution fusion | flops 1098907648 | bytes 30425088 | tf_op jit(solution)/shard_map/qhd,khd->hqk/dot_general | solution.py:96
  210.5 8.1 %convert_bitcast_fusion.1 = bf16[2048,8,128]{2,0,1:T(8,128)(2,1)} fusion(bf16[8,256,2048]{2,1,0:T(8,128)(2,1)} %multiply_convert_fusion, bf16[256,1024]{1,0:T(8,128)(2,1)S(1)} %copy-done), kind=kOutput, calls=%fused_computation.9 | convolution fusion | flops 1075838976 | bytes 13107200 | tf_op jit(solution)/shard_map/hqk,qhd->khd/dot_general | solution.py:103
  218.6 7.4 %pad_maximum_fusion = bf16[2048,16,128]{2,0,1:T(8,128)(2,1)} fusion(bf16[2048,8,128]{2,0,1:T(8,128)(2,1)} %convert_bitcast_fusion, bf16[2048,8,128]{2,0,1:T(8,128)(2,1)} %convert_bitcast_fusion.1), kind=kLoop, calls=%fused_computation.6 | loop fusion | flops 4194304 | bytes 16777216 | tf_op jit(solution)/shard_map/concatenate | solution.py:109
  226.1 17.5 %collective-permute-done.1 = bf16[256,1280]{1,0:T(8,128)(2,1)} collective-permute-done((bf16[256,1280]{1,0:T(8,128)(2,1)}, bf16[256,1280]{1,0:T(8,128)(2,1)}, u32[]{:S(2)}, u32[]{:S(2)}) %collective-permute-start.1) | collective-permute-done | bytes 655392 | tf_op jit(solution)/shard_map/ppermute | solution.py:55
  243.6 2.8 convert_add_fusion
  248.2 46.2 %all_to_all.19 = bf16[256,8,640]{0,2,1:T(8,128)(2,1)} all-to-all(bf16[256,8,640]{0,2,1:T(8,128)(2,1)S(1)} %bitcast.53), channel_id=1, replica_groups=mesh['seq'=8,'fsdp'=4] {'seq'}, dimensions={1} | all-to-all | bytes 5242880 | tf_op jit(solution)/shard_map/all_to_all | solution.py:88
  294.4 3.2 copy.72
  297.5 8.6 %convolution_multiply_fusion = f32[8,256,128]{1,2,0:T(8,128)} fusion(bf16[8,256,2048]{2,1,0:T(8,128)(2,1)} %multiply_convert_fusion, bf16[2048,8,128]{0,2,1:T(8,128)(2,1)} %bitcast.52), kind=kOutput, calls=%fused_computation.10 | convolution fusion | flops 1074003968 | bytes 13631488 | tf_op jit(solution)/shard_map/hqk,khd->qhd/dot_general | solution.py:100
  306.2 2.5 copy.73
  308.7 7.8 %fusion.9 = f32[1024,640]{1,0:T(8,128)} fusion(bf16[2048,1024]{0,1:T(8,128)(2,1)} %all-gather.12.cloned.1.call-done, bf16[2048,640]{1,0:T(8,128)(2,1)S(1)} %bitcast.61), kind=kOutput, calls=%fused_computation.30 | convolution fusion | flops 2684354560 | bytes 9437184 | tf_op jit(solution)/shard_map/th,td->hd/dot_general | solution.py:89
  316.5 8.3 %reduce-scatter.2.cloned.1.call-done = bf16[256,16,128]{2,0,1:T(8,128)(2,1)} async-done(((bf16[2048,16,128]{2,0,1:T(8,128)(2,1)}), bf16[256,16,128]{2,0,1:T(8,128)(2,1)}) %reduce-scatter.2.cloned.1.call-update) | async-done | bytes 1048592 | tf_op jit(solution)/shard_map/reduce_scatter | solution.py:111
  (56 shorter events, 31.7 us)
Async XLA Ops:
  7.2 81.9 %copy-start = (bf16[256,1024]{1,0:T(8,128)(2,1)S(1)}, bf16[256,1024]{1,0:T(8,128)(2,1)}, u32[]{:S(2)}) copy-start(bf16[256,1024]{1,0:T(8,128)(2,1)} %param.6) | copy-start | bytes 1572868
  7.2 69.6 %all-gather.8.cloned.1.call-start = ((), (), s32[]{:S(2)}) async-start(), calls=%async_computation.3 | async-start | bytes 4718592 | tf_op jit(solution)/shard_map/all_gather | solution.py:64
  7.9 81.1 %all-gather.6.cloned.1.call-start = ((), (), s32[]{:S(2)}) async-start(), calls=%async_computation.2 | async-start | bytes 4718592 | tf_op jit(solution)/shard_map/all_gather | solution.py:63
  10.0 144.0 %all-gather.10.cloned.1.call-start = ((), (), s32[]{:S(2)}) async-start(), calls=%async_computation.4 | async-start | bytes 11796480 | tf_op jit(solution)/shard_map/all_gather | solution.py:78
  10.8 297.9 %all-gather.12.cloned.1.call-start = ((), (), s32[]{:S(2)}) async-start(), calls=%async_computation.6 | async-start | bytes 4718592 | tf_op jit(solution)/shard_map/all_gather | solution.py:87
  13.0 62.6 %collective-permute-start.5 = (bf16[256,1280]{0,1:T(8,128)(2,1)}, bf16[256,1280]{0,1:T(8,128)(2,1)}, u32[]{:S(2)}, u32[]{:S(2)}) collective-permute-start(bf16[256,1280]{0,1:T(8,128)(2,1)} %copy.60), channel_id=1, source_target_pairs={{0,3},{1,0},{2,1},{3,2},{4,7},{5,4},{6,5},{7,6},{8,11},{9,8},{10,9... | collective-permute-start | bytes 1966088 | tf_op jit(solution)/shard_map/ppermute | solution.py:29
  18.1 56.3 %collective-permute-start.4 = (bf16[256,1280]{0,1:T(8,128)(2,1)}, bf16[256,1280]{0,1:T(8,128)(2,1)}, u32[]{:S(2)}, u32[]{:S(2)}) collective-permute-start(bf16[256,1280]{0,1:T(8,128)(2,1)} %copy.60), channel_id=1, source_target_pairs={{0,2},{1,3},{2,0},{3,1},{4,6},{5,7},{6,4},{7,5},{8,10},{9,11},{10,... | collective-permute-start | bytes 1966088 | tf_op jit(solution)/shard_map/ppermute | solution.py:29
  18.1 43.4 %collective-permute-start.3 = (bf16[256,1280]{0,1:T(8,128)(2,1)}, bf16[256,1280]{0,1:T(8,128)(2,1)}, u32[]{:S(2)}, u32[]{:S(2)}) collective-permute-start(bf16[256,1280]{0,1:T(8,128)(2,1)} %copy.60), channel_id=1, source_target_pairs={{0,1},{1,2},{2,3},{3,0},{4,5},{5,6},{6,7},{7,4},{8,9},{9,10},{10,1... | collective-permute-start | bytes 1966088 | tf_op jit(solution)/shard_map/ppermute | solution.py:29
  76.7 77.3 %copy-start.2 = (bf16[256,5120]{0,1:T(8,128)(2,1)}, bf16[256,5120]{0,1:T(8,128)(2,1)S(1)}, u32[]{:S(2)}) copy-start(bf16[256,5120]{0,1:T(8,128)(2,1)S(1)} %constant_dynamic-update-slice_fusion) | copy-start | bytes 7864324
  89.1 5.4 %copy-start.4 = (pred[256,2048]{1,0:T(8,128)(4,1)S(1)}, pred[256,2048]{1,0:T(8,128)(4,1)}, u32[]{:S(2)}) copy-start(pred[256,2048]{1,0:T(8,128)(4,1)} %broadcast_compare_fusion) | copy-start | bytes 1572868
  94.4 6.9 %copy-start.1 = (f32[8,256,2048]{2,1,0:T(8,128)}, f32[8,256,2048]{2,1,0:T(8,128)S(1)}, u32[]{:S(2)}) copy-start(f32[8,256,2048]{2,1,0:T(8,128)S(1)} %get-tuple-element.33) | copy-start | bytes 50331652
  163.0 10.7 %copy-start.7 = (bf16[256,1024]{0,1:T(8,128)(2,1)}, bf16[256,1024]{0,1:T(8,128)(2,1)S(1)}, u32[]{:S(2)}) copy-start(bf16[256,1024]{0,1:T(8,128)(2,1)S(1)} %copy.64) | copy-start | bytes 1572868
  173.7 151.2 %reduce-scatter.2.cloned.1.call-start = ((), (), s32[]{:S(2)}) async-start(), calls=%async_computation.5 | async-start | bytes 9437184 | tf_op jit(solution)/shard_map/reduce_scatter | solution.py:111
  173.9 13.0 %copy-start.5 = (pred[256,2048]{1,0:T(8,128)(4,1)S(1)}, pred[256,2048]{1,0:T(8,128)(4,1)}, u32[]{:S(2)}) copy-start(pred[256,2048]{1,0:T(8,128)(4,1)} %broadcast_compare_fusion) | copy-start | bytes 1572868
  173.9 12.9 %copy-start.8 = (bf16[256,1024]{0,1:T(8,128)(2,1)S(1)}, bf16[256,1024]{0,1:T(8,128)(2,1)}, u32[]{:S(2)}) copy-start(bf16[256,1024]{0,1:T(8,128)(2,1)} %copy-done.7) | copy-start | bytes 1572868
  182.4 43.6 %collective-permute-start = (bf16[256,1280]{1,0:T(8,128)(2,1)}, bf16[256,1280]{1,0:T(8,128)(2,1)}, u32[]{:S(2)}, u32[]{:S(2)}) collective-permute-start(bf16[256,1280]{1,0:T(8,128)(2,1)} %get-tuple-element.29), channel_id=1, source_target_pairs={{0,1},{1,2},{2,3},{3,0},{4,5},{5,6},{6,7},{7,4},{8,9},{9,10},{10,1... | collective-permute-start | bytes 1966088 | tf_op jit(solution)/shard_map/ppermute | solution.py:55
  183.9 42.1 %collective-permute-start.2 = (bf16[256,1280]{1,0:T(8,128)(2,1)}, bf16[256,1280]{1,0:T(8,128)(2,1)}, u32[]{:S(2)}, u32[]{:S(2)}) collective-permute-start(bf16[256,1280]{1,0:T(8,128)(2,1)} %get-tuple-element.30), channel_id=1, source_target_pairs={{0,3},{1,0},{2,1},{3,2},{4,7},{5,4},{6,5},{7,6},{8,11},{9,8},{10,9... | collective-permute-start | bytes 1966088 | tf_op jit(solution)/shard_map/ppermute | solution.py:55
  186.3 57.3 %collective-permute-start.1 = (bf16[256,1280]{1,0:T(8,128)(2,1)}, bf16[256,1280]{1,0:T(8,128)(2,1)}, u32[]{:S(2)}, u32[]{:S(2)}) collective-permute-start(bf16[256,1280]{1,0:T(8,128)(2,1)} %get-tuple-element.31), channel_id=1, source_target_pairs={{0,2},{1,3},{2,0},{3,1},{4,6},{5,7},{6,4},{7,5},{8,10},{9,11},{10,... | collective-permute-start | bytes 1966088 | tf_op jit(solution)/shard_map/ppermute | solution.py:55
  246.4 1.7 copy-start.3
  324.8 5.0 %copy-start.6 = (bf16[256,16,128]{2,0,1:T(8,128)(2,1)S(1)}, bf16[256,16,128]{2,0,1:T(8,128)(2,1)}, u32[]{:S(2)}) copy-start(bf16[256,16,128]{2,0,1:T(8,128)(2,1)} %reduce-scatter.2.cloned.1.call-done) | copy-start | bytes 3145732
Sparse Core Ops, SparseCore 0:
  9.9 39.3 all-gather.7
  51.7 37.3 all-gather.5
  91.0 63.0 all-gather.9
  173.8 37.3 all-gather.11
  246.6 78.2 reduce-scatter.1

commit v5 on v3

--- a/solution.py
+++ b/solution.py
@@ -93,25 +93,40 @@
     row_delta = jnp.sum(
         grad_heads.astype(jnp.float32) * attended_heads.astype(jnp.float32), axis=2
     ).T
-    grad_probs = jnp.einsum(
-        "qhd,khd->hqk", grad_heads, value_heads, preferred_element_type=jnp.float32
-    )
-    grad_scores = (probs * (grad_probs - row_delta[:, :, None])).astype(jnp.bfloat16)
-    query_sum = jnp.einsum(
-        "hqk,khd->qhd", grad_scores, key_heads, preferred_element_type=jnp.float32
-    )
-    key_part = jnp.einsum(
-        "hqk,qhd->khd", grad_scores, query_heads, preferred_element_type=jnp.float32
-    )
-    value_part = jnp.einsum(
-        "hqk,qhd->khd", weights, grad_heads, preferred_element_type=jnp.float32
-    )
-    both_parts = jnp.concatenate([key_part, value_part], axis=1).astype(jnp.bfloat16)
-    both_sums = lax.psum_scatter(both_parts, "seq", scatter_dimension=0, tiled=True).astype(
-        jnp.float32
-    )
-    key_sum = both_sums[:, :local_heads]
-    value_sum = both_sums[:, local_heads:]
+    halves = 2 if local_heads % 2 == 0 else 1
+    span = local_heads // halves
+    query_sums, key_sums, value_sums = [], [], []
+    for half in range(halves):
+        heads = slice(half * span, (half + 1) * span)
+        half_grads = grad_heads[:, heads]
+        grad_probs = jnp.einsum(
+            "qhd,khd->hqk", half_grads, value_heads[:, heads], preferred_element_type=jnp.float32
+        )
+        grad_scores = (probs[heads] * (grad_probs - row_delta[heads, :, None])).astype(
+            jnp.bfloat16
+        )
+        query_sums.append(
+            jnp.einsum(
+                "hqk,khd->qhd", grad_scores, key_heads[:, heads], preferred_element_type=jnp.float32
+            )
+        )
+        key_part = jnp.einsum(
+            "hqk,qhd->khd", grad_scores, query_heads[:, heads], preferred_element_type=jnp.float32
+        )
+        value_part = jnp.einsum(
+            "hqk,qhd->khd", weights[heads], half_grads, preferred_element_type=jnp.float32
+        )
+        both_parts = jnp.concatenate([key_part, value_part], axis=1).astype(jnp.bfloat16)
+        if half == 0:
+            attn_output, both_parts = lax.optimization_barrier((attn_output, both_parts))
+        both_sums = lax.psum_scatter(both_parts, "seq", scatter_dimension=0, tiled=True).astype(
+            jnp.float32
+        )
+        key_sums.append(both_sums[:, :span])
+        value_sums.append(both_sums[:, span:])
+    query_sum = jnp.concatenate(query_sums, axis=1)
+    key_sum = jnp.concatenate(key_sums, axis=1)
+    value_sum = jnp.concatenate(value_sums, axis=1)
     score_scale = HEAD_DIM ** (-0.5)
     grad_queries = (query_sum * score_scale).reshape(local_tokens, local_heads * HEAD_DIM)
     grad_keys = (key_sum * score_scale).reshape(local_tokens, local_heads * HEAD_DIM)

time: 353 us -> 375 us (1.062)
  blocking collectives: 9.29 us -> 44.5 us
  matrix products: 77.3 us -> 67 us
    all_to_all x1 -> x0, waiting for transfers between devices: 40.1 us -> none  [shards(): cotangent_cols = lax.all_to_all(cotangent_full, 'seq', 1, 0, tiled=True)]
    all_to_all x0 -> x1, blocking collectives: none -> 35.4 us  [shards(): cotangent_cols = lax.all_to_all(cotangent_full, 'seq', 1, 0, tiled=True)]
    all_gather x1, waiting for transfers between devices: 0.01 us -> 34.5 us  [shards(): all_attended = lax.all_gather(attended_flat, 'seq', axis=0, tiled=True)]
    reduce_scatter x1 -> x2, waiting for transfers between devices: 0.01 us -> 22.9 us  [shards(): lax.psum_scatter(both_parts, 'seq', scatter_dimension=0, tiled=True)]
    ppermute x3, waiting for transfers between devices: 41.6 us -> 27.5 us  [permute_sum_scatter(): total = total + lax.ppermute(piece, axis, route).astype(jnp.float32)]
    convert_element_type x1, other arithmetic: 1.51 us -> 9.46 us  [shards(): weights = probs.astype(jnp.bfloat16)]
    all_gather x1, waiting for transfers between devices: 52.7 us -> 45.5 us  [shards(): weight_full = lax.all_gather(out_weight, 'seq', axis=1, tiled=True)]
    dot_general x4 -> x8, matrix products: 37.4 us -> 30.2 us  [the longest x2 8.65 us: shards(): jnp.einsum('hqk,qhd->khd', weights[heads], half_grads, preferred_element_...]
  transfers between devices with their start and end apart: 12 -> 12, of which waited for: 7 -> 8; matrix products, arithmetic and copies ran while one was open for 28% -> 22% of each run, Pallas kernels for 0% -> 0%
where the time goes in v5:
time: 375 us; the launch traced here: 374 us
  waiting for transfers between devices  179 us (48%)
  matrix products  67 us (18%)
  blocking collectives  44.5 us (12%)
  local copies, waits for them, and re-layouts  34.2 us (9%)
  other arithmetic  22.1 us (6%)
  between operations  14.6 us (4%)
  starting transfers between devices  12.6 us (3%)
    all_gather x1, waiting for transfers between devices, shards(): weight_full = lax.all_gather(out_weight, 'seq', axis=1, tiled=True)  45.5 us
    all_to_all x1, blocking collectives, shards(): cotangent_cols = lax.all_to_all(cotangent_full, 'seq', 1, 0, tiled=True)  35.4 us
    all_gather x1, waiting for transfers between devices, shards(): all_attended = lax.all_gather(attended_flat, 'seq', axis=0, tiled=True)  34.5 us
    ppermute x3, waiting for transfers between devices, shift_pieces(): pieces.append(lax.ppermute(block, axis, route))  28.3 us
    ppermute x3, waiting for transfers between devices, permute_sum_scatter(): total = total + lax.ppermute(piece, axis, route).astype(jnp.float32)  27.5 us
    reduce_scatter x2, waiting for transfers between devices, shards(): lax.psum_scatter(both_parts, 'seq', scatter_dimension=0, tiled=True)  22.9 us
    all_gather x1, waiting for transfers between devices, shards(): all_keys = lax.all_gather(key_states, 'seq', axis=0, tiled=True)  18.5 us
    unnamed x36, local copies, waits for them, and re-layouts  12.4 us
  transfers between devices with their start and end apart: 12, of which 8 were waited for; matrix products, arithmetic and copies ran while one was open for 22% of the time, Pallas kernels for 0%

profile of v5, /device:TPU:0, one launch (start us, length us, event | category | flops | bytes accessed | tf_op | source)
XLA Modules:
  0.0 374.0 jit_solution(13934152995788470795)
XLA Ops:
  20.0 9.1 %all-gather = s32[8,1,256]{2,1,0:T(1,128)S(1)} all-gather(s32[1,1,256]{2,1,0:T(1,128)S(1)} %bitcast.73), channel_id=1, replica_groups=mesh['seq'=8,'fsdp'=4] {'seq'}, dimensions={0}, use_global_device_ids=true | all-gather | bytes 9216 | tf_op jit(solution)/shard_map/all_gather | solution.py:65
  35.3 26.0 %collective-permute-done.4 = bf16[256,1280]{0,1:T(8,128)(2,1)} collective-permute-done((bf16[256,1280]{0,1:T(8,128)(2,1)}, bf16[256,1280]{0,1:T(8,128)(2,1)}, u32[]{:S(2)}, u32[]{:S(2)}) %collective-permute-start.4) | collective-permute-done | bytes 655392 | tf_op jit(solution)/shard_map/ppermute | solution.py:29
  63.7 6.9 %copy.82 = bf16[2048,1024]{0,1:T(8,128)(2,1)} copy(bf16[2048,1024]{1,0:T(8,128)(2,1)} %all-gather.8.cloned.1.call-done) | data formatting | bytes 8388608 | tf_op jit(solution)/shard_map/all_gather | solution.py:64
  70.5 18.5 %all-gather.6.cloned.1.call-done = bf16[2048,1024]{0,1:T(8,128)(2,1)} async-done(((bf16[256,1024]{0,1:T(8,128)(2,1)}), bf16[2048,1024]{0,1:T(8,128)(2,1)}) %all-gather.6.cloned.1.call-update) | async-done | bytes 4194320 | tf_op jit(solution)/shard_map/all_gather | solution.py:63
  89.0 5.4 %fusion = (f32[8,256]{1,0:T(8,128)S(1)}, f32[8,256,2048]{2,1,0:T(8,128)S(1)}) fusion(pred[256,2048]{1,0:T(8,128)(4,1)S(1)} %broadcast_compare_fusion, bf16[256,8,128]{0,2,1:T(8,128)(2,1)} %bitcast.55, bf16[2048,8,128]{0,2,1:T(8,128)(2,1)} %bitcast.50), kind=kOutput, calls=%fused_computation.3 | convolution fusion | flops 1086322688 | bytes 22028288 | tf_op jit(solution)/shard_map/qhd,khd->hqk/dot_general | solution.py:17
  94.5 4.5 %exponential_reduce_fusion = f32[8,256]{1,0:T(8,128)S(1)} fusion(f32[8,256,2048]{2,1,0:T(8,128)S(1)} %get-tuple-element.36, f32[8,256]{1,0:T(8,128)S(1)} %get-tuple-element.35, pred[256,2048]{1,0:T(8,128)(4,1)S(1)} %broadcast_compare_fusion), kind=kLoop, calls=%fused_computation.1 | loop fusion | flops 16775168 | bytes 17317888 | tf_op jit(solution)/shard_map/reduce_sum | solution.py:70
  99.0 9.5 %fusion.35 = (bf16[8,256,2048]{2,1,0:T(8,128)(2,1)}, f32[8,256,2048]{2,1,0:T(8,128)}) fusion(f32[8,256]{1,0:T(8,128)S(1)} %log_add_fusion, f32[8,256,2048]{2,1,0:T(8,128)S(1)} %get-tuple-element.36, pred[256,2048]{1,0:T(8,128)(4,1)S(1)} %broadcast_compare_fusion), kind=kLoop, calls=%fused_computation.49 | loop fusion | flops 16777216 | bytes 42475520 | tf_op jit(solution)/shard_map/convert_element_type | solution.py:72
  108.5 45.5 %all-gather.10.cloned.1.call-done = bf16[1024,5120]{1,0:T(8,128)(2,1)} async-done(((bf16[1024,640]{1,0:T(8,128)(2,1)}), bf16[1024,5120]{1,0:T(8,128)(2,1)}) %all-gather.10.cloned.1.call-update) | async-done | bytes 10485776 | tf_op jit(solution)/shard_map/all_gather | solution.py:78
  154.0 7.7 %convolution_convert_fusion.3 = bf16[256,1024]{1,0:T(8,128)(2,1)} fusion(bf16[256,5120]{0,1:T(8,128)(2,1)S(1)} %constant_dynamic-update-slice_fusion, bf16[1024,5120]{1,0:T(8,128)(2,1)} %all-gather.10.cloned.1.call-done), kind=kOutput, calls=%fused_computation.30 | convolution fusion | flops 2684616704 | bytes 13631488 | tf_op jit(solution)/shard_map/td,hd->th/dot_general | solution.py:84
  162.9 8.5 %multiply_reduce_fusion = (f32[256,8]{0,1:T(8,128)S(1)}, bf16[8,256,128]{1,2,0:T(8,128)(2,1)}) fusion(bf16[256,1024]{0,1:T(8,128)(2,1)S(1)} %copy.87, bf16[8,256,2048]{2,1,0:T(8,128)(2,1)} %get-tuple-element.24, bf16[2048,8,128]{0,2,1:T(8,128)(2,1)} %bitcast.58), kind=kOutput, calls=%fused_computation.37 | convolution fusion | flops 1075050496 | bytes 13639680 | tf_op jit(solution)/shard_map/hqk,khd->qhd/dot_general | solution.py:73
  171.4 4.0 %fusion.15 = bf16[2048,4,128]{2,0,1:T(8,128)(2,1)S(1)} fusion(bf16[256,8,128]{0,2,1:T(8,128)(2,1)S(1)} %bitcast.67, bf16[8,256,2048]{2,1,0:T(8,128)(2,1)} %get-tuple-element.24), kind=kOutput, calls=%fused_computation.21 | convolution fusion | flops 537919488 | bytes 6815744 | tf_op jit(solution)/shard_map/hqk,qhd->khd/dot_general | solution.py:116
  175.5 4.7 %fusion.1 = bf16[4,256,2048]{2,1,0:T(8,128)(2,1)S(1)} fusion(f32[8,256,2048]{2,1,0:T(8,128)} %get-tuple-element.25, f32[4,256]{1,0:T(4,128)S(1)} %get-tuple-element.33, bf16[256,8,128]{0,2,1:T(8,128)(2,1)S(1)} %bitcast.68, bf16[2048,8,128]{0,2,1:T(8,128)(2,1)S(1)} %bitcast.59), kind=kOutput, calls=%fused_computation.5 | convolution fusion | flops 543162368 | bytes 15208448 | tf_op jit(solution)/shard_map/qhd,khd->hqk/dot_general | solution.py:102
  186.4 7.2 %convolution_convert_fusion = bf16[256,5120]{1,0:T(8,128)(2,1)S(1)} fusion(bf16[256,1024]{0,1:T(8,128)(2,1)} %bitcast.64, bf16[1024,5120]{1,0:T(8,128)(2,1)} %all-gather.10.cloned.1.call-done), kind=kOutput, calls=%fused_computation.8 | convolution fusion | flops 2685665280 | bytes 13631488 | tf_op jit(solution)/shard_map/dot_general | solution.py:79
  200.3 4.6 %fusion.18 = bf16[2048,4,128]{2,0,1:T(8,128)(2,1)S(1)} fusion(bf16[256,8,128]{0,2,1:T(8,128)(2,1)S(1)} %bitcast.69, bf16[8,256,2048]{2,1,0:T(8,128)(2,1)} %get-tuple-element.24), kind=kOutput, calls=%fused_computation.22 | convolution fusion | flops 537919488 | bytes 6815744 | tf_op jit(solution)/shard_map/hqk,qhd->khd/dot_general | solution.py:116
  205.0 3.3 fusion.2
  208.3 4.1 %fusion.13 = bf16[2048,4,128]{2,0,1:T(8,128)(2,1)S(1)} fusion(bf16[4,256,2048]{2,1,0:T(8,128)(2,1)} %fusion.2, bf16[256,8,128]{0,2,1:T(8,128)(2,1)S(1)} %bitcast.57), kind=kOutput, calls=%fused_computation.19 | convolution fusion | flops 537919488 | bytes 6553600 | tf_op jit(solution)/shard_map/hqk,qhd->khd/dot_general | solution.py:113
  214.8 27.4 %collective-permute-done.1 = bf16[256,1280]{1,0:T(8,128)(2,1)} collective-permute-done((bf16[256,1280]{1,0:T(8,128)(2,1)}, bf16[256,1280]{1,0:T(8,128)(2,1)}, u32[]{:S(2)}, u32[]{:S(2)}) %collective-permute-start.1) | collective-permute-done | bytes 655392 | tf_op jit(solution)/shard_map/ppermute | solution.py:55
  246.7 35.4 %all_to_all.19 = bf16[256,8,640]{0,2,1:T(8,128)(2,1)} all-to-all(bf16[256,8,640]{0,2,1:T(8,128)(2,1)S(1)} %bitcast.53), channel_id=1, replica_groups=mesh['seq'=8,'fsdp'=4] {'seq'}, dimensions={1} | all-to-all | bytes 5242880 | tf_op jit(solution)/shard_map/all_to_all | solution.py:88
  282.1 4.5 %copy.103 = bf16[8,256,640]{2,1,0:T(8,128)(2,1)} copy(bf16[8,256,640]{1,2,0:T(8,128)(2,1)} %bitcast.54) | data formatting | bytes 5242880 | tf_op jit(solution)/shard_map/all_to_all | solution.py:88
  286.6 4.3 %fusion.30 = f32[256,4,128]{2,0,1:T(8,128)S(1)} fusion(bf16[4,256,2048]{2,1,0:T(8,128)(2,1)} %copy-done.4, bf16[2048,8,128]{0,2,1:T(8,128)(2,1)} %bitcast.51), kind=kOutput, calls=%fused_computation.33 | convolution fusion | flops 536870912 | bytes 6815744 | tf_op jit(solution)/shard_map/hqk,khd->qhd/dot_general | solution.py:109
  290.9 3.5 fusion.27
  297.3 22.9 %reduce-scatter.3.cloned.1.call-done = bf16[256,8,128]{2,0,1:T(8,128)(2,1)} async-done(((bf16[2048,8,128]{2,0,1:T(8,128)(2,1)}), bf16[256,8,128]{2,0,1:T(8,128)(2,1)}) %reduce-scatter.3.cloned.1.call-update) | async-done | bytes 524304 | tf_op jit(solution)/shard_map/reduce_scatter | solution.py:122
  324.8 34.5 %all-gather.12.cloned.1.call-done = bf16[2048,1024]{0,1:T(8,128)(2,1)} async-done(((bf16[256,1024]{0,1:T(8,128)(2,1)}), bf16[2048,1024]{0,1:T(8,128)(2,1)}) %all-gather.12.cloned.1.call-update) | async-done | bytes 4194320 | tf_op jit(solution)/shard_map/all_gather | solution.py:87
  359.3 7.9 %fusion.39 = f32[1024,640]{1,0:T(8,128)} fusion(bf16[2048,1024]{0,1:T(8,128)(2,1)} %all-gather.12.cloned.1.call-done, bf16[2048,640]{1,0:T(8,128)(2,1)} %bitcast.66), kind=kOutput, calls=%fused_computation.53 | convolution fusion | flops 2684354560 | bytes 9437184 | tf_op jit(solution)/shard_map/th,td->hd/dot_general | solution.py:89
  (82 shorter events, 49.6 us)
Async XLA Ops:
  7.2 12.8 %copy-start.10 = (s32[256]{0:T(256)S(1)}, s32[256]{0:T(256)}, u32[]{:S(2)}) copy-start(s32[256]{0:T(256)} %param.9) | copy-start | bytes 3076
  7.2 22.4 %copy-start.7 = (bf16[256,1024]{1,0:T(8,128)(2,1)S(1)}, bf16[256,1024]{1,0:T(8,128)(2,1)}, u32[]{:S(2)}) copy-start(bf16[256,1024]{1,0:T(8,128)(2,1)} %param.6) | copy-start | bytes 1572868
  7.2 56.5 %all-gather.8.cloned.1.call-start = ((), (), s32[]{:S(2)}) async-start(), calls=%async_computation.4 | async-start | bytes 4718592 | tf_op jit(solution)/shard_map/all_gather | solution.py:64
  7.9 81.1 %all-gather.6.cloned.1.call-start = ((), (), s32[]{:S(2)}) async-start(), calls=%async_computation.3 | async-start | bytes 4718592 | tf_op jit(solution)/shard_map/all_gather | solution.py:63
  10.0 143.9 %all-gather.10.cloned.1.call-start = ((), (), s32[]{:S(2)}) async-start(), calls=%async_computation.5 | async-start | bytes 11796480 | tf_op jit(solution)/shard_map/all_gather | solution.py:78
  10.8 285.4 %reduce-scatter.5.cloned.1.call-start = ((), (), s32[]{:S(2)}) async-start(), calls=%async_computation.7 | async-start | bytes 4718592 | tf_op jit(solution)/shard_map/reduce_scatter | solution.py:122
  13.0 21.1 %collective-permute-start.3 = (bf16[256,1280]{0,1:T(8,128)(2,1)}, bf16[256,1280]{0,1:T(8,128)(2,1)}, u32[]{:S(2)}, u32[]{:S(2)}) collective-permute-start(bf16[256,1280]{0,1:T(8,128)(2,1)} %copy.83), channel_id=1, source_target_pairs={{0,1},{1,2},{2,3},{3,0},{4,5},{5,6},{6,7},{7,4},{8,9},{9,10},{10,1... | collective-permute-start | bytes 1966088 | tf_op jit(solution)/shard_map/ppermute | solution.py:29
  16.0 45.3 %collective-permute-start.4 = (bf16[256,1280]{0,1:T(8,128)(2,1)}, bf16[256,1280]{0,1:T(8,128)(2,1)}, u32[]{:S(2)}, u32[]{:S(2)}) collective-permute-start(bf16[256,1280]{0,1:T(8,128)(2,1)} %copy.83), channel_id=1, source_target_pairs={{0,2},{1,3},{2,0},{3,1},{4,6},{5,7},{6,4},{7,5},{8,10},{9,11},{10,... | collective-permute-start | bytes 1966088 | tf_op jit(solution)/shard_map/ppermute | solution.py:29
  18.6 43.8 %collective-permute-start.5 = (bf16[256,1280]{0,1:T(8,128)(2,1)}, bf16[256,1280]{0,1:T(8,128)(2,1)}, u32[]{:S(2)}, u32[]{:S(2)}) collective-permute-start(bf16[256,1280]{0,1:T(8,128)(2,1)} %copy.83), channel_id=1, source_target_pairs={{0,3},{1,0},{2,1},{3,2},{4,7},{5,4},{6,5},{7,6},{8,11},{9,8},{10,9... | collective-permute-start | bytes 1966088 | tf_op jit(solution)/shard_map/ppermute | solution.py:29
  63.6 90.4 %copy-start.1 = (bf16[256,5120]{0,1:T(8,128)(2,1)}, bf16[256,5120]{0,1:T(8,128)(2,1)S(1)}, u32[]{:S(2)}) copy-start(bf16[256,5120]{0,1:T(8,128)(2,1)S(1)} %constant_dynamic-update-slice_fusion) | copy-start | bytes 7864324
  162.9 12.5 %copy-start.8 = (bf16[256,1024]{0,1:T(8,128)(2,1)}, bf16[256,1024]{0,1:T(8,128)(2,1)S(1)}, u32[]{:S(2)}) copy-start(bf16[256,1024]{0,1:T(8,128)(2,1)S(1)} %copy.87) | copy-start | bytes 1572868
  175.5 6.7 %copy-start.3 = (bf16[256,1024]{0,1:T(8,128)(2,1)S(1)}, bf16[256,1024]{0,1:T(8,128)(2,1)}, u32[]{:S(2)}) copy-start(bf16[256,1024]{0,1:T(8,128)(2,1)} %copy.78) | copy-start | bytes 1572868
  186.2 133.9 %reduce-scatter.3.cloned.1.call-start = ((), (), s32[]{:S(2)}) async-start(), calls=%async_computation.6 | async-start | bytes 4718592 | tf_op jit(solution)/shard_map/reduce_scatter | solution.py:122
  186.3 13.9 %copy-start.9 = (bf16[256,1024]{0,1:T(8,128)(2,1)S(1)}, bf16[256,1024]{0,1:T(8,128)(2,1)}, u32[]{:S(2)}) copy-start(bf16[256,1024]{0,1:T(8,128)(2,1)} %copy-done.8) | copy-start | bytes 1572868
  186.3 18.6 %slice-start = ((s8[16777216]{0:T(1024)(128)(4,1)}), s8[4194304]{0:T(1024)(128)(4,1)S(1)}, s32[]{:S(2)}) async-start(s8[16777216]{0:T(1024)(128)(4,1)} %bitcast.48), calls=%async_computation.9 | async-start | bytes 8388608
  186.4 18.6 %slice-start.1 = ((s8[16777216]{0:T(1024)(128)(4,1)}), s8[4194304]{0:T(1024)(128)(4,1)S(1)}, s32[]{:S(2)}) async-start(s8[16777216]{0:T(1024)(128)(4,1)} %bitcast.48), calls=%async_computation.10 | async-start | bytes 8388608
  193.6 11.3 %slice-start.2 = ((s8[16777216]{0:T(1024)(128)(4,1)}), s8[4194304]{0:T(1024)(128)(4,1)S(1)}, s32[]{:S(2)}) async-start(s8[16777216]{0:T(1024)(128)(4,1)} %bitcast.48), calls=%async_computation.11 | async-start | bytes 8388608
  194.9 19.9 %collective-permute-start = (bf16[256,1280]{1,0:T(8,128)(2,1)}, bf16[256,1280]{1,0:T(8,128)(2,1)}, u32[]{:S(2)}, u32[]{:S(2)}) collective-permute-start(bf16[256,1280]{1,0:T(8,128)(2,1)} %get-tuple-element.26), channel_id=1, source_target_pairs={{0,1},{1,2},{2,3},{3,0},{4,5},{5,6},{6,7},{7,4},{8,9},{9,10},{10,1... | collective-permute-start | bytes 1966088 | tf_op jit(solution)/shard_map/ppermute | solution.py:55
  196.4 45.7 %collective-permute-start.1 = (bf16[256,1280]{1,0:T(8,128)(2,1)}, bf16[256,1280]{1,0:T(8,128)(2,1)}, u32[]{:S(2)}, u32[]{:S(2)}) collective-permute-start(bf16[256,1280]{1,0:T(8,128)(2,1)} %get-tuple-element.28), channel_id=1, source_target_pairs={{0,2},{1,3},{2,0},{3,1},{4,6},{5,7},{6,4},{7,5},{8,10},{9,11},{10,... | collective-permute-start | bytes 1966088 | tf_op jit(solution)/shard_map/ppermute | solution.py:55
  198.8 6.1 %slice-start.3 = ((s8[16777216]{0:T(1024)(128)(4,1)}), s8[4194304]{0:T(1024)(128)(4,1)S(1)}, s32[]{:S(2)}) async-start(s8[16777216]{0:T(1024)(128)(4,1)} %bitcast.48), calls=%async_computation.12 | async-start | bytes 8388608
  198.8 6.1 %copy-start.6 = (bf16[2048,1024]{0,1:T(8,128)(2,1)S(1)}, bf16[2048,1024]{0,1:T(8,128)(2,1)}, u32[]{:S(2)}) copy-start(bf16[2048,1024]{0,1:T(8,128)(2,1)} %copy.82) | copy-start | bytes 12582916
  198.8 43.3 %collective-permute-start.2 = (bf16[256,1280]{1,0:T(8,128)(2,1)}, bf16[256,1280]{1,0:T(8,128)(2,1)}, u32[]{:S(2)}, u32[]{:S(2)}) collective-permute-start(bf16[256,1280]{1,0:T(8,128)(2,1)} %get-tuple-element.27), channel_id=1, source_target_pairs={{0,3},{1,0},{2,1},{3,2},{4,7},{5,4},{6,5},{7,6},{8,11},{9,8},{10,9... | collective-permute-start | bytes 1966088 | tf_op jit(solution)/shard_map/ppermute | solution.py:55
  245.0 114.3 %all-gather.12.cloned.1.call-start = ((), (), s32[]{:S(2)}) async-start(), calls=%async_computation.8 | async-start | bytes 4718592 | tf_op jit(solution)/shard_map/all_gather | solution.py:87
  286.6 4.3 %copy-start = (bf16[2048,1024]{0,1:T(8,128)(2,1)S(1)}, bf16[2048,1024]{0,1:T(8,128)(2,1)}, u32[]{:S(2)}) copy-start(bf16[2048,1024]{0,1:T(8,128)(2,1)} %all-gather.6.cloned.1.call-done) | copy-start | bytes 12582916
  (3 other events, 7.8 us)
Sparse Core Ops, SparseCore 0:
  9.9 39.2 all-gather.7
  51.7 37.3 all-gather.5
  91.0 62.9 all-gather.9
  186.4 51.0 reduce-scatter.4
  245.1 74.9 reduce-scatter.2
  321.9 37.3 all-gather.11

commit v6 on v5

--- a/solution.py
+++ b/solution.py
@@ -86,9 +86,6 @@
     ).astype(jnp.bfloat16)
     all_attended = lax.all_gather(attended_flat, "seq", axis=0, tiled=True)
     cotangent_cols = lax.all_to_all(cotangent_full, "seq", 1, 0, tiled=True)
-    grad_weight = jnp.einsum(
-        "th,td->hd", all_attended, cotangent_cols, preferred_element_type=jnp.float32
-    )
     grad_heads = split_heads(grad_attended)
     row_delta = jnp.sum(
         grad_heads.astype(jnp.float32) * attended_heads.astype(jnp.float32), axis=2
@@ -118,12 +115,17 @@
         )
         both_parts = jnp.concatenate([key_part, value_part], axis=1).astype(jnp.bfloat16)
         if half == 0:
-            attn_output, both_parts = lax.optimization_barrier((attn_output, both_parts))
+            attn_output, all_attended, both_parts = lax.optimization_barrier(
+                (attn_output, all_attended, both_parts)
+            )
         both_sums = lax.psum_scatter(both_parts, "seq", scatter_dimension=0, tiled=True).astype(
             jnp.float32
         )
         key_sums.append(both_sums[:, :span])
         value_sums.append(both_sums[:, span:])
+    grad_weight = jnp.einsum(
+        "th,td->hd", all_attended, cotangent_cols, preferred_element_type=jnp.float32
+    )
     query_sum = jnp.concatenate(query_sums, axis=1)
     key_sum = jnp.concatenate(key_sums, axis=1)
     value_sum = jnp.concatenate(value_sums, axis=1)

time: 375 us -> 339 us (0.904)
  waiting for transfers between devices: 179 us -> 138 us
  blocking collectives: 44.5 us -> 50.1 us
    all_gather x1, waiting for transfers between devices: 34.5 us -> 0.01 us  [shards(): all_attended = lax.all_gather(attended_flat, 'seq', axis=0, tiled=True)]
    reduce_scatter x2, waiting for transfers between devices: 22.9 us -> 16.3 us  [shards(): lax.psum_scatter(both_parts, 'seq', scatter_dimension=0, tiled=True)]
    all_to_all x1, blocking collectives: 35.4 us -> 41 us  [shards(): cotangent_cols = lax.all_to_all(cotangent_full, 'seq', 1, 0, tiled=True)]
    unnamed x36 -> x34, local copies, waits for them, and re-layouts: 12.4 us -> 10.9 us
  transfers between devices with their start and end apart: 12 -> 12, of which waited for: 8 -> 7; matrix products, arithmetic and copies ran while one was open for 22% -> 29% of each run, Pallas kernels for 0% -> 0%
where the time goes in v6:
time: 339 us; the launch traced here: 338 us
  waiting for transfers between devices  138 us (41%)
  matrix products  67.5 us (20%)
  blocking collectives  50.1 us (15%)
  local copies, waits for them, and re-layouts  32.9 us (10%)
  other arithmetic  22.2 us (7%)
  between operations  14.6 us (4%)
  starting transfers between devices  12.8 us (4%)
    all_gather x1, waiting for transfers between devices, shards(): weight_full = lax.all_gather(out_weight, 'seq', axis=1, tiled=True)  45.5 us
    all_to_all x1, blocking collectives, shards(): cotangent_cols = lax.all_to_all(cotangent_full, 'seq', 1, 0, tiled=True)  41 us
    ppermute x3, waiting for transfers between devices, shift_pieces(): pieces.append(lax.ppermute(block, axis, route))  28.3 us
    ppermute x3, waiting for transfers between devices, permute_sum_scatter(): total = total + lax.ppermute(piece, axis, route).astype(jnp.float32)  27.6 us
    all_gather x1, waiting for transfers between devices, shards(): all_keys = lax.all_gather(key_states, 'seq', axis=0, tiled=True)  18.5 us
    reduce_scatter x2, waiting for transfers between devices, shards(): lax.psum_scatter(both_parts, 'seq', scatter_dimension=0, tiled=True)  16.3 us
    unnamed x34, local copies, waits for them, and re-layouts  10.9 us
    convert_element_type x1, other arithmetic, shards(): weights = probs.astype(jnp.bfloat16)  9.44 us
  transfers between devices with their start and end apart: 12, of which 7 were waited for; matrix products, arithmetic and copies ran while one was open for 29% of the time, Pallas kernels for 0%

profile of v6, /device:TPU:0, one launch (start us, length us, event | category | flops | bytes accessed | tf_op | source)
XLA Modules:
  0.0 337.7 jit_solution(13538706371866200887)
XLA Ops:
  13.0 3.1 collective-permute-start.3
  20.0 9.1 %all-gather = s32[8,1,256]{2,1,0:T(1,128)S(1)} all-gather(s32[1,1,256]{2,1,0:T(1,128)S(1)} %bitcast.73), channel_id=1, replica_groups=mesh['seq'=8,'fsdp'=4] {'seq'}, dimensions={0}, use_global_device_ids=true | all-gather | bytes 9216 | tf_op jit(solution)/shard_map/all_gather | solution.py:65
  35.3 26.0 %collective-permute-done.4 = bf16[256,1280]{0,1:T(8,128)(2,1)} collective-permute-done((bf16[256,1280]{0,1:T(8,128)(2,1)}, bf16[256,1280]{0,1:T(8,128)(2,1)}, u32[]{:S(2)}, u32[]{:S(2)}) %collective-permute-start.4) | collective-permute-done | bytes 655392 | tf_op jit(solution)/shard_map/ppermute | solution.py:29
  63.7 6.9 %copy.82 = bf16[2048,1024]{0,1:T(8,128)(2,1)} copy(bf16[2048,1024]{1,0:T(8,128)(2,1)} %all-gather.8.cloned.1.call-done) | data formatting | bytes 8388608 | tf_op jit(solution)/shard_map/all_gather | solution.py:64
  70.5 18.5 %all-gather.6.cloned.1.call-done = bf16[2048,1024]{0,1:T(8,128)(2,1)} async-done(((bf16[256,1024]{0,1:T(8,128)(2,1)}), bf16[2048,1024]{0,1:T(8,128)(2,1)}) %all-gather.6.cloned.1.call-update) | async-done | bytes 4194320 | tf_op jit(solution)/shard_map/all_gather | solution.py:63
  89.0 5.4 %fusion = (f32[8,256]{1,0:T(8,128)S(1)}, f32[8,256,2048]{2,1,0:T(8,128)S(1)}) fusion(pred[256,2048]{1,0:T(8,128)(4,1)S(1)} %broadcast_compare_fusion, bf16[256,8,128]{0,2,1:T(8,128)(2,1)} %bitcast.55, bf16[2048,8,128]{0,2,1:T(8,128)(2,1)} %bitcast.50), kind=kOutput, calls=%fused_computation.3 | convolution fusion | flops 1086322688 | bytes 22028288 | tf_op jit(solution)/shard_map/qhd,khd->hqk/dot_general | solution.py:17
  94.5 4.5 %exponential_reduce_fusion = f32[8,256]{1,0:T(8,128)S(1)} fusion(f32[8,256,2048]{2,1,0:T(8,128)S(1)} %get-tuple-element.38, f32[8,256]{1,0:T(8,128)S(1)} %get-tuple-element.37, pred[256,2048]{1,0:T(8,128)(4,1)S(1)} %broadcast_compare_fusion), kind=kLoop, calls=%fused_computation.1 | loop fusion | flops 16775168 | bytes 17317888 | tf_op jit(solution)/shard_map/reduce_sum | solution.py:70
  99.0 9.4 %fusion.35 = (bf16[8,256,2048]{2,1,0:T(8,128)(2,1)}, f32[8,256,2048]{2,1,0:T(8,128)}) fusion(f32[8,256]{1,0:T(8,128)S(1)} %log_add_fusion, f32[8,256,2048]{2,1,0:T(8,128)S(1)} %get-tuple-element.38, pred[256,2048]{1,0:T(8,128)(4,1)S(1)} %broadcast_compare_fusion), kind=kLoop, calls=%fused_computation.49 | loop fusion | flops 16777216 | bytes 42475520 | tf_op jit(solution)/shard_map/convert_element_type | solution.py:72
  108.5 45.5 %all-gather.10.cloned.1.call-done = bf16[1024,5120]{1,0:T(8,128)(2,1)} async-done(((bf16[1024,640]{1,0:T(8,128)(2,1)}), bf16[1024,5120]{1,0:T(8,128)(2,1)}) %all-gather.10.cloned.1.call-update) | async-done | bytes 10485776 | tf_op jit(solution)/shard_map/all_gather | solution.py:78
  154.0 7.7 %convolution_convert_fusion.3 = bf16[256,1024]{1,0:T(8,128)(2,1)} fusion(bf16[256,5120]{0,1:T(8,128)(2,1)S(1)} %constant_dynamic-update-slice_fusion, bf16[1024,5120]{1,0:T(8,128)(2,1)} %all-gather.10.cloned.1.call-done), kind=kOutput, calls=%fused_computation.30 | convolution fusion | flops 2684616704 | bytes 13631488 | tf_op jit(solution)/shard_map/td,hd->th/dot_general | solution.py:84
  162.9 8.5 %multiply_reduce_fusion = (f32[256,8]{0,1:T(8,128)S(1)}, bf16[8,256,128]{1,2,0:T(8,128)(2,1)}) fusion(bf16[256,1024]{0,1:T(8,128)(2,1)S(1)} %copy.87, bf16[8,256,2048]{2,1,0:T(8,128)(2,1)} %get-tuple-element.26, bf16[2048,8,128]{0,2,1:T(8,128)(2,1)} %bitcast.58), kind=kOutput, calls=%fused_computation.37 | convolution fusion | flops 1075050496 | bytes 13639680 | tf_op jit(solution)/shard_map/hqk,khd->qhd/dot_general | solution.py:73
  171.7 5.1 %fusion.1 = bf16[4,256,2048]{2,1,0:T(8,128)(2,1)S(1)} fusion(f32[8,256,2048]{2,1,0:T(8,128)} %get-tuple-element.27, f32[4,256]{1,0:T(4,128)S(1)} %get-tuple-element.35, bf16[256,8,128]{0,2,1:T(8,128)(2,1)S(1)} %bitcast.67, bf16[2048,8,128]{0,2,1:T(8,128)(2,1)} %bitcast.59), kind=kOutput, calls=%fused_computation.5 | convolution fusion | flops 543162368 | bytes 15208448 | tf_op jit(solution)/shard_map/qhd,khd->hqk/dot_general | solution.py:99
  178.5 4.0 %fusion.15 = bf16[2048,4,128]{2,0,1:T(8,128)(2,1)S(1)} fusion(bf16[256,8,128]{0,2,1:T(8,128)(2,1)S(1)} %bitcast.68, bf16[8,256,2048]{2,1,0:T(8,128)(2,1)} %get-tuple-element.26), kind=kOutput, calls=%fused_computation.21 | convolution fusion | flops 537919488 | bytes 6815744 | tf_op jit(solution)/shard_map/hqk,qhd->khd/dot_general | solution.py:113
  185.2 7.2 %convolution_convert_fusion = bf16[256,5120]{1,0:T(8,128)(2,1)S(1)} fusion(bf16[256,1024]{0,1:T(8,128)(2,1)} %bitcast.65, bf16[1024,5120]{1,0:T(8,128)(2,1)} %all-gather.10.cloned.1.call-done), kind=kOutput, calls=%fused_computation.8 | convolution fusion | flops 2685665280 | bytes 13631488 | tf_op jit(solution)/shard_map/dot_general | solution.py:79
  199.1 4.5 %fusion.18 = bf16[2048,4,128]{2,0,1:T(8,128)(2,1)S(1)} fusion(bf16[256,8,128]{0,2,1:T(8,128)(2,1)S(1)} %bitcast.69, bf16[8,256,2048]{2,1,0:T(8,128)(2,1)} %get-tuple-element.26), kind=kOutput, calls=%fused_computation.22 | convolution fusion | flops 537919488 | bytes 6815744 | tf_op jit(solution)/shard_map/hqk,qhd->khd/dot_general | solution.py:113
  203.7 3.4 fusion.2
  207.1 3.9 %fusion.13 = bf16[2048,4,128]{2,0,1:T(8,128)(2,1)S(1)} fusion(bf16[4,256,2048]{2,1,0:T(8,128)(2,1)} %fusion.2, bf16[256,8,128]{0,2,1:T(8,128)(2,1)S(1)} %bitcast.57), kind=kOutput, calls=%fused_computation.19 | convolution fusion | flops 537919488 | bytes 6553600 | tf_op jit(solution)/shard_map/hqk,qhd->khd/dot_general | solution.py:110
  213.6 27.4 %collective-permute-done.1 = bf16[256,1280]{1,0:T(8,128)(2,1)} collective-permute-done((bf16[256,1280]{1,0:T(8,128)(2,1)}, bf16[256,1280]{1,0:T(8,128)(2,1)}, u32[]{:S(2)}, u32[]{:S(2)}) %collective-permute-start.1) | collective-permute-done | bytes 655392 | tf_op jit(solution)/shard_map/ppermute | solution.py:55
  245.6 41.0 %all_to_all.19 = bf16[256,8,640]{0,2,1:T(8,128)(2,1)} all-to-all(bf16[256,8,640]{0,2,1:T(8,128)(2,1)S(1)} %bitcast.53), channel_id=1, replica_groups=mesh['seq'=8,'fsdp'=4] {'seq'}, dimensions={1} | all-to-all | bytes 5242880 | tf_op jit(solution)/shard_map/all_to_all | solution.py:88
  286.5 4.6 %copy.103 = bf16[8,256,640]{2,1,0:T(8,128)(2,1)} copy(bf16[8,256,640]{1,2,0:T(8,128)(2,1)} %bitcast.54) | data formatting | bytes 5242880 | tf_op jit(solution)/shard_map/all_to_all | solution.py:88
  291.1 4.2 %fusion.30 = f32[256,4,128]{2,0,1:T(8,128)S(1)} fusion(bf16[4,256,2048]{2,1,0:T(8,128)(2,1)} %copy-done.5, bf16[2048,8,128]{0,2,1:T(8,128)(2,1)} %bitcast.51), kind=kOutput, calls=%fused_computation.33 | convolution fusion | flops 536870912 | bytes 6815744 | tf_op jit(solution)/shard_map/hqk,khd->qhd/dot_general | solution.py:106
  295.4 3.7 %fusion.27 = f32[256,4,128]{2,0,1:T(8,128)S(1)} fusion(bf16[4,256,2048]{2,1,0:T(8,128)(2,1)} %fusion.2, bf16[2048,8,128]{0,2,1:T(8,128)(2,1)S(1)} %bitcast.52), kind=kOutput, calls=%fused_computation.32 | convolution fusion | flops 536870912 | bytes 6815744 | tf_op jit(solution)/shard_map/hqk,khd->qhd/dot_general | solution.py:106
  301.9 8.0 %fusion.39 = f32[1024,640]{1,0:T(8,128)} fusion(bf16[2048,1024]{0,1:T(8,128)(2,1)} %all-gather.12.cloned.1.call-done, bf16[2048,640]{1,0:T(8,128)(2,1)} %bitcast.66), kind=kOutput, calls=%fused_computation.53 | convolution fusion | flops 2684354560 | bytes 9437184 | tf_op jit(solution)/shard_map/th,td->hd/dot_general | solution.py:126
  309.9 16.3 %reduce-scatter.3.cloned.1.call-done = bf16[256,8,128]{2,0,1:T(8,128)(2,1)} async-done(((bf16[2048,8,128]{2,0,1:T(8,128)(2,1)}), bf16[256,8,128]{2,0,1:T(8,128)(2,1)}) %reduce-scatter.3.cloned.1.call-update) | async-done | bytes 524304 | tf_op jit(solution)/shard_map/reduce_scatter | solution.py:121
  (80 shorter events, 45.0 us)
Async XLA Ops:
  7.2 12.8 %copy-start.9 = (s32[256]{0:T(256)S(1)}, s32[256]{0:T(256)}, u32[]{:S(2)}) copy-start(s32[256]{0:T(256)} %param.9) | copy-start | bytes 3076
  7.2 22.4 %copy-start.6 = (bf16[256,1024]{1,0:T(8,128)(2,1)S(1)}, bf16[256,1024]{1,0:T(8,128)(2,1)}, u32[]{:S(2)}) copy-start(bf16[256,1024]{1,0:T(8,128)(2,1)} %param.6) | copy-start | bytes 1572868
  7.2 56.5 %all-gather.8.cloned.1.call-start = ((), (), s32[]{:S(2)}) async-start(), calls=%async_computation.4 | async-start | bytes 4718592 | tf_op jit(solution)/shard_map/all_gather | solution.py:64
  7.9 81.1 %all-gather.6.cloned.1.call-start = ((), (), s32[]{:S(2)}) async-start(), calls=%async_computation.3 | async-start | bytes 4718592 | tf_op jit(solution)/shard_map/all_gather | solution.py:63
  10.0 143.9 %all-gather.10.cloned.1.call-start = ((), (), s32[]{:S(2)}) async-start(), calls=%async_computation.5 | async-start | bytes 11796480 | tf_op jit(solution)/shard_map/all_gather | solution.py:78
  10.8 233.0 %all-gather.12.cloned.1.call-start = ((), (), s32[]{:S(2)}) async-start(), calls=%async_computation.6 | async-start | bytes 4718592 | tf_op jit(solution)/shard_map/all_gather | solution.py:87
  13.0 21.1 %collective-permute-start.3 = (bf16[256,1280]{0,1:T(8,128)(2,1)}, bf16[256,1280]{0,1:T(8,128)(2,1)}, u32[]{:S(2)}, u32[]{:S(2)}) collective-permute-start(bf16[256,1280]{0,1:T(8,128)(2,1)} %copy.83), channel_id=1, source_target_pairs={{0,1},{1,2},{2,3},{3,0},{4,5},{5,6},{6,7},{7,4},{8,9},{9,10},{10,1... | collective-permute-start | bytes 1966088 | tf_op jit(solution)/shard_map/ppermute | solution.py:29
  16.0 45.3 %collective-permute-start.4 = (bf16[256,1280]{0,1:T(8,128)(2,1)}, bf16[256,1280]{0,1:T(8,128)(2,1)}, u32[]{:S(2)}, u32[]{:S(2)}) collective-permute-start(bf16[256,1280]{0,1:T(8,128)(2,1)} %copy.83), channel_id=1, source_target_pairs={{0,2},{1,3},{2,0},{3,1},{4,6},{5,7},{6,4},{7,5},{8,10},{9,11},{10,... | collective-permute-start | bytes 1966088 | tf_op jit(solution)/shard_map/ppermute | solution.py:29
  18.6 43.8 %collective-permute-start.5 = (bf16[256,1280]{0,1:T(8,128)(2,1)}, bf16[256,1280]{0,1:T(8,128)(2,1)}, u32[]{:S(2)}, u32[]{:S(2)}) collective-permute-start(bf16[256,1280]{0,1:T(8,128)(2,1)} %copy.83), channel_id=1, source_target_pairs={{0,3},{1,0},{2,1},{3,2},{4,7},{5,4},{6,5},{7,6},{8,11},{9,8},{10,9... | collective-permute-start | bytes 1966088 | tf_op jit(solution)/shard_map/ppermute | solution.py:29
  63.6 90.4 %copy-start.1 = (bf16[256,5120]{0,1:T(8,128)(2,1)}, bf16[256,5120]{0,1:T(8,128)(2,1)S(1)}, u32[]{:S(2)}) copy-start(bf16[256,5120]{0,1:T(8,128)(2,1)S(1)} %constant_dynamic-update-slice_fusion) | copy-start | bytes 7864324
  162.9 15.6 %copy-start.7 = (bf16[256,1024]{0,1:T(8,128)(2,1)}, bf16[256,1024]{0,1:T(8,128)(2,1)S(1)}, u32[]{:S(2)}) copy-start(bf16[256,1024]{0,1:T(8,128)(2,1)S(1)} %copy.87) | copy-start | bytes 1572868
  171.4 129.4 %reduce-scatter.5.cloned.1.call-start = ((), (), s32[]{:S(2)}) async-start(), calls=%async_computation.8 | async-start | bytes 4718592 | tf_op jit(solution)/shard_map/reduce_scatter | solution.py:121
  171.7 5.2 %copy-start.3 = (bf16[256,1024]{0,1:T(8,128)(2,1)S(1)}, bf16[256,1024]{0,1:T(8,128)(2,1)}, u32[]{:S(2)}) copy-start(bf16[256,1024]{0,1:T(8,128)(2,1)} %copy.78) | copy-start | bytes 1572868
  176.8 5.7 %copy-start.5 = (bf16[4,256,2048]{2,1,0:T(8,128)(2,1)}, bf16[4,256,2048]{2,1,0:T(8,128)(2,1)S(1)}, u32[]{:S(2)}) copy-start(bf16[4,256,2048]{2,1,0:T(8,128)(2,1)S(1)} %fusion.1) | copy-start | bytes 12582916
  185.0 141.2 %reduce-scatter.3.cloned.1.call-start = ((), (), s32[]{:S(2)}) async-start(), calls=%async_computation.7 | async-start | bytes 4718592 | tf_op jit(solution)/shard_map/reduce_scatter | solution.py:121
  185.1 14.0 %copy-start.8 = (bf16[256,1024]{0,1:T(8,128)(2,1)S(1)}, bf16[256,1024]{0,1:T(8,128)(2,1)}, u32[]{:S(2)}) copy-start(bf16[256,1024]{0,1:T(8,128)(2,1)} %copy-done.7) | copy-start | bytes 1572868
  185.2 18.5 %slice-start = ((s8[16777216]{0:T(1024)(128)(4,1)}), s8[4194304]{0:T(1024)(128)(4,1)S(1)}, s32[]{:S(2)}) async-start(s8[16777216]{0:T(1024)(128)(4,1)} %bitcast.48), calls=%async_computation.9 | async-start | bytes 8388608
  185.2 18.5 %slice-start.1 = ((s8[16777216]{0:T(1024)(128)(4,1)}), s8[4194304]{0:T(1024)(128)(4,1)S(1)}, s32[]{:S(2)}) async-start(s8[16777216]{0:T(1024)(128)(4,1)} %bitcast.48), calls=%async_computation.10 | async-start | bytes 8388608
  192.4 11.3 %slice-start.2 = ((s8[16777216]{0:T(1024)(128)(4,1)}), s8[4194304]{0:T(1024)(128)(4,1)S(1)}, s32[]{:S(2)}) async-start(s8[16777216]{0:T(1024)(128)(4,1)} %bitcast.48), calls=%async_computation.11 | async-start | bytes 8388608
  193.7 19.9 %collective-permute-start = (bf16[256,1280]{1,0:T(8,128)(2,1)}, bf16[256,1280]{1,0:T(8,128)(2,1)}, u32[]{:S(2)}, u32[]{:S(2)}) collective-permute-start(bf16[256,1280]{1,0:T(8,128)(2,1)} %get-tuple-element.28), channel_id=1, source_target_pairs={{0,1},{1,2},{2,3},{3,0},{4,5},{5,6},{6,7},{7,4},{8,9},{9,10},{10,1... | collective-permute-start | bytes 1966088 | tf_op jit(solution)/shard_map/ppermute | solution.py:55
  195.3 45.7 %collective-permute-start.1 = (bf16[256,1280]{1,0:T(8,128)(2,1)}, bf16[256,1280]{1,0:T(8,128)(2,1)}, u32[]{:S(2)}, u32[]{:S(2)}) collective-permute-start(bf16[256,1280]{1,0:T(8,128)(2,1)} %get-tuple-element.30), channel_id=1, source_target_pairs={{0,2},{1,3},{2,0},{3,1},{4,6},{5,7},{6,4},{7,5},{8,10},{9,11},{10,... | collective-permute-start | bytes 1966088 | tf_op jit(solution)/shard_map/ppermute | solution.py:55
  197.7 6.0 %slice-start.3 = ((s8[16777216]{0:T(1024)(128)(4,1)}), s8[4194304]{0:T(1024)(128)(4,1)S(1)}, s32[]{:S(2)}) async-start(s8[16777216]{0:T(1024)(128)(4,1)} %bitcast.48), calls=%async_computation.12 | async-start | bytes 8388608
  197.7 6.0 %copy-start.4 = (bf16[2048,1024]{0,1:T(8,128)(2,1)S(1)}, bf16[2048,1024]{0,1:T(8,128)(2,1)}, u32[]{:S(2)}) copy-start(bf16[2048,1024]{0,1:T(8,128)(2,1)} %copy.82) | copy-start | bytes 12582916
  197.7 43.3 %collective-permute-start.2 = (bf16[256,1280]{1,0:T(8,128)(2,1)}, bf16[256,1280]{1,0:T(8,128)(2,1)}, u32[]{:S(2)}, u32[]{:S(2)}) collective-permute-start(bf16[256,1280]{1,0:T(8,128)(2,1)} %get-tuple-element.29), channel_id=1, source_target_pairs={{0,3},{1,0},{2,1},{3,2},{4,7},{5,4},{6,5},{7,6},{8,11},{9,8},{10,9... | collective-permute-start | bytes 1966088 | tf_op jit(solution)/shard_map/ppermute | solution.py:55
  (2 other events, 6.0 us)
Sparse Core Ops, SparseCore 0:
  9.9 39.2 all-gather.7
  51.7 37.3 all-gather.5
  91.0 62.9 all-gather.9
  171.6 37.3 all-gather.11
  212.1 62.4 reduce-scatter.4
  277.8 48.3 reduce-scatter.2

commit v7 on v6

--- a/solution.py
+++ b/solution.py
@@ -63,6 +63,9 @@
     all_keys = lax.all_gather(key_states, "seq", axis=0, tiled=True)
     all_values = lax.all_gather(value_states, "seq", axis=0, tiled=True)
     all_pos = lax.all_gather(positions, "seq", axis=0, tiled=True)
+    cotangent_full = permute_gather(cotangent, "fsdp", 1)
+    cotangent_cols = lax.all_to_all(cotangent_full, "seq", 1, 0, tiled=True)
+    cotangent_cols, all_values = lax.optimization_barrier((cotangent_cols, all_values))
     key_heads = split_heads(all_keys)
     value_heads = split_heads(all_values)
     scores = masked_scores(query_heads, key_heads, positions, all_pos)
@@ -80,12 +83,10 @@
         jnp.bfloat16
     )
     attn_output = permute_sum_scatter(partial_sum, "fsdp", 1)
-    cotangent_full = permute_gather(cotangent, "fsdp", 1)
     grad_attended = jnp.einsum(
         "td,hd->th", cotangent_full, weight_full, preferred_element_type=jnp.float32
     ).astype(jnp.bfloat16)
     all_attended = lax.all_gather(attended_flat, "seq", axis=0, tiled=True)
-    cotangent_cols = lax.all_to_all(cotangent_full, "seq", 1, 0, tiled=True)
     grad_heads = split_heads(grad_attended)
     row_delta = jnp.sum(
         grad_heads.astype(jnp.float32) * attended_heads.astype(jnp.float32), axis=2

time: 339 us -> 349 us (1.029)
  waiting for transfers between devices: 138 us -> 159 us
  local copies, waits for them, and re-layouts: 32.9 us -> 23.9 us
  blocking collectives: 50.1 us -> 44.4 us
  starting transfers between devices: 12.8 us -> 16.6 us
    all_to_all x1 -> x0, blocking collectives: 41 us -> none  [shards(): cotangent_cols = lax.all_to_all(cotangent_full, 'seq', 1, 0, tiled=True)]
    reduce_scatter x2, waiting for transfers between devices: 16.3 us -> 55.3 us  [shards(): lax.psum_scatter(both_parts, 'seq', scatter_dimension=0, tiled=True)]
    all_gather x1, blocking collectives: 9.12 us -> 44.4 us  [shards(): all_pos = lax.all_gather(positions, 'seq', axis=0, tiled=True)]
    all_gather x1, waiting for transfers between devices: 18.5 us -> 0.01 us  [shards(): all_keys = lax.all_gather(key_states, 'seq', axis=0, tiled=True)]
    ppermute x3, waiting for transfers between devices: 28.3 us -> 39.8 us  [shift_pieces(): pieces.append(lax.ppermute(block, axis, route))]
    all_gather x1, waiting for transfers between devices: 45.5 us -> 35.4 us  [shards(): weight_full = lax.all_gather(out_weight, 'seq', axis=1, tiled=True)]
    all_gather x1 -> x0, local copies, waits for them, and re-layouts: 6.88 us -> none  [shards(): all_values = lax.all_gather(value_states, 'seq', axis=0, tiled=True)]
    all_to_all x0 -> x1, starting transfers between devices: none -> 3.73 us  [shards(): cotangent_cols = lax.all_to_all(cotangent_full, 'seq', 1, 0, tiled=True)]
  transfers between devices with their start and end apart: 12 -> 13, of which waited for: 7 -> 7; matrix products, arithmetic and copies ran while one was open for 29% -> 25% of each run, Pallas kernels for 0% -> 0%
where the time goes in v7:
time: 349 us; the launch traced here: 348 us
  waiting for transfers between devices  159 us (46%)
  matrix products  67.5 us (19%)
  blocking collectives  44.4 us (13%)
  local copies, waits for them, and re-layouts  23.9 us (7%)
  other arithmetic  22.2 us (6%)
  starting transfers between devices  16.6 us (5%)
  between operations  14.5 us (4%)
    reduce_scatter x2, waiting for transfers between devices, shards(): lax.psum_scatter(both_parts, 'seq', scatter_dimension=0, tiled=True)  55.3 us
    all_gather x1, blocking collectives, shards(): all_pos = lax.all_gather(positions, 'seq', axis=0, tiled=True)  44.4 us
    ppermute x3, waiting for transfers between devices, shift_pieces(): pieces.append(lax.ppermute(block, axis, route))  39.8 us
    all_gather x1, waiting for transfers between devices, shards(): weight_full = lax.all_gather(out_weight, 'seq', axis=1, tiled=True)  35.4 us
    ppermute x3, waiting for transfers between devices, permute_sum_scatter(): total = total + lax.ppermute(piece, axis, route).astype(jnp.float32)  27.5 us
    unnamed x35, local copies, waits for them, and re-layouts  11.9 us
    convert_element_type x1, other arithmetic, shards(): weights = probs.astype(jnp.bfloat16)  9.45 us
    dot_general x1, matrix products, shards(): jnp.einsum('hqk,khd->qhd', weights, value_heads, preferred_element_type=j...  8.55 us
  transfers between devices with their start and end apart: 13, of which 7 were waited for; matrix products, arithmetic and copies ran while one was open for 25% of the time, Pallas kernels for 0%

profile of v7, /device:TPU:0, one launch (start us, length us, event | category | flops | bytes accessed | tf_op | source)
XLA Modules:
  0.0 347.9 jit_solution(15244120665177871162)
XLA Ops:
  12.4 3.1 collective-permute-start
  19.7 13.7 %collective-permute-done = bf16[256,1280]{0,1:T(8,128)(2,1)} collective-permute-done((bf16[256,1280]{0,1:T(8,128)(2,1)S(1)}, bf16[256,1280]{0,1:T(8,128)(2,1)}, u32[]{:S(2)}, u32[]{:S(2)}) %collective-permute-start) | collective-permute-done | bytes 655392 | tf_op jit(solution)/shard_map/ppermute | solution.py:29
  34.6 26.1 %collective-permute-done.1 = bf16[256,1280]{0,1:T(8,128)(2,1)} collective-permute-done((bf16[256,1280]{0,1:T(8,128)(2,1)S(1)}, bf16[256,1280]{0,1:T(8,128)(2,1)}, u32[]{:S(2)}, u32[]{:S(2)}) %collective-permute-start.1) | collective-permute-done | bytes 655392 | tf_op jit(solution)/shard_map/ppermute | solution.py:29
  64.5 3.7 %all-to-all-start = ((bf16[256,8,640]{0,2,1:T(8,128)(2,1)}), bf16[256,8,640]{0,2,1:T(8,128)(2,1)S(1)}, u32[]{:S(2)}, u32[]{:S(2)}) async-start(bf16[256,8,640]{0,2,1:T(8,128)(2,1)} %bitcast.54), calls=%async_computation | async-start | bytes 5242880 | tf_op jit(solution)/shard_map/all_to_all | solution.py:67
  70.3 44.4 %all-gather = s32[8,1,256]{2,1,0:T(1,128)S(1)} all-gather(s32[1,1,256]{2,1,0:T(1,128)S(1)} %bitcast.73), channel_id=1, replica_groups=mesh['seq'=8,'fsdp'=4] {'seq'}, dimensions={0}, use_global_device_ids=true | all-gather | bytes 9216 | tf_op jit(solution)/shard_map/all_gather | solution.py:65
  117.7 5.6 %fusion = (f32[8,256]{1,0:T(8,128)S(1)}, f32[8,256,2048]{2,1,0:T(8,128)S(1)}) fusion(pred[256,2048]{1,0:T(8,128)(4,1)S(1)} %broadcast_compare_fusion, bf16[256,8,128]{0,2,1:T(8,128)(2,1)} %bitcast.55, bf16[2048,8,128]{0,2,1:T(8,128)(2,1)} %bitcast.50), kind=kOutput, calls=%fused_computation.3 | convolution fusion | flops 1086322688 | bytes 22028288 | tf_op jit(solution)/shard_map/qhd,khd->hqk/dot_general | solution.py:17
  123.3 4.5 %exponential_reduce_fusion = f32[8,256]{1,0:T(8,128)S(1)} fusion(f32[8,256,2048]{2,1,0:T(8,128)S(1)} %get-tuple-element.42, f32[8,256]{1,0:T(8,128)S(1)} %get-tuple-element.41, pred[256,2048]{1,0:T(8,128)(4,1)S(1)} %broadcast_compare_fusion), kind=kLoop, calls=%fused_computation.1 | loop fusion | flops 16775168 | bytes 17317888 | tf_op jit(solution)/shard_map/reduce_sum | solution.py:73
  127.8 9.4 %fusion.35 = (bf16[8,256,2048]{2,1,0:T(8,128)(2,1)}, f32[8,256,2048]{2,1,0:T(8,128)}) fusion(f32[8,256]{1,0:T(8,128)S(1)} %log_add_fusion, f32[8,256,2048]{2,1,0:T(8,128)S(1)} %get-tuple-element.42, pred[256,2048]{1,0:T(8,128)(4,1)S(1)} %broadcast_compare_fusion), kind=kLoop, calls=%fused_computation.49 | loop fusion | flops 16777216 | bytes 42475520 | tf_op jit(solution)/shard_map/convert_element_type | solution.py:75
  137.3 35.4 %all-gather.10.cloned.1.call-done = bf16[1024,5120]{1,0:T(8,128)(2,1)} async-done(((bf16[1024,640]{1,0:T(8,128)(2,1)}), bf16[1024,5120]{1,0:T(8,128)(2,1)}) %all-gather.10.cloned.1.call-update) | async-done | bytes 10485776 | tf_op jit(solution)/shard_map/all_gather | solution.py:81
  172.7 7.7 %convolution_convert_fusion.3 = bf16[256,1024]{1,0:T(8,128)(2,1)} fusion(bf16[256,5120]{0,1:T(8,128)(2,1)S(1)} %copy-done.2, bf16[1024,5120]{1,0:T(8,128)(2,1)} %all-gather.10.cloned.1.call-done), kind=kOutput, calls=%fused_computation.30 | convolution fusion | flops 2684616704 | bytes 13631488 | tf_op jit(solution)/shard_map/td,hd->th/dot_general | solution.py:86
  181.7 8.6 %multiply_reduce_fusion = (f32[256,8]{0,1:T(8,128)S(1)}, bf16[8,128,256]{2,1,0:T(8,128)(2,1)}) fusion(bf16[256,1024]{0,1:T(8,128)(2,1)S(1)} %copy.86, bf16[2048,8,128]{0,2,1:T(8,128)(2,1)} %bitcast.60, bf16[8,256,2048]{2,1,0:T(8,128)(2,1)} %get-tuple-element.30), kind=kOutput, calls=%fused_computation.37 | convolution fusion | flops 1075050496 | bytes 13639680 | tf_op jit(solution)/shard_map/hqk,khd->qhd/dot_general | solution.py:76
  190.5 5.1 %fusion.1 = bf16[4,256,2048]{2,1,0:T(8,128)(2,1)S(1)} fusion(f32[8,256,2048]{2,1,0:T(8,128)} %get-tuple-element.31, f32[4,256]{1,0:T(4,128)S(1)} %get-tuple-element.39, bf16[256,8,128]{0,2,1:T(8,128)(2,1)S(1)} %bitcast.67, bf16[2048,8,128]{0,2,1:T(8,128)(2,1)} %bitcast.61), kind=kOutput, calls=%fused_computation.5 | convolution fusion | flops 543162368 | bytes 15208448 | tf_op jit(solution)/shard_map/qhd,khd->hqk/dot_general | solution.py:100
  197.3 4.0 %fusion.15 = bf16[2048,4,128]{2,0,1:T(8,128)(2,1)S(1)} fusion(bf16[256,8,128]{0,2,1:T(8,128)(2,1)S(1)} %bitcast.68, bf16[8,256,2048]{2,1,0:T(8,128)(2,1)} %get-tuple-element.30), kind=kOutput, calls=%fused_computation.21 | convolution fusion | flops 537919488 | bytes 6815744 | tf_op jit(solution)/shard_map/hqk,qhd->khd/dot_general | solution.py:114
  203.8 7.2 %convolution_convert_fusion = bf16[256,5120]{1,0:T(8,128)(2,1)S(1)} fusion(bf16[256,1024]{0,1:T(8,128)(2,1)} %bitcast.59, bf16[1024,5120]{1,0:T(8,128)(2,1)} %all-gather.10.cloned.1.call-done), kind=kOutput, calls=%fused_computation.8 | convolution fusion | flops 2685665280 | bytes 13631488 | tf_op jit(solution)/shard_map/dot_general | solution.py:82
  217.8 4.5 %fusion.18 = bf16[2048,4,128]{2,0,1:T(8,128)(2,1)S(1)} fusion(bf16[256,8,128]{0,2,1:T(8,128)(2,1)S(1)} %bitcast.69, bf16[8,256,2048]{2,1,0:T(8,128)(2,1)} %get-tuple-element.30), kind=kOutput, calls=%fused_computation.22 | convolution fusion | flops 537919488 | bytes 6815744 | tf_op jit(solution)/shard_map/hqk,qhd->khd/dot_general | solution.py:114
  222.4 3.4 fusion.2
  225.7 4.0 %fusion.13 = bf16[2048,4,128]{2,0,1:T(8,128)(2,1)S(1)} fusion(bf16[4,256,2048]{2,1,0:T(8,128)(2,1)} %fusion.2, bf16[256,8,128]{0,2,1:T(8,128)(2,1)S(1)} %bitcast.57), kind=kOutput, calls=%fused_computation.19 | convolution fusion | flops 537919488 | bytes 6553600 | tf_op jit(solution)/shard_map/hqk,qhd->khd/dot_general | solution.py:111
  232.3 27.4 %collective-permute-done.4 = bf16[256,1280]{1,0:T(8,128)(2,1)} collective-permute-done((bf16[256,1280]{1,0:T(8,128)(2,1)}, bf16[256,1280]{1,0:T(8,128)(2,1)}, u32[]{:S(2)}, u32[]{:S(2)}) %collective-permute-start.4) | collective-permute-done | bytes 655392 | tf_op jit(solution)/shard_map/ppermute | solution.py:55
  259.6 2.8 convert_add_fusion
  262.5 4.3 %fusion.30 = f32[256,4,128]{2,0,1:T(8,128)S(1)} fusion(bf16[4,256,2048]{2,1,0:T(8,128)(2,1)} %copy-done.5, bf16[2048,8,128]{0,2,1:T(8,128)(2,1)} %bitcast.51), kind=kOutput, calls=%fused_computation.33 | convolution fusion | flops 536870912 | bytes 6815744 | tf_op jit(solution)/shard_map/hqk,khd->qhd/dot_general | solution.py:107
  266.8 3.5 %fusion.27 = f32[256,4,128]{2,0,1:T(8,128)S(1)} fusion(bf16[4,256,2048]{2,1,0:T(8,128)(2,1)} %fusion.2, bf16[2048,8,128]{0,2,1:T(8,128)(2,1)S(1)} %bitcast.52), kind=kOutput, calls=%fused_computation.32 | convolution fusion | flops 536870912 | bytes 6815744 | tf_op jit(solution)/shard_map/hqk,khd->qhd/dot_general | solution.py:107
  272.1 10.0 %reduce-scatter.5.cloned.1.call-done = bf16[256,8,128]{2,0,1:T(8,128)(2,1)} async-done(((bf16[2048,8,128]{2,0,1:T(8,128)(2,1)}), bf16[256,8,128]{2,0,1:T(8,128)(2,1)}) %reduce-scatter.5.cloned.1.call-update) | async-done | bytes 524304 | tf_op jit(solution)/shard_map/reduce_scatter | solution.py:122
  283.2 7.9 %fusion.39 = f32[1024,640]{1,0:T(8,128)} fusion(bf16[2048,1024]{0,1:T(8,128)(2,1)} %all-gather.12.cloned.1.call-done, bf16[2048,640]{1,0:T(8,128)(2,1)} %bitcast.66), kind=kOutput, calls=%fused_computation.53 | convolution fusion | flops 2684354560 | bytes 9437184 | tf_op jit(solution)/shard_map/th,td->hd/dot_general | solution.py:127
  291.1 45.3 %reduce-scatter.3.cloned.1.call-done = bf16[256,8,128]{2,0,1:T(8,128)(2,1)} async-done(((bf16[2048,8,128]{2,0,1:T(8,128)(2,1)}), bf16[256,8,128]{2,0,1:T(8,128)(2,1)}) %reduce-scatter.3.cloned.1.call-update) | async-done | bytes 524304 | tf_op jit(solution)/shard_map/reduce_scatter | solution.py:122
  (81 shorter events, 41.5 us)
Async XLA Ops:
  7.2 110.5 %all-gather.6.cloned.1.call-start = ((), (), s32[]{:S(2)}) async-start(), calls=%async_computation.3 | async-start | bytes 4718592 | tf_op jit(solution)/shard_map/all_gather | solution.py:64
  9.3 108.3 %all-gather.8.cloned.1.call-start = ((), (), s32[]{:S(2)}) async-start(), calls=%async_computation.4 | async-start | bytes 4718592 | tf_op jit(solution)/shard_map/all_gather | solution.py:63
  11.5 161.2 %all-gather.10.cloned.1.call-start = ((), (), s32[]{:S(2)}) async-start(), calls=%async_computation.5 | async-start | bytes 11796480 | tf_op jit(solution)/shard_map/all_gather | solution.py:81
  12.4 21.0 %collective-permute-start = (bf16[256,1280]{0,1:T(8,128)(2,1)S(1)}, bf16[256,1280]{0,1:T(8,128)(2,1)}, u32[]{:S(2)}, u32[]{:S(2)}) collective-permute-start(bf16[256,1280]{0,1:T(8,128)(2,1)S(1)} %copy.76), channel_id=1, source_target_pairs={{0,1},{1,2},{2,3},{3,0},{4,5},{5,6},{6,7},{7,4},{8,9},{9,10},{10,1... | collective-permute-start | bytes 1966088 | tf_op jit(solution)/shard_map/ppermute | solution.py:29
  15.6 45.1 %collective-permute-start.1 = (bf16[256,1280]{0,1:T(8,128)(2,1)S(1)}, bf16[256,1280]{0,1:T(8,128)(2,1)}, u32[]{:S(2)}, u32[]{:S(2)}) collective-permute-start(bf16[256,1280]{0,1:T(8,128)(2,1)S(1)} %copy.76), channel_id=1, source_target_pairs={{0,2},{1,3},{2,0},{3,1},{4,6},{5,7},{6,4},{7,5},{8,10},{9,11},{10,... | collective-permute-start | bytes 1966088 | tf_op jit(solution)/shard_map/ppermute | solution.py:29
  18.1 43.7 %collective-permute-start.2 = (bf16[256,1280]{0,1:T(8,128)(2,1)S(1)}, bf16[256,1280]{0,1:T(8,128)(2,1)}, u32[]{:S(2)}, u32[]{:S(2)}) collective-permute-start(bf16[256,1280]{0,1:T(8,128)(2,1)S(1)} %copy.76), channel_id=1, source_target_pairs={{0,3},{1,0},{2,1},{3,2},{4,7},{5,4},{6,5},{7,6},{8,11},{9,8},{10,9... | collective-permute-start | bytes 1966088 | tf_op jit(solution)/shard_map/ppermute | solution.py:29
  34.5 35.7 %copy-start.9 = (s32[256]{0:T(256)S(1)}, s32[256]{0:T(256)}, u32[]{:S(2)}) copy-start(s32[256]{0:T(256)} %param.9) | copy-start | bytes 3076
  64.5 50.6 %all-to-all-start = ((bf16[256,8,640]{0,2,1:T(8,128)(2,1)}), bf16[256,8,640]{0,2,1:T(8,128)(2,1)S(1)}, u32[]{:S(2)}, u32[]{:S(2)}) async-start(bf16[256,8,640]{0,2,1:T(8,128)(2,1)} %bitcast.54), calls=%async_computation | async-start | bytes 5242880 | tf_op jit(solution)/shard_map/all_to_all | solution.py:67
  68.2 194.3 %all-gather.12.cloned.1.call-start = ((), (), s32[]{:S(2)}) async-start(), calls=%async_computation.6 | async-start | bytes 4718592 | tf_op jit(solution)/shard_map/all_gather | solution.py:89
  127.8 44.9 %copy-start.2 = (bf16[256,5120]{0,1:T(8,128)(2,1)S(1)}, bf16[256,5120]{0,1:T(8,128)(2,1)}, u32[]{:S(2)}) copy-start(bf16[256,5120]{0,1:T(8,128)(2,1)} %copy-done.1) | copy-start | bytes 7864324
  181.6 15.7 %copy-start.6 = (bf16[256,1024]{0,1:T(8,128)(2,1)}, bf16[256,1024]{0,1:T(8,128)(2,1)S(1)}, u32[]{:S(2)}) copy-start(bf16[256,1024]{0,1:T(8,128)(2,1)S(1)} %copy.86) | copy-start | bytes 1572868
  190.2 91.8 %reduce-scatter.5.cloned.1.call-start = ((), (), s32[]{:S(2)}) async-start(), calls=%async_computation.8 | async-start | bytes 4718592 | tf_op jit(solution)/shard_map/reduce_scatter | solution.py:122
  190.5 5.2 %copy-start.3 = (bf16[256,1024]{0,1:T(8,128)(2,1)S(1)}, bf16[256,1024]{0,1:T(8,128)(2,1)}, u32[]{:S(2)}) copy-start(bf16[256,1024]{0,1:T(8,128)(2,1)} %copy.82) | copy-start | bytes 1572868
  195.6 5.7 %copy-start.5 = (bf16[4,256,2048]{2,1,0:T(8,128)(2,1)}, bf16[4,256,2048]{2,1,0:T(8,128)(2,1)S(1)}, u32[]{:S(2)}) copy-start(bf16[4,256,2048]{2,1,0:T(8,128)(2,1)S(1)} %fusion.1) | copy-start | bytes 12582916
  203.7 132.7 %reduce-scatter.3.cloned.1.call-start = ((), (), s32[]{:S(2)}) async-start(), calls=%async_computation.7 | async-start | bytes 4718592 | tf_op jit(solution)/shard_map/reduce_scatter | solution.py:122
  203.8 14.0 %copy-start.7 = (bf16[256,1024]{0,1:T(8,128)(2,1)S(1)}, bf16[256,1024]{0,1:T(8,128)(2,1)}, u32[]{:S(2)}) copy-start(bf16[256,1024]{0,1:T(8,128)(2,1)} %copy-done.6) | copy-start | bytes 1572868
  203.8 18.5 %slice-start = ((s8[16777216]{0:T(1024)(128)(4,1)}), s8[4194304]{0:T(1024)(128)(4,1)S(1)}, s32[]{:S(2)}) async-start(s8[16777216]{0:T(1024)(128)(4,1)} %bitcast.48), calls=%async_computation.9 | async-start | bytes 8388608
  203.8 18.5 %slice-start.1 = ((s8[16777216]{0:T(1024)(128)(4,1)}), s8[4194304]{0:T(1024)(128)(4,1)S(1)}, s32[]{:S(2)}) async-start(s8[16777216]{0:T(1024)(128)(4,1)} %bitcast.48), calls=%async_computation.10 | async-start | bytes 8388608
  211.1 11.3 %slice-start.2 = ((s8[16777216]{0:T(1024)(128)(4,1)}), s8[4194304]{0:T(1024)(128)(4,1)S(1)}, s32[]{:S(2)}) async-start(s8[16777216]{0:T(1024)(128)(4,1)} %bitcast.48), calls=%async_computation.11 | async-start | bytes 8388608
  212.4 19.9 %collective-permute-start.3 = (bf16[256,1280]{1,0:T(8,128)(2,1)}, bf16[256,1280]{1,0:T(8,128)(2,1)}, u32[]{:S(2)}, u32[]{:S(2)}) collective-permute-start(bf16[256,1280]{1,0:T(8,128)(2,1)} %get-tuple-element.32), channel_id=1, source_target_pairs={{0,1},{1,2},{2,3},{3,0},{4,5},{5,6},{6,7},{7,4},{8,9},{9,10},{10,1... | collective-permute-start | bytes 1966088 | tf_op jit(solution)/shard_map/ppermute | solution.py:55
  213.9 45.7 %collective-permute-start.4 = (bf16[256,1280]{1,0:T(8,128)(2,1)}, bf16[256,1280]{1,0:T(8,128)(2,1)}, u32[]{:S(2)}, u32[]{:S(2)}) collective-permute-start(bf16[256,1280]{1,0:T(8,128)(2,1)} %get-tuple-element.34), channel_id=1, source_target_pairs={{0,2},{1,3},{2,0},{3,1},{4,6},{5,7},{6,4},{7,5},{8,10},{9,11},{10,... | collective-permute-start | bytes 1966088 | tf_op jit(solution)/shard_map/ppermute | solution.py:55
  216.3 6.0 %slice-start.3 = ((s8[16777216]{0:T(1024)(128)(4,1)}), s8[4194304]{0:T(1024)(128)(4,1)S(1)}, s32[]{:S(2)}) async-start(s8[16777216]{0:T(1024)(128)(4,1)} %bitcast.48), calls=%async_computation.12 | async-start | bytes 8388608
  216.3 6.0 %copy-start.4 = (bf16[2048,1024]{0,1:T(8,128)(2,1)S(1)}, bf16[2048,1024]{0,1:T(8,128)(2,1)}, u32[]{:S(2)}) copy-start(bf16[2048,1024]{0,1:T(8,128)(2,1)} %all-gather.6.cloned.1.call-done) | copy-start | bytes 12582916
  216.3 43.3 %collective-permute-start.5 = (bf16[256,1280]{1,0:T(8,128)(2,1)}, bf16[256,1280]{1,0:T(8,128)(2,1)}, u32[]{:S(2)}, u32[]{:S(2)}) collective-permute-start(bf16[256,1280]{1,0:T(8,128)(2,1)} %get-tuple-element.33), channel_id=1, source_target_pairs={{0,3},{1,0},{2,1},{3,2},{4,7},{5,4},{6,5},{7,6},{8,11},{9,8},{10,9... | collective-permute-start | bytes 1966088 | tf_op jit(solution)/shard_map/ppermute | solution.py:55
  (3 other events, 10.8 us)
Sparse Core Ops, SparseCore 0:
  10.4 40.0 all-gather.5
  53.0 53.2 all-gather.7
  108.2 64.4 all-gather.9
  190.4 37.3 all-gather.11
  230.9 51.0 reduce-scatter.4
  285.3 51.0 reduce-scatter.2

commit v8 on v6

--- a/solution.py
+++ b/solution.py
@@ -60,8 +60,11 @@
     local_tokens = query_states.shape[0]
     query_heads = split_heads(query_states)
     local_heads = query_heads.shape[1]
-    all_keys = lax.all_gather(key_states, "seq", axis=0, tiled=True)
-    all_values = lax.all_gather(value_states, "seq", axis=0, tiled=True)
+    model_cols = key_states.shape[1]
+    packed = jnp.concatenate([key_states, value_states], axis=1)
+    all_packed = lax.all_gather(packed, "seq", axis=0, tiled=True)
+    all_keys = all_packed[:, :model_cols]
+    all_values = all_packed[:, model_cols:]
     all_pos = lax.all_gather(positions, "seq", axis=0, tiled=True)
     key_heads = split_heads(all_keys)
     value_heads = split_heads(all_values)

time: 339 us -> 318 us (0.938)
  waiting for transfers between devices: 138 us -> 117 us
  other arithmetic: 22.2 us -> 34.8 us
  blocking collectives: 50.1 us -> 44.5 us
  matrix products: 67.5 us -> 63.7 us
    all_gather x1, waiting for transfers between devices: 45.5 us -> 25.9 us  [shards(): weight_full = lax.all_gather(out_weight, 'seq', axis=1, tiled=True)]
    ppermute x3, waiting for transfers between devices: 27.6 us -> 43.5 us  [permute_sum_scatter(): total = total + lax.ppermute(piece, axis, route).astype(jnp.float32)]
    all_gather x2 -> x1, waiting for transfers between devices: 18.5 us -> 6.21 us  [shards(): all_packed = lax.all_gather(packed, 'seq', axis=0, tiled=True)]
    convert_element_type x1, other arithmetic: 9.44 us -> 16.3 us  [shards(): weights = probs.astype(jnp.bfloat16)]
    all_gather x1 -> x0, local copies, waits for them, and re-layouts: 6.88 us -> none  [shards(): all_values = lax.all_gather(value_states, 'seq', axis=0, tiled=True)]
    all_to_all x1, blocking collectives: 41 us -> 35.4 us  [shards(): cotangent_cols = lax.all_to_all(cotangent_full, 'seq', 1, 0, tiled=True)]
    slice x0 -> x1, local copies, waits for them, and re-layouts: none -> 5.32 us  [shards(): all_keys = all_packed[:, :model_cols]]
    reduce_sum x1, other arithmetic: 4.51 us -> 9.16 us  [shards(): jnp.sum(jnp.exp(scores - row_max[:, :, None]), axis=2)]
  transfers between devices with their start and end apart: 12 -> 11, of which waited for: 7 -> 7; matrix products, arithmetic and copies ran while one was open for 29% -> 33% of each run, Pallas kernels for 0% -> 0%
where the time goes in v8:
time: 318 us; the launch traced here: 317 us
  waiting for transfers between devices  117 us (37%)
  matrix products  63.7 us (20%)
  blocking collectives  44.5 us (14%)
  other arithmetic  34.8 us (11%)
  local copies, waits for them, and re-layouts  31.9 us (10%)
  between operations  14.2 us (4%)
  starting transfers between devices  11.6 us (4%)
    ppermute x3, waiting for transfers between devices, permute_sum_scatter(): total = total + lax.ppermute(piece, axis, route).astype(jnp.float32)  43.5 us
    all_to_all x1, blocking collectives, shards(): cotangent_cols = lax.all_to_all(cotangent_full, 'seq', 1, 0, tiled=True)  35.4 us
    ppermute x3, waiting for transfers between devices, shift_pieces(): pieces.append(lax.ppermute(block, axis, route))  28.3 us
    all_gather x1, waiting for transfers between devices, shards(): weight_full = lax.all_gather(out_weight, 'seq', axis=1, tiled=True)  25.9 us
    convert_element_type x1, other arithmetic, shards(): weights = probs.astype(jnp.bfloat16)  16.3 us
    unnamed x41, local copies, waits for them, and re-layouts  12.8 us
    reduce_scatter x2, waiting for transfers between devices, shards(): lax.psum_scatter(both_parts, 'seq', scatter_dimension=0, tiled=True)  11.8 us
    dot_general x2, matrix products, shards(): jnp.einsum('qhd,khd->hqk', half_grads, value_heads[:, heads], preferred_e...  9.73 us
  transfers between devices with their start and end apart: 11, of which 7 were waited for; matrix products, arithmetic and copies ran while one was open for 33% of the time, Pallas kernels for 0%

profile of v8, /device:TPU:0, one launch (start us, length us, event | category | flops | bytes accessed | tf_op | source)
XLA Modules:
  0.0 317.3 jit_solution(15091850449423641396)
XLA Ops:
  12.8 3.1 collective-permute-start.3
  19.8 9.1 %all-gather = s32[8,1,256]{2,1,0:T(1,128)S(1)} all-gather(s32[1,1,256]{2,1,0:T(1,128)S(1)} %bitcast.82), channel_id=1, replica_groups=mesh['seq'=8,'fsdp'=4] {'seq'}, dimensions={0}, use_global_device_ids=true | all-gather | bytes 9216 | tf_op jit(solution)/shard_map/all_gather | solution.py:68
  35.0 26.1 %collective-permute-done.4 = bf16[256,1280]{0,1:T(8,128)(2,1)} collective-permute-done((bf16[256,1280]{0,1:T(8,128)(2,1)}, bf16[256,1280]{0,1:T(8,128)(2,1)}, u32[]{:S(2)}, u32[]{:S(2)}) %collective-permute-start.4) | collective-permute-done | bytes 655392 | tf_op jit(solution)/shard_map/ppermute | solution.py:29
  63.4 6.2 %all-gather.5.cloned.1.call-done = bf16[2048,2048]{0,1:T(8,128)(2,1)} async-done(((bf16[256,2048]{0,1:T(8,128)(2,1)}), bf16[2048,2048]{0,1:T(8,128)(2,1)}) %all-gather.5.cloned.1.call-update) | async-done | bytes 8388624 | tf_op jit(solution)/shard_map/all_gather | solution.py:65
  69.6 5.3 %fusion.26 = (bf16[2048,1024]{0,1:T(8,128)(2,1)S(1)}, bf16[2048,1024]{0,1:T(8,128)(2,1)}) fusion(bf16[2048,2048]{0,1:T(8,128)(2,1)} %all-gather.5.cloned.1.call-done), kind=kLoop, calls=%fused_computation.47 | loop fusion | bytes 16777216 | tf_op jit(solution)/shard_map/slice | solution.py:66
  75.0 8.1 %fusion = (f32[8,256]{1,0:T(8,128)S(1)}, f32[8,2048,256]{2,1,0:T(8,128)}) fusion(pred[256,2048]{0,1:T(8,128)(4,1)S(1)} %broadcast_compare_fusion, bf16[2048,8,128]{0,2,1:T(8,128)(2,1)S(1)} %bitcast.62, bf16[256,8,128]{0,2,1:T(8,128)(2,1)S(1)} %bitcast.69), kind=kOutput, calls=%fused_computation.3 | convolution fusion | flops 1086322688 | bytes 22028288 | tf_op jit(solution)/shard_map/qhd,khd->hqk/dot_general | solution.py:17
  83.1 9.2 %exponential_reduce_fusion = f32[8,256]{1,0:T(8,128)S(1)} fusion(f32[8,2048,256]{2,1,0:T(8,128)} %get-tuple-element.40, f32[8,256]{1,0:T(8,128)S(1)} %get-tuple-element.39, pred[256,2048]{0,1:T(8,128)(4,1)S(1)} %broadcast_compare_fusion), kind=kLoop, calls=%fused_computation.2 | loop fusion | flops 16775168 | bytes 17317888 | tf_op jit(solution)/shard_map/reduce_sum | solution.py:73
  92.3 16.3 %fusion.25 = (bf16[8,256,2048]{1,2,0:T(8,128)(2,1)}, f32[8,256,2048]{1,2,0:T(8,128)}) fusion(f32[8,256]{1,0:T(8,128)S(1)} %log_add_fusion, f32[8,2048,256]{2,1,0:T(8,128)} %get-tuple-element.40, pred[256,2048]{0,1:T(8,128)(4,1)S(1)} %broadcast_compare_fusion), kind=kLoop, calls=%fused_computation.46 | loop fusion | flops 16777216 | bytes 42475520 | tf_op jit(solution)/shard_map/convert_element_type | solution.py:75
  108.6 25.9 %all-gather.7.cloned.1.call-done = bf16[1024,5120]{1,0:T(8,128)(2,1)} async-done(((bf16[1024,640]{1,0:T(8,128)(2,1)}), bf16[1024,5120]{1,0:T(8,128)(2,1)}) %all-gather.7.cloned.1.call-update) | async-done | bytes 10485776 | tf_op jit(solution)/shard_map/all_gather | solution.py:81
  134.5 6.9 %convolution_convert_fusion.3 = bf16[256,1024]{1,0:T(8,128)(2,1)S(1)} fusion(bf16[256,5120]{0,1:T(8,128)(2,1)S(1)} %constant_dynamic-update-slice_fusion, bf16[1024,5120]{1,0:T(8,128)(2,1)} %all-gather.7.cloned.1.call-done), kind=kOutput, calls=%fused_computation.26 | convolution fusion | flops 2684616704 | bytes 13631488 | tf_op jit(solution)/shard_map/td,hd->th/dot_general | solution.py:87
  141.7 6.9 %multiply_reduce_fusion = (f32[256,8]{0,1:T(8,128)S(1)}, bf16[8,128,256]{2,1,0:T(8,128)(2,1)}) fusion(bf16[256,1024]{0,1:T(8,128)(2,1)S(1)} %copy.103, bf16[2048,8,128]{0,2,1:T(8,128)(2,1)} %bitcast.59, bf16[8,256,2048]{1,2,0:T(8,128)(2,1)} %get-tuple-element.26), kind=kOutput, calls=%fused_computation.34 | convolution fusion | flops 1075050496 | bytes 13639680 | tf_op jit(solution)/shard_map/hqk,khd->qhd/dot_general | solution.py:76
  148.7 5.4 %fusion.1 = bf16[4,256,2048]{1,2,0:T(8,128)(2,1)S(1)} fusion(f32[8,256,2048]{1,2,0:T(8,128)} %get-tuple-element.27, f32[4,256]{1,0:T(4,128)S(1)} %get-tuple-element.37, bf16[256,8,128]{0,2,1:T(8,128)(2,1)S(1)} %bitcast.75, bf16[2048,8,128]{0,2,1:T(8,128)(2,1)} %bitcast.60), kind=kOutput, calls=%fused_computation.5 | convolution fusion | flops 543162368 | bytes 15208448 | tf_op jit(solution)/shard_map/qhd,khd->hqk/dot_general | solution.py:102
  155.4 4.0 %fusion.15 = bf16[2048,4,128]{2,0,1:T(8,128)(2,1)S(1)} fusion(bf16[256,8,128]{0,2,1:T(8,128)(2,1)S(1)} %bitcast.76, bf16[8,256,2048]{1,2,0:T(8,128)(2,1)} %get-tuple-element.26), kind=kOutput, calls=%fused_computation.21 | convolution fusion | flops 537919488 | bytes 6815744 | tf_op jit(solution)/shard_map/hqk,qhd->khd/dot_general | solution.py:116
  162.8 7.2 %convolution_convert_fusion = bf16[256,5120]{1,0:T(8,128)(2,1)S(1)} fusion(bf16[256,1024]{0,1:T(8,128)(2,1)S(1)} %bitcast.68, bf16[1024,5120]{1,0:T(8,128)(2,1)} %all-gather.7.cloned.1.call-done), kind=kOutput, calls=%fused_computation.8 | convolution fusion | flops 2685665280 | bytes 13631488 | tf_op jit(solution)/shard_map/dot_general | solution.py:82
  171.2 3.3 %collective-permute-start.2 = (bf16[256,1280]{1,0:T(8,128)(2,1)}, bf16[256,1280]{1,0:T(8,128)(2,1)}, u32[]{:S(2)}, u32[]{:S(2)}) collective-permute-start(bf16[256,1280]{1,0:T(8,128)(2,1)} %get-tuple-element.31), channel_id=1, source_target_pairs={{0,3},{1,0},{2,1},{3,2},{4,7},{5,4},{6,5},{7,6},{8,11},{9,8},{10,9... | collective-permute-start | bytes 1966088 | tf_op jit(solution)/shard_map/ppermute | solution.py:55
  175.7 3.6 %fusion.18 = bf16[2048,4,128]{2,0,1:T(8,128)(2,1)S(1)} fusion(bf16[256,8,128]{0,2,1:T(8,128)(2,1)S(1)} %bitcast.77, bf16[8,256,2048]{1,2,0:T(8,128)(2,1)} %get-tuple-element.26), kind=kOutput, calls=%fused_computation.22 | convolution fusion | flops 537919488 | bytes 6815744 | tf_op jit(solution)/shard_map/hqk,qhd->khd/dot_general | solution.py:116
  179.3 4.3 %fusion.2 = bf16[4,256,2048]{1,2,0:T(8,128)(2,1)S(1)} fusion(f32[8,256,2048]{1,2,0:T(8,128)} %get-tuple-element.27, f32[4,256]{1,0:T(4,128)S(1)} %get-tuple-element.38, bf16[256,8,128]{0,2,1:T(8,128)(2,1)S(1)} %bitcast.78, bf16[2048,8,128]{0,2,1:T(8,128)(2,1)S(1)} %bitcast.61), kind=kOutput, calls=%fused_computation.7 | convolution fusion | flops 543162368 | bytes 15208448 | tf_op jit(solution)/shard_map/qhd,khd->hqk/dot_general | solution.py:102
  190.1 41.4 %collective-permute-done.1 = bf16[256,1280]{1,0:T(8,128)(2,1)} collective-permute-done((bf16[256,1280]{1,0:T(8,128)(2,1)}, bf16[256,1280]{1,0:T(8,128)(2,1)}, u32[]{:S(2)}, u32[]{:S(2)}) %collective-permute-start.1) | collective-permute-done | bytes 655392 | tf_op jit(solution)/shard_map/ppermute | solution.py:55
  231.5 2.9 convert_add_fusion
  236.1 35.4 %all_to_all.19 = bf16[256,8,640]{0,2,1:T(8,128)(2,1)} all-to-all(bf16[256,8,640]{0,2,1:T(8,128)(2,1)S(1)} %bitcast.65), channel_id=1, replica_groups=mesh['seq'=8,'fsdp'=4] {'seq'}, dimensions={1} | all-to-all | bytes 5242880 | tf_op jit(solution)/shard_map/all_to_all | solution.py:91
  271.5 4.5 %copy.123 = bf16[8,256,640]{2,1,0:T(8,128)(2,1)} copy(bf16[8,256,640]{1,2,0:T(8,128)(2,1)} %bitcast.66) | data formatting | bytes 5242880 | tf_op jit(solution)/shard_map/all_to_all | solution.py:91
  275.9 5.2 %convolution_bitcast_fusion = f32[256,4,128]{2,0,1:T(8,128)S(1)} fusion(bf16[2048,8,128]{0,2,1:T(8,128)(2,1)} %bitcast.63, bf16[4,256,2048]{1,2,0:T(8,128)(2,1)} %copy-done.9), kind=kOutput, calls=%fused_computation.28 | convolution fusion | flops 536870912 | bytes 8912896 | tf_op jit(solution)/shard_map/hqk,khd->qhd/dot_general | solution.py:109
  286.4 7.9 %fusion.30 = f32[1024,640]{1,0:T(8,128)} fusion(bf16[2048,1024]{0,1:T(8,128)(2,1)} %all-gather.9.cloned.1.call-done, bf16[2048,640]{1,0:T(8,128)(2,1)} %bitcast.79), kind=kOutput, calls=%fused_computation.51 | convolution fusion | flops 2684354560 | bytes 9437184 | tf_op jit(solution)/shard_map/th,td->hd/dot_general | solution.py:129
  294.3 11.8 %reduce-scatter.3.cloned.1.call-done = bf16[256,8,128]{2,0,1:T(8,128)(2,1)} async-done(((bf16[2048,8,128]{2,0,1:T(8,128)(2,1)}), bf16[256,8,128]{2,0,1:T(8,128)(2,1)}) %reduce-scatter.3.cloned.1.call-update) | async-done | bytes 524304 | tf_op jit(solution)/shard_map/reduce_scatter | solution.py:124
  (84 shorter events, 43.0 us)
Async XLA Ops:
  7.2 4.5 %copy-start.14 = (bf16[256,1280]{1,0:T(8,128)(2,1)S(1)}, bf16[256,1280]{1,0:T(8,128)(2,1)}, u32[]{:S(2)}) copy-start(bf16[256,1280]{1,0:T(8,128)(2,1)} %param.11) | copy-start | bytes 1966084
  7.2 12.6 %copy-start.16 = (s32[256]{0:T(256)S(1)}, s32[256]{0:T(256)}, u32[]{:S(2)}) copy-start(s32[256]{0:T(256)} %param.9) | copy-start | bytes 3076
  7.2 22.2 %copy-start.15 = (bf16[256,1024]{1,0:T(8,128)(2,1)S(1)}, bf16[256,1024]{1,0:T(8,128)(2,1)}, u32[]{:S(2)}) copy-start(bf16[256,1024]{1,0:T(8,128)(2,1)} %param.6) | copy-start | bytes 1572868
  7.2 62.4 %all-gather.5.cloned.1.call-start = ((), (), s32[]{:S(2)}) async-start(), calls=%async_computation.3 | async-start | bytes 9437184 | tf_op jit(solution)/shard_map/all_gather | solution.py:65
  10.9 123.7 %all-gather.7.cloned.1.call-start = ((), (), s32[]{:S(2)}) async-start(), calls=%async_computation.4 | async-start | bytes 11796480 | tf_op jit(solution)/shard_map/all_gather | solution.py:81
  11.6 222.7 %all-gather.9.cloned.1.call-start = ((), (), s32[]{:S(2)}) async-start(), calls=%async_computation.5 | async-start | bytes 4718592 | tf_op jit(solution)/shard_map/all_gather | solution.py:90
  12.8 21.1 %collective-permute-start.3 = (bf16[256,1280]{0,1:T(8,128)(2,1)}, bf16[256,1280]{0,1:T(8,128)(2,1)}, u32[]{:S(2)}, u32[]{:S(2)}) collective-permute-start(bf16[256,1280]{0,1:T(8,128)(2,1)} %copy.99), channel_id=1, source_target_pairs={{0,1},{1,2},{2,3},{3,0},{4,5},{5,6},{6,7},{7,4},{8,9},{9,10},{10,1... | collective-permute-start | bytes 1966088 | tf_op jit(solution)/shard_map/ppermute | solution.py:29
  15.8 45.3 %collective-permute-start.4 = (bf16[256,1280]{0,1:T(8,128)(2,1)}, bf16[256,1280]{0,1:T(8,128)(2,1)}, u32[]{:S(2)}, u32[]{:S(2)}) collective-permute-start(bf16[256,1280]{0,1:T(8,128)(2,1)} %copy.99), channel_id=1, source_target_pairs={{0,2},{1,3},{2,0},{3,1},{4,6},{5,7},{6,4},{7,5},{8,10},{9,11},{10,... | collective-permute-start | bytes 1966088 | tf_op jit(solution)/shard_map/ppermute | solution.py:29
  18.4 43.8 %collective-permute-start.5 = (bf16[256,1280]{0,1:T(8,128)(2,1)}, bf16[256,1280]{0,1:T(8,128)(2,1)}, u32[]{:S(2)}, u32[]{:S(2)}) collective-permute-start(bf16[256,1280]{0,1:T(8,128)(2,1)} %copy.99), channel_id=1, source_target_pairs={{0,3},{1,0},{2,1},{3,2},{4,7},{5,4},{6,5},{7,6},{8,11},{9,8},{10,9... | collective-permute-start | bytes 1966088 | tf_op jit(solution)/shard_map/ppermute | solution.py:29
  63.4 71.1 %copy-start.3 = (bf16[256,5120]{0,1:T(8,128)(2,1)}, bf16[256,5120]{0,1:T(8,128)(2,1)S(1)}, u32[]{:S(2)}) copy-start(bf16[256,5120]{0,1:T(8,128)(2,1)S(1)} %constant_dynamic-update-slice_fusion) | copy-start | bytes 7864324
  69.6 5.3 %copy-start.6 = (bf16[256,1024]{0,1:T(8,128)(2,1)S(1)}, bf16[256,1024]{0,1:T(8,128)(2,1)}, u32[]{:S(2)}) copy-start(bf16[256,1024]{0,1:T(8,128)(2,1)} %copy.95) | copy-start | bytes 1572868
  75.0 8.2 %copy-start.1 = (bf16[2048,1024]{0,1:T(8,128)(2,1)}, bf16[2048,1024]{0,1:T(8,128)(2,1)S(1)}, u32[]{:S(2)}) copy-start(bf16[2048,1024]{0,1:T(8,128)(2,1)S(1)} %get-tuple-element.28) | copy-start | bytes 12582916
  141.7 13.7 %copy-start.12 = (bf16[256,1024]{0,1:T(8,128)(2,1)}, bf16[256,1024]{0,1:T(8,128)(2,1)S(1)}, u32[]{:S(2)}) copy-start(bf16[256,1024]{0,1:T(8,128)(2,1)S(1)} %copy.103) | copy-start | bytes 1572868
  148.6 136.7 %reduce-scatter.5.cloned.1.call-start = ((), (), s32[]{:S(2)}) async-start(), calls=%async_computation.7 | async-start | bytes 4718592 | tf_op jit(solution)/shard_map/reduce_scatter | solution.py:124
  148.7 5.4 %copy-start.7 = (bf16[256,1024]{0,1:T(8,128)(2,1)S(1)}, bf16[256,1024]{0,1:T(8,128)(2,1)}, u32[]{:S(2)}) copy-start(bf16[256,1024]{0,1:T(8,128)(2,1)} %copy.95) | copy-start | bytes 1572868
  154.1 5.3 %copy-start.9 = (bf16[4,256,2048]{1,2,0:T(8,128)(2,1)}, bf16[4,256,2048]{1,2,0:T(8,128)(2,1)S(1)}, u32[]{:S(2)}) copy-start(bf16[4,256,2048]{1,2,0:T(8,128)(2,1)S(1)} %fusion.1) | copy-start | bytes 12582916
  161.8 144.4 %reduce-scatter.3.cloned.1.call-start = ((), (), s32[]{:S(2)}) async-start(), calls=%async_computation.6 | async-start | bytes 4718592 | tf_op jit(solution)/shard_map/reduce_scatter | solution.py:124
  162.8 12.9 %copy-start.13 = (bf16[256,1024]{0,1:T(8,128)(2,1)S(1)}, bf16[256,1024]{0,1:T(8,128)(2,1)}, u32[]{:S(2)}) copy-start(bf16[256,1024]{0,1:T(8,128)(2,1)} %copy-done.12) | copy-start | bytes 1572868
  171.2 18.8 %collective-permute-start.2 = (bf16[256,1280]{1,0:T(8,128)(2,1)}, bf16[256,1280]{1,0:T(8,128)(2,1)}, u32[]{:S(2)}, u32[]{:S(2)}) collective-permute-start(bf16[256,1280]{1,0:T(8,128)(2,1)} %get-tuple-element.31), channel_id=1, source_target_pairs={{0,3},{1,0},{2,1},{3,2},{4,7},{5,4},{6,5},{7,6},{8,11},{9,8},{10,9... | collective-permute-start | bytes 1966088 | tf_op jit(solution)/shard_map/ppermute | solution.py:55
  174.6 56.9 %collective-permute-start.1 = (bf16[256,1280]{1,0:T(8,128)(2,1)}, bf16[256,1280]{1,0:T(8,128)(2,1)}, u32[]{:S(2)}, u32[]{:S(2)}) collective-permute-start(bf16[256,1280]{1,0:T(8,128)(2,1)} %get-tuple-element.32), channel_id=1, source_target_pairs={{0,2},{1,3},{2,0},{3,1},{4,6},{5,7},{6,4},{7,5},{8,10},{9,11},{10,... | collective-permute-start | bytes 1966088 | tf_op jit(solution)/shard_map/ppermute | solution.py:55
  174.6 4.7 %copy-start = (bf16[2048,1024]{0,1:T(8,128)(2,1)S(1)}, bf16[2048,1024]{0,1:T(8,128)(2,1)}, u32[]{:S(2)}) copy-start(bf16[2048,1024]{0,1:T(8,128)(2,1)} %get-tuple-element.29) | copy-start | bytes 12582916
  174.6 56.9 %collective-permute-start = (bf16[256,1280]{1,0:T(8,128)(2,1)S(1)}, bf16[256,1280]{1,0:T(8,128)(2,1)}, u32[]{:S(2)}, u32[]{:S(2)}) collective-permute-start(bf16[256,1280]{1,0:T(8,128)(2,1)S(1)} %get-tuple-element.30), channel_id=1, source_target_pairs={{0,1},{1,2},{2,3},{3,0},{4,5},{5,6},{6,7},{7,4},{8,9},{9,10},{10,1... | collective-permute-start | bytes 1966088 | tf_op jit(solution)/shard_map/ppermute | solution.py:55
  275.9 5.2 %copy-start.2 = (bf16[2048,1024]{0,1:T(8,128)(2,1)S(1)}, bf16[2048,1024]{0,1:T(8,128)(2,1)}, u32[]{:S(2)}) copy-start(bf16[2048,1024]{0,1:T(8,128)(2,1)} %copy-done.1) | copy-start | bytes 12582916
  275.9 6.0 %copy-start.11 = (bf16[4,256,2048]{1,2,0:T(8,128)(2,1)S(1)}, bf16[4,256,2048]{1,2,0:T(8,128)(2,1)}, u32[]{:S(2)}) copy-start(bf16[4,256,2048]{1,2,0:T(8,128)(2,1)} %copy-done.10) | copy-start | bytes 12582916
  (4 other events, 9.2 us)
Sparse Core Ops, SparseCore 0:
  11.0 58.5 all-gather.4
  71.5 62.9 all-gather.6
  148.8 37.3 all-gather.8
  189.3 51.0 reduce-scatter.4
  243.7 62.4 reduce-scatter.2

commit v9 on v8

--- a/solution.py
+++ b/solution.py
@@ -61,10 +61,15 @@
     query_heads = split_heads(query_states)
     local_heads = query_heads.shape[1]
     model_cols = key_states.shape[1]
+    seq_count = lax.axis_size("seq")
     packed = jnp.concatenate([key_states, value_states], axis=1)
-    all_packed = lax.all_gather(packed, "seq", axis=0, tiled=True)
+    flat = jnp.concatenate([packed.reshape(-1), out_weight.reshape(-1)])
+    all_flat = lax.all_gather(flat, "seq", axis=0, tiled=False)
+    all_packed = all_flat[:, : packed.size].reshape(seq_count * local_tokens, 2 * model_cols)
     all_keys = all_packed[:, :model_cols]
     all_values = all_packed[:, model_cols:]
+    weight_blocks = all_flat[:, packed.size :].reshape((seq_count,) + out_weight.shape)
+    weight_full = weight_blocks.transpose(1, 0, 2).reshape(out_weight.shape[0], -1)
     all_pos = lax.all_gather(positions, "seq", axis=0, tiled=True)
     key_heads = split_heads(all_keys)
     value_heads = split_heads(all_values)
@@ -78,7 +83,6 @@
     )
     attended_heads = attended.astype(jnp.bfloat16)
     attended_flat = attended_heads.reshape(local_tokens, local_heads * HEAD_DIM)
-    weight_full = lax.all_gather(out_weight, "seq", axis=1, tiled=True)
     partial_sum = jnp.dot(attended_flat, weight_full, preferred_element_type=jnp.float32).astype(
         jnp.bfloat16
     )

time: 318 us -> 420 us (1.32); the launches traced: 317 us -> 415 us
  local copies, waits for them, and re-layouts: 31.9 us -> 108 us
  waiting for transfers between devices: 117 us -> 135 us
  other arithmetic: 34.8 us -> 40.2 us
    slice x0 -> x3, local copies, waits for them, and re-layouts: none -> 23.9 us  [the longest x1 9.81 us: shards(): all_flat[:, packed.size:].reshape((seq_count,) + out_weight.shape)]
    all_gather x0 -> x1, local copies, waits for them, and re-layouts: none -> 20.7 us  [shards(): all_flat = lax.all_gather(flat, 'seq', axis=0, tiled=False)]
    all_gather x2 -> x1, waiting for transfers between devices: 32.2 us -> 49.7 us  [shards(): all_flat = lax.all_gather(flat, 'seq', axis=0, tiled=False)]
    reshape x0 -> x2, local copies, waits for them, and re-layouts: none -> 13.2 us  [the longest x1 10.6 us: shards(): all_flat[:, :packed.size].reshape(seq_count * local_tokens, 2 * model_cols)]
    unnamed x41 -> x43, local copies, waits for them, and re-layouts: 12.8 us -> 22.5 us
    slice x1 -> x2, local copies, waits for them, and re-layouts: 5.32 us -> 12.8 us  [shards(): all_keys = all_packed[:, :model_cols]]
    concatenate x1, other arithmetic: 1.04 us -> 8.35 us  [shards(): flat = jnp.concatenate([packed.reshape(-1), out_weight.reshape(-1)])]
    dot_general x1, matrix products: 6.93 us -> 2.61 us  [shards(): jnp.einsum('hqk,khd->qhd', weights, value_heads, preferred_element_type=j...]
  transfers between devices with their start and end apart: 11 -> 10, of which waited for: 7 -> 6; matrix products, arithmetic and copies ran while one was open for 33% -> 15% of each run, Pallas kernels for 0% -> 0%
where the time goes in v9:
time: 420 us; the launch traced here: 415 us
  waiting for transfers between devices  135 us (32%)
  local copies, waits for them, and re-layouts  108 us (26%)
  matrix products  60 us (14%)
  blocking collectives  44.9 us (11%)
  other arithmetic  40.2 us (10%)
  between operations  14.5 us (3%)
  starting transfers between devices  11.8 us (3%)
    all_gather x1, waiting for transfers between devices, shards(): all_flat = lax.all_gather(flat, 'seq', axis=0, tiled=False)  49.7 us
    ppermute x3, waiting for transfers between devices, permute_sum_scatter(): total = total + lax.ppermute(piece, axis, route).astype(jnp.float32)  43.3 us
    all_to_all x1, blocking collectives, shards(): cotangent_cols = lax.all_to_all(cotangent_full, 'seq', 1, 0, tiled=True)  35.6 us
    ppermute x3, waiting for transfers between devices, shift_pieces(): pieces.append(lax.ppermute(block, axis, route))  28.1 us
    unnamed x43, local copies, waits for them, and re-layouts  22.5 us
    all_gather x1, local copies, waits for them, and re-layouts, shards(): all_flat = lax.all_gather(flat, 'seq', axis=0, tiled=False)  20.7 us
    reduce_scatter x2, waiting for transfers between devices, shards(): lax.psum_scatter(both_parts, 'seq', scatter_dimension=0, tiled=True)  14.1 us
    convert_element_type x1, other arithmetic, shards(): weights = probs.astype(jnp.bfloat16)  13.1 us
  transfers between devices with their start and end apart: 10, of which 6 were waited for; matrix products, arithmetic and copies ran while one was open for 15% of the time, Pallas kernels for 0%

profile of v9, /device:TPU:0, one launch (start us, length us, event | category | flops | bytes accessed | tf_op | source)
XLA Modules:
  0.0 414.6 jit_solution(7344904089034040698)
XLA Ops:
  11.4 8.4 %pad_maximum_fusion.2 = bf16[1179648]{0:T(1024)(128)(2,1)} fusion(bf16[655360]{0:T(1024)(128)(2,1)S(1)} %reshape.96, bf16[524288]{0:T(1024)(128)(2,1)S(1)} %bitcast.86), kind=kLoop, calls=%fused_computation.23 | loop fusion | flops 4718592 | bytes 4718592 | tf_op jit(solution)/shard_map/concatenate | solution.py:66
  27.9 9.3 %all-gather.1 = s32[8,1,256]{2,1,0:T(1,128)S(1)} all-gather(s32[1,1,256]{2,1,0:T(1,128)S(1)} %bitcast.94), channel_id=1, replica_groups=mesh['seq'=8,'fsdp'=4] {'seq'}, dimensions={0}, use_global_device_ids=true | all-gather | bytes 9216 | tf_op jit(solution)/shard_map/all_gather | solution.py:73
  43.1 26.1 %collective-permute-done.4 = bf16[256,1280]{0,1:T(8,128)(2,1)} collective-permute-done((bf16[256,1280]{0,1:T(8,128)(2,1)}, bf16[256,1280]{0,1:T(8,128)(2,1)}, u32[]{:S(2)}, u32[]{:S(2)}) %collective-permute-start.4) | collective-permute-done | bytes 655392 | tf_op jit(solution)/shard_map/ppermute | solution.py:29
  71.5 49.7 %all-gather.7.cloned.1.call-done = bf16[9437184]{0:T(1024)(128)(2,1)} async-done(((bf16[1179648]{0:T(1024)(128)(2,1)}), bf16[9437184]{0:T(1024)(128)(2,1)}) %all-gather.7.cloned.1.call-update) | async-done | bytes 18874384 | tf_op jit(solution)/shard_map/all_gather | solution.py:67
  121.2 20.7 %reshape.106 = bf16[8,1179648]{1,0:T(8,128)(2,1)} reshape(bf16[9437184]{0:T(1024)(128)(2,1)} %all-gather.7.cloned.1.call-done) | data formatting | bytes 37748736 | tf_op jit(solution)/shard_map/all_gather | solution.py:67
  142.0 9.8 %slice.91 = bf16[8,655360]{1,0:T(8,128)(2,1)} slice(bf16[8,1179648]{1,0:T(8,128)(2,1)} %reshape.106), slice={[0:8], [524288:1179648]} | slice | bytes 20971520 | tf_op jit(solution)/shard_map/slice | solution.py:71
  151.8 7.6 %slice.88 = bf16[8,524288]{1,0:T(8,128)(2,1)} slice(bf16[8,1179648]{1,0:T(8,128)(2,1)} %reshape.106), slice={[0:8], [0:524288]} | slice | bytes 16777216 | tf_op jit(solution)/shard_map/slice | solution.py:68
  159.3 10.5 %copy.146 = bf16[128,8,8,640]{3,1,2,0:T(8,128)(2,1)} copy(bf16[128,8,8,640]{3,2,1,0:T(8,128)(2,1)} %bitcast.69) | data formatting | bytes 20971520
  169.9 7.7 %convolution_convert_fusion.3 = bf16[256,1024]{1,0:T(8,128)(2,1)} fusion(bf16[256,5120]{0,1:T(8,128)(2,1)S(1)} %constant_dynamic-update-slice_fusion, bf16[1024,5120]{1,0:T(8,128)(2,1)} %bitcast.67), kind=kOutput, calls=%fused_computation.27 | convolution fusion | flops 2684616704 | bytes 13631488 | tf_op jit(solution)/shard_map/td,hd->th/dot_general | solution.py:91
  178.8 10.6 %reshape.97 = bf16[2048,2048]{1,0:T(8,128)(2,1)} reshape(bf16[8,524288]{1,0:T(8,128)(2,1)} %slice.88) | data formatting | bytes 16777216 | tf_op jit(solution)/shard_map/reshape | solution.py:68
  189.5 6.1 %fusion.26 = (bf16[2048,1024]{1,0:T(8,128)(2,1)}, bf16[2048,1024]{1,0:T(8,128)(2,1)}) fusion(bf16[2048,2048]{1,0:T(8,128)(2,1)} %reshape.97), kind=kLoop, calls=%fused_computation.48 | loop fusion | bytes 16777216 | tf_op jit(solution)/shard_map/slice | solution.py:69
  195.6 6.5 %copy.92 = bf16[2048,1024]{0,1:T(8,128)(2,1)} copy(bf16[2048,1024]{1,0:T(8,128)(2,1)} %get-tuple-element.29) | data formatting | bytes 8388608 | tf_op jit(solution)/shard_map/slice | solution.py:70
  202.1 6.7 %copy.93 = bf16[2048,1024]{0,1:T(8,128)(2,1)} copy(bf16[2048,1024]{1,0:T(8,128)(2,1)} %get-tuple-element.28) | data formatting | bytes 8388608 | tf_op jit(solution)/shard_map/slice | solution.py:69
  208.8 11.1 %fusion = (f32[8,256]{1,0:T(8,128)S(1)}, f32[8,2048,256]{2,1,0:T(8,128)}) fusion(pred[256,2048]{0,1:T(8,128)(4,1)S(1)} %broadcast_compare_fusion, bf16[2048,8,128]{0,2,1:T(8,128)(2,1)} %bitcast.73, bf16[256,8,128]{0,2,1:T(8,128)(2,1)S(1)} %bitcast.80), kind=kOutput, calls=%fused_computation.3 | convolution fusion | flops 1086322688 | bytes 22028288 | tf_op jit(solution)/shard_map/qhd,khd->hqk/dot_general | solution.py:17
  219.9 9.2 %exponential_reduce_fusion = f32[8,256]{1,0:T(8,128)S(1)} fusion(f32[8,2048,256]{2,1,0:T(8,128)} %get-tuple-element.40, f32[8,256]{1,0:T(8,128)S(1)} %get-tuple-element.39, pred[256,2048]{0,1:T(8,128)(4,1)S(1)} %broadcast_compare_fusion), kind=kLoop, calls=%fused_computation.2 | loop fusion | flops 16775168 | bytes 17317888 | tf_op jit(solution)/shard_map/reduce_sum | solution.py:78
  229.1 13.1 %fusion.25 = (bf16[8,256,2048]{1,2,0:T(8,128)(2,1)S(1)}, f32[8,256,2048]{1,2,0:T(8,128)}) fusion(f32[8,256]{1,0:T(8,128)S(1)} %log_add_fusion, f32[8,2048,256]{2,1,0:T(8,128)} %get-tuple-element.40, pred[256,2048]{0,1:T(8,128)(4,1)S(1)} %broadcast_compare_fusion), kind=kLoop, calls=%fused_computation.47 | loop fusion | flops 16777216 | bytes 42475520 | tf_op jit(solution)/shard_map/convert_element_type | solution.py:80
  245.9 5.5 %fusion.1 = bf16[4,256,2048]{1,2,0:T(8,128)(2,1)S(1)} fusion(f32[8,256,2048]{1,2,0:T(8,128)} %get-tuple-element.27, f32[4,256]{1,0:T(4,128)S(1)} %get-tuple-element.37, bf16[256,8,128]{0,2,1:T(8,128)(2,1)S(1)} %bitcast.87, bf16[2048,8,128]{0,2,1:T(8,128)(2,1)} %bitcast.70), kind=kOutput, calls=%fused_computation.5 | convolution fusion | flops 543162368 | bytes 15208448 | tf_op jit(solution)/shard_map/qhd,khd->hqk/dot_general | solution.py:106
  257.3 7.2 %convolution_convert_fusion = bf16[256,5120]{1,0:T(8,128)(2,1)S(1)} fusion(bf16[256,1024]{0,1:T(8,128)(2,1)S(1)} %bitcast.79, bf16[1024,5120]{1,0:T(8,128)(2,1)} %bitcast.68), kind=kOutput, calls=%fused_computation.8 | convolution fusion | flops 2685665280 | bytes 13631488 | tf_op jit(solution)/shard_map/dot_general | solution.py:86
  273.9 4.4 %fusion.2 = bf16[4,256,2048]{1,2,0:T(8,128)(2,1)S(1)} fusion(f32[8,256,2048]{1,2,0:T(8,128)} %get-tuple-element.27, f32[4,256]{1,0:T(4,128)S(1)} %get-tuple-element.38, bf16[256,8,128]{0,2,1:T(8,128)(2,1)S(1)} %bitcast.90, bf16[2048,8,128]{0,2,1:T(8,128)(2,1)S(1)} %bitcast.72), kind=kOutput, calls=%fused_computation.7 | convolution fusion | flops 543162368 | bytes 15208448 | tf_op jit(solution)/shard_map/qhd,khd->hqk/dot_general | solution.py:106
  284.7 41.4 %collective-permute-done.1 = bf16[256,1280]{1,0:T(8,128)(2,1)} collective-permute-done((bf16[256,1280]{1,0:T(8,128)(2,1)}, bf16[256,1280]{1,0:T(8,128)(2,1)}, u32[]{:S(2)}, u32[]{:S(2)}) %collective-permute-start.1) | collective-permute-done | bytes 655392 | tf_op jit(solution)/shard_map/ppermute | solution.py:55
  330.6 35.6 %all_to_all.19 = bf16[256,8,640]{0,2,1:T(8,128)(2,1)} all-to-all(bf16[256,8,640]{0,2,1:T(8,128)(2,1)S(1)} %bitcast.76), channel_id=1, replica_groups=mesh['seq'=8,'fsdp'=4] {'seq'}, dimensions={1} | all-to-all | bytes 5242880 | tf_op jit(solution)/shard_map/all_to_all | solution.py:95
  370.7 4.5 %convolution_bitcast_fusion = f32[256,4,128]{2,0,1:T(8,128)S(1)} fusion(bf16[2048,8,128]{0,2,1:T(8,128)(2,1)} %bitcast.74, bf16[4,256,2048]{1,2,0:T(8,128)(2,1)} %copy-done.10), kind=kOutput, calls=%fused_computation.29 | convolution fusion | flops 536870912 | bytes 8912896 | tf_op jit(solution)/shard_map/hqk,khd->qhd/dot_general | solution.py:113
  381.2 8.0 %fusion.30 = f32[1024,640]{1,0:T(8,128)} fusion(bf16[2048,1024]{0,1:T(8,128)(2,1)} %all-gather.5.cloned.1.call-done, bf16[2048,640]{1,0:T(8,128)(2,1)} %bitcast.91), kind=kOutput, calls=%fused_computation.52 | convolution fusion | flops 2684354560 | bytes 9437184 | tf_op jit(solution)/shard_map/th,td->hd/dot_general | solution.py:133
  389.2 14.1 %reduce-scatter.3.cloned.1.call-done = bf16[256,8,128]{2,0,1:T(8,128)(2,1)} async-done(((bf16[2048,8,128]{2,0,1:T(8,128)(2,1)}), bf16[256,8,128]{2,0,1:T(8,128)(2,1)}) %reduce-scatter.3.cloned.1.call-update) | async-done | bytes 524304 | tf_op jit(solution)/shard_map/reduce_scatter | solution.py:128
  (91 shorter events, 66.3 us)
Async XLA Ops:
  7.2 114.1 %all-gather.7.cloned.1.call-start = ((), (), s32[]{:S(2)}) async-start(), calls=%async_computation.6 | async-start | bytes 21233664 | tf_op jit(solution)/shard_map/all_gather | solution.py:67
  11.1 8.7 %copy-start.15 = (bf16[256,1280]{1,0:T(8,128)(2,1)S(1)}, bf16[256,1280]{1,0:T(8,128)(2,1)}, u32[]{:S(2)}) copy-start(bf16[256,1280]{1,0:T(8,128)(2,1)} %param.11) | copy-start | bytes 1966084
  11.4 16.5 %copy-start.17 = (s32[256]{0:T(256)S(1)}, s32[256]{0:T(256)}, u32[]{:S(2)}) copy-start(s32[256]{0:T(256)} %param.9) | copy-start | bytes 3076
  11.4 26.3 %copy-start.16 = (bf16[256,1024]{1,0:T(8,128)(2,1)S(1)}, bf16[256,1024]{1,0:T(8,128)(2,1)}, u32[]{:S(2)}) copy-start(bf16[256,1024]{1,0:T(8,128)(2,1)} %param.6) | copy-start | bytes 1572868
  19.8 309.1 %all-gather.5.cloned.1.call-start = ((), (), s32[]{:S(2)}) async-start(), calls=%async_computation.3 | async-start | bytes 4718592 | tf_op jit(solution)/shard_map/all_gather | solution.py:94
  20.9 21.1 %collective-permute-start.3 = (bf16[256,1280]{0,1:T(8,128)(2,1)}, bf16[256,1280]{0,1:T(8,128)(2,1)}, u32[]{:S(2)}, u32[]{:S(2)}) collective-permute-start(bf16[256,1280]{0,1:T(8,128)(2,1)} %copy.98), channel_id=1, source_target_pairs={{0,1},{1,2},{2,3},{3,0},{4,5},{5,6},{6,7},{7,4},{8,9},{9,10},{10,1... | collective-permute-start | bytes 1966088 | tf_op jit(solution)/shard_map/ppermute | solution.py:29
  24.0 45.3 %collective-permute-start.4 = (bf16[256,1280]{0,1:T(8,128)(2,1)}, bf16[256,1280]{0,1:T(8,128)(2,1)}, u32[]{:S(2)}, u32[]{:S(2)}) collective-permute-start(bf16[256,1280]{0,1:T(8,128)(2,1)} %copy.98), channel_id=1, source_target_pairs={{0,2},{1,3},{2,0},{3,1},{4,6},{5,7},{6,4},{7,5},{8,10},{9,11},{10,... | collective-permute-start | bytes 1966088 | tf_op jit(solution)/shard_map/ppermute | solution.py:29
  26.5 43.8 %collective-permute-start.5 = (bf16[256,1280]{0,1:T(8,128)(2,1)}, bf16[256,1280]{0,1:T(8,128)(2,1)}, u32[]{:S(2)}, u32[]{:S(2)}) collective-permute-start(bf16[256,1280]{0,1:T(8,128)(2,1)} %copy.98), channel_id=1, source_target_pairs={{0,3},{1,0},{2,1},{3,2},{4,7},{5,4},{6,5},{7,6},{8,11},{9,8},{10,9... | collective-permute-start | bytes 1966088 | tf_op jit(solution)/shard_map/ppermute | solution.py:29
  71.5 98.4 %copy-start.5 = (bf16[256,5120]{0,1:T(8,128)(2,1)}, bf16[256,5120]{0,1:T(8,128)(2,1)S(1)}, u32[]{:S(2)}) copy-start(bf16[256,5120]{0,1:T(8,128)(2,1)S(1)} %constant_dynamic-update-slice_fusion) | copy-start | bytes 7864324
  178.8 73.8 %copy-start.13 = (bf16[256,1024]{0,1:T(8,128)(2,1)}, bf16[256,1024]{0,1:T(8,128)(2,1)S(1)}, u32[]{:S(2)}) copy-start(bf16[256,1024]{0,1:T(8,128)(2,1)S(1)} %copy.102) | copy-start | bytes 1572868
  202.1 6.7 %copy-start.8 = (bf16[256,1024]{0,1:T(8,128)(2,1)S(1)}, bf16[256,1024]{0,1:T(8,128)(2,1)}, u32[]{:S(2)}) copy-start(bf16[256,1024]{0,1:T(8,128)(2,1)} %copy.94) | copy-start | bytes 1572868
  229.1 13.1 %copy-start.2 = (bf16[2048,1024]{0,1:T(8,128)(2,1)S(1)}, bf16[2048,1024]{0,1:T(8,128)(2,1)}, u32[]{:S(2)}) copy-start(bf16[2048,1024]{0,1:T(8,128)(2,1)} %copy.92) | copy-start | bytes 12582916
  242.2 3.4 copy-start
  245.6 134.4 %reduce-scatter.5.cloned.1.call-start = ((), (), s32[]{:S(2)}) async-start(), calls=%async_computation.5 | async-start | bytes 4718592 | tf_op jit(solution)/shard_map/reduce_scatter | solution.py:128
  245.9 6.8 %copy-start.1 = (bf16[8,256,2048]{1,2,0:T(8,128)(2,1)S(1)}, bf16[8,256,2048]{1,2,0:T(8,128)(2,1)}, u32[]{:S(2)}) copy-start(bf16[8,256,2048]{1,2,0:T(8,128)(2,1)} %copy-done) | copy-start | bytes 25165828
  256.3 146.9 %reduce-scatter.3.cloned.1.call-start = ((), (), s32[]{:S(2)}) async-start(), calls=%async_computation.4 | async-start | bytes 4718592 | tf_op jit(solution)/shard_map/reduce_scatter | solution.py:128
  257.3 12.9 %copy-start.14 = (bf16[256,1024]{0,1:T(8,128)(2,1)S(1)}, bf16[256,1024]{0,1:T(8,128)(2,1)}, u32[]{:S(2)}) copy-start(bf16[256,1024]{0,1:T(8,128)(2,1)} %copy-done.13) | copy-start | bytes 1572868
  265.8 18.9 %collective-permute-start.2 = (bf16[256,1280]{1,0:T(8,128)(2,1)}, bf16[256,1280]{1,0:T(8,128)(2,1)}, u32[]{:S(2)}, u32[]{:S(2)}) collective-permute-start(bf16[256,1280]{1,0:T(8,128)(2,1)} %get-tuple-element.31), channel_id=1, source_target_pairs={{0,3},{1,0},{2,1},{3,2},{4,7},{5,4},{6,5},{7,6},{8,11},{9,8},{10,9... | collective-permute-start | bytes 1966088 | tf_op jit(solution)/shard_map/ppermute | solution.py:55
  269.1 56.9 %collective-permute-start.1 = (bf16[256,1280]{1,0:T(8,128)(2,1)}, bf16[256,1280]{1,0:T(8,128)(2,1)}, u32[]{:S(2)}, u32[]{:S(2)}) collective-permute-start(bf16[256,1280]{1,0:T(8,128)(2,1)} %get-tuple-element.32), channel_id=1, source_target_pairs={{0,2},{1,3},{2,0},{3,1},{4,6},{5,7},{6,4},{7,5},{8,10},{9,11},{10,... | collective-permute-start | bytes 1966088 | tf_op jit(solution)/shard_map/ppermute | solution.py:55
  269.1 4.7 %copy-start.3 = (bf16[2048,1024]{0,1:T(8,128)(2,1)S(1)}, bf16[2048,1024]{0,1:T(8,128)(2,1)}, u32[]{:S(2)}) copy-start(bf16[2048,1024]{0,1:T(8,128)(2,1)} %copy.92) | copy-start | bytes 12582916
  269.1 56.9 %collective-permute-start = (bf16[256,1280]{1,0:T(8,128)(2,1)S(1)}, bf16[256,1280]{1,0:T(8,128)(2,1)}, u32[]{:S(2)}, u32[]{:S(2)}) collective-permute-start(bf16[256,1280]{1,0:T(8,128)(2,1)S(1)} %get-tuple-element.30), channel_id=1, source_target_pairs={{0,1},{1,2},{2,3},{3,0},{4,5},{5,6},{6,7},{7,4},{8,9},{9,10},{10,1... | collective-permute-start | bytes 1966088 | tf_op jit(solution)/shard_map/ppermute | solution.py:55
  273.9 4.5 %copy-start.9 = (bf16[256,1024]{0,1:T(8,128)(2,1)S(1)}, bf16[256,1024]{0,1:T(8,128)(2,1)}, u32[]{:S(2)}) copy-start(bf16[256,1024]{0,1:T(8,128)(2,1)} %copy.94) | copy-start | bytes 1572868
  370.7 4.5 %copy-start.4 = (bf16[2048,1024]{0,1:T(8,128)(2,1)S(1)}, bf16[2048,1024]{0,1:T(8,128)(2,1)}, u32[]{:S(2)}) copy-start(bf16[2048,1024]{0,1:T(8,128)(2,1)} %copy.93) | copy-start | bytes 12582916
  370.7 6.0 %copy-start.12 = (bf16[4,256,2048]{1,2,0:T(8,128)(2,1)S(1)}, bf16[4,256,2048]{1,2,0:T(8,128)(2,1)}, u32[]{:S(2)}) copy-start(bf16[4,256,2048]{1,2,0:T(8,128)(2,1)} %copy-done.11) | copy-start | bytes 12582916
  (4 other events, 7.3 us)
Sparse Core Ops, SparseCore 0:
  19.9 101.3 all-gather.6
  245.8 37.3 all-gather.4
  286.5 51.0 reduce-scatter.4
  340.8 62.3 reduce-scatter.2

commit v10 on v8

--- a/solution.py
+++ b/solution.py
@@ -44,6 +44,32 @@
     return full
 
 
+def pair_gather(block, axis, dim):
+    count = lax.axis_size(axis)
+    if count % 2:
+        return permute_gather(block, axis, dim)
+    me = lax.axis_index(axis)
+    mate = me + 1 - 2 * (me % 2)
+    chips = count // 2
+    width = block.shape[dim]
+    shape = list(block.shape)
+    shape[dim] = width * count
+    full = jnp.zeros(shape, block.dtype)
+    pair_route = [(i, i ^ 1) for i in range(count)]
+    for step in range(chips):
+        if step:
+            route = [(i, (i + 2 * step) % count) for i in range(count)]
+            piece = lax.ppermute(block, axis, route)
+        else:
+            piece = block
+        mate_piece = lax.ppermute(piece, axis, pair_route)
+        for source, part in (((me - 2 * step) % count, piece), ((mate - 2 * step) % count, mate_piece)):
+            start = [0] * block.ndim
+            start[dim] = source * width
+            full = lax.dynamic_update_slice(full, part, start)
+    return full
+
+
 def permute_sum_scatter(block, axis, dim):
     count = lax.axis_size(axis)
     me = lax.axis_index(axis)
@@ -87,7 +113,7 @@
     grad_attended = jnp.einsum(
         "td,hd->th", cotangent_full, weight_full, preferred_element_type=jnp.float32
     ).astype(jnp.bfloat16)
-    all_attended = lax.all_gather(attended_flat, "seq", axis=0, tiled=True)
+    all_attended = pair_gather(attended_flat, "seq", 0)
     cotangent_cols = lax.all_to_all(cotangent_full, "seq", 1, 0, tiled=True)
     grad_heads = split_heads(grad_attended)
     row_delta = jnp.sum(

time: 318 us -> 324 us (1.019)
  waiting for transfers between devices: 117 us -> 98.9 us
  local copies, waits for them, and re-layouts: 31.9 us -> 44.9 us
  blocking collectives: 44.5 us -> 55.7 us
  matrix products: 63.7 us -> 59.2 us
  starting transfers between devices: 11.6 us -> 15.1 us
    ppermute x3, waiting for transfers between devices: 43.5 us -> 24.1 us  [permute_sum_scatter(): total = total + lax.ppermute(piece, axis, route).astype(jnp.float32)]
    ppermute x0 -> x7, waiting for transfers between devices: none -> 13.5 us  [the longest x3 13.5 us: pair_gather(): piece = lax.ppermute(block, axis, route)]
    reduce_scatter x2, waiting for transfers between devices: 11.8 us -> 0.02 us  [shards(): lax.psum_scatter(both_parts, 'seq', scatter_dimension=0, tiled=True)]
    all_to_all x1, blocking collectives: 35.4 us -> 46.6 us  [shards(): cotangent_cols = lax.all_to_all(cotangent_full, 'seq', 1, 0, tiled=True)]
    dynamic_update_slice x0 -> x8, local copies, waits for them, and re-layouts: none -> 10.5 us  [pair_gather(): full = lax.dynamic_update_slice(full, part, start)]
    dot_general x2, matrix products: 9.73 us -> 6.09 us  [shards(): jnp.einsum('qhd,khd->hqk', half_grads, value_heads[:, heads], preferred_e...]
    ppermute x0 -> x7, starting transfers between devices: none -> 3.56 us  [the longest x3 2.67 us: pair_gather(): piece = lax.ppermute(block, axis, route)]
    unnamed x41 -> x55, local copies, waits for them, and re-layouts: 12.8 us -> 14.7 us
  transfers between devices with their start and end apart: 11 -> 17, of which waited for: 7 -> 6; matrix products, arithmetic and copies ran while one was open for 33% -> 31% of each run, Pallas kernels for 0% -> 0%
where the time goes in v10:
time: 324 us; the launch traced here: 323 us
  waiting for transfers between devices  98.9 us (31%)
  matrix products  59.2 us (18%)
  blocking collectives  55.7 us (17%)
  local copies, waits for them, and re-layouts  44.9 us (14%)
  other arithmetic  34.8 us (11%)
  starting transfers between devices  15.1 us (5%)
  between operations  14.5 us (4%)
    all_to_all x1, blocking collectives, shards(): cotangent_cols = lax.all_to_all(cotangent_full, 'seq', 1, 0, tiled=True)  46.6 us
    ppermute x3, waiting for transfers between devices, shift_pieces(): pieces.append(lax.ppermute(block, axis, route))  28.3 us
    all_gather x1, waiting for transfers between devices, shards(): weight_full = lax.all_gather(out_weight, 'seq', axis=1, tiled=True)  26 us
    ppermute x3, waiting for transfers between devices, permute_sum_scatter(): total = total + lax.ppermute(piece, axis, route).astype(jnp.float32)  24.1 us
    convert_element_type x1, other arithmetic, shards(): weights = probs.astype(jnp.bfloat16)  16.3 us
    unnamed x55, local copies, waits for them, and re-layouts  14.7 us
    ppermute x3, waiting for transfers between devices, pair_gather(): piece = lax.ppermute(block, axis, route)  13.5 us
    dynamic_update_slice x8, local copies, waits for them, and re-layouts, pair_gather(): full = lax.dynamic_update_slice(full, part, start)  10.5 us
  transfers between devices with their start and end apart: 17, of which 6 were waited for; matrix products, arithmetic and copies ran while one was open for 31% of the time, Pallas kernels for 0%

profile of v10, /device:TPU:0, one launch (start us, length us, event | category | flops | bytes accessed | tf_op | source)
XLA Modules:
  0.0 323.1 jit_solution(10133161042064272893)
XLA Ops:
  12.8 3.1 collective-permute-start.10
  15.8 2.6 collective-permute-start.11
  19.8 9.1 %all-gather = s32[8,1,256]{2,1,0:T(1,128)S(1)} all-gather(s32[1,1,256]{2,1,0:T(1,128)S(1)} %bitcast.88), channel_id=1, replica_groups=mesh['seq'=8,'fsdp'=4] {'seq'}, dimensions={0}, use_global_device_ids=true | all-gather | bytes 9216 | tf_op jit(solution)/shard_map/all_gather | solution.py:94
  35.0 26.1 %collective-permute-done.11 = bf16[256,1280]{0,1:T(8,128)(2,1)} collective-permute-done((bf16[256,1280]{0,1:T(8,128)(2,1)}, bf16[256,1280]{0,1:T(8,128)(2,1)}, u32[]{:S(2)}, u32[]{:S(2)}) %collective-permute-start.11) | collective-permute-done | bytes 655392 | tf_op jit(solution)/shard_map/ppermute | solution.py:29
  63.4 6.2 %all-gather.4.cloned.1.call-done = bf16[2048,2048]{0,1:T(8,128)(2,1)} async-done(((bf16[256,2048]{0,1:T(8,128)(2,1)}), bf16[2048,2048]{0,1:T(8,128)(2,1)}) %all-gather.4.cloned.1.call-update) | async-done | bytes 8388624 | tf_op jit(solution)/shard_map/all_gather | solution.py:91
  69.6 5.3 %fusion.26 = (bf16[2048,1024]{0,1:T(8,128)(2,1)S(1)}, bf16[2048,1024]{0,1:T(8,128)(2,1)}) fusion(bf16[2048,2048]{0,1:T(8,128)(2,1)} %all-gather.4.cloned.1.call-done), kind=kLoop, calls=%fused_computation.55 | loop fusion | bytes 16777216 | tf_op jit(solution)/shard_map/slice | solution.py:92
  75.0 8.1 %fusion = (f32[8,256]{1,0:T(8,128)S(1)}, f32[8,2048,256]{2,1,0:T(8,128)}) fusion(pred[256,2048]{0,1:T(8,128)(4,1)S(1)} %broadcast_compare_fusion, bf16[2048,8,128]{0,2,1:T(8,128)(2,1)S(1)} %bitcast.64, bf16[256,8,128]{0,2,1:T(8,128)(2,1)S(1)} %bitcast.75), kind=kOutput, calls=%fused_computation.3 | convolution fusion | flops 1086322688 | bytes 22028288 | tf_op jit(solution)/shard_map/qhd,khd->hqk/dot_general | solution.py:17
  83.1 9.2 %exponential_reduce_fusion = f32[8,256]{1,0:T(8,128)S(1)} fusion(f32[8,2048,256]{2,1,0:T(8,128)} %get-tuple-element.40, f32[8,256]{1,0:T(8,128)S(1)} %get-tuple-element.39, pred[256,2048]{0,1:T(8,128)(4,1)S(1)} %broadcast_compare_fusion), kind=kLoop, calls=%fused_computation.2 | loop fusion | flops 16775168 | bytes 17317888 | tf_op jit(solution)/shard_map/reduce_sum | solution.py:99
  92.3 16.3 %fusion.25 = (bf16[8,256,2048]{1,2,0:T(8,128)(2,1)}, f32[8,256,2048]{1,2,0:T(8,128)}) fusion(f32[8,256]{1,0:T(8,128)S(1)} %log_add_fusion, f32[8,2048,256]{2,1,0:T(8,128)} %get-tuple-element.40, pred[256,2048]{0,1:T(8,128)(4,1)S(1)} %broadcast_compare_fusion), kind=kLoop, calls=%fused_computation.54 | loop fusion | flops 16777216 | bytes 42475520 | tf_op jit(solution)/shard_map/convert_element_type | solution.py:101
  108.6 26.0 %all-gather.6.cloned.1.call-done = bf16[1024,5120]{1,0:T(8,128)(2,1)} async-done(((bf16[1024,640]{1,0:T(8,128)(2,1)}), bf16[1024,5120]{1,0:T(8,128)(2,1)}) %all-gather.6.cloned.1.call-update) | async-done | bytes 10485776 | tf_op jit(solution)/shard_map/all_gather | solution.py:107
  134.5 6.9 %convolution_convert_fusion.3 = bf16[256,1024]{1,0:T(8,128)(2,1)S(1)} fusion(bf16[256,5120]{0,1:T(8,128)(2,1)S(1)} %constant_dynamic-update-slice_fusion, bf16[1024,5120]{1,0:T(8,128)(2,1)} %all-gather.6.cloned.1.call-done), kind=kOutput, calls=%fused_computation.26 | convolution fusion | flops 2684616704 | bytes 13631488 | tf_op jit(solution)/shard_map/td,hd->th/dot_general | solution.py:113
  141.7 6.2 %multiply_reduce_fusion = (f32[256,8]{0,1:T(8,128)S(1)}, bf16[8,128,256]{2,1,0:T(8,128)(2,1)S(1)}) fusion(bf16[256,1024]{0,1:T(8,128)(2,1)S(1)} %copy.103, bf16[2048,8,128]{0,2,1:T(8,128)(2,1)} %bitcast.61, bf16[8,256,2048]{1,2,0:T(8,128)(2,1)} %get-tuple-element.26), kind=kOutput, calls=%fused_computation.34 | convolution fusion | flops 1075050496 | bytes 13639680 | tf_op jit(solution)/shard_map/hqk,khd->qhd/dot_general | solution.py:102
  147.9 5.6 %fusion.15 = bf16[2048,4,128]{2,0,1:T(8,128)(2,1)} fusion(bf16[256,8,128]{0,2,1:T(8,128)(2,1)S(1)} %bitcast.81, bf16[8,256,2048]{1,2,0:T(8,128)(2,1)} %get-tuple-element.26), kind=kOutput, calls=%fused_computation.21 | convolution fusion | flops 537919488 | bytes 6815744 | tf_op jit(solution)/shard_map/hqk,qhd->khd/dot_general | solution.py:142
  163.9 8.3 %convolution_convert_fusion = bf16[256,5120]{1,0:T(8,128)(2,1)S(1)} fusion(bf16[256,1024]{0,1:T(8,128)(2,1)S(1)} %bitcast.71, bf16[1024,5120]{1,0:T(8,128)(2,1)} %all-gather.6.cloned.1.call-done), kind=kOutput, calls=%fused_computation.8 | convolution fusion | flops 2685665280 | bytes 13631488 | tf_op jit(solution)/shard_map/dot_general | solution.py:108
  173.5 3.3 %collective-permute-start.2 = (bf16[256,1280]{1,0:T(8,128)(2,1)}, bf16[256,1280]{1,0:T(8,128)(2,1)}, u32[]{:S(2)}, u32[]{:S(2)}) collective-permute-start(bf16[256,1280]{1,0:T(8,128)(2,1)} %get-tuple-element.31), channel_id=1, source_target_pairs={{0,3},{1,0},{2,1},{3,2},{4,7},{5,4},{6,5},{7,6},{8,11},{9,8},{10,9... | collective-permute-start | bytes 1966088 | tf_op jit(solution)/shard_map/ppermute | solution.py:81
  179.2 4.5 %fusion.2 = bf16[4,256,2048]{1,2,0:T(8,128)(2,1)S(1)} fusion(f32[8,256,2048]{1,2,0:T(8,128)} %get-tuple-element.27, f32[4,256]{1,0:T(4,128)S(1)} %get-tuple-element.38, bf16[256,8,128]{0,2,1:T(8,128)(2,1)S(1)} %bitcast.84, bf16[2048,8,128]{0,2,1:T(8,128)(2,1)S(1)} %bitcast.63), kind=kOutput, calls=%fused_computation.7 | convolution fusion | flops 543162368 | bytes 15208448 | tf_op jit(solution)/shard_map/qhd,khd->hqk/dot_general | solution.py:128
  189.0 2.4 pad_maximum_fusion
  195.2 13.5 %collective-permute-done.6 = bf16[256,1024]{0,1:T(8,128)(2,1)} collective-permute-done((bf16[256,1024]{0,1:T(8,128)(2,1)S(1)}, bf16[256,1024]{0,1:T(8,128)(2,1)}, u32[]{:S(2)}, u32[]{:S(2)}) %collective-permute-start.6) | collective-permute-done | bytes 524320 | tf_op jit(solution)/shard_map/ppermute | solution.py:62
  209.3 24.1 %collective-permute-done.1 = bf16[256,1280]{1,0:T(8,128)(2,1)} collective-permute-done((bf16[256,1280]{1,0:T(8,128)(2,1)}, bf16[256,1280]{1,0:T(8,128)(2,1)}, u32[]{:S(2)}, u32[]{:S(2)}) %collective-permute-start.1) | collective-permute-done | bytes 655392 | tf_op jit(solution)/shard_map/ppermute | solution.py:81
  233.4 2.9 convert_add_fusion
  242.9 46.6 %all_to_all.19 = bf16[256,8,640]{0,2,1:T(8,128)(2,1)} all-to-all(bf16[256,8,640]{0,2,1:T(8,128)(2,1)S(1)} %bitcast.67), channel_id=1, replica_groups=mesh['seq'=8,'fsdp'=4] {'seq'}, dimensions={1} | all-to-all | bytes 5242880 | tf_op jit(solution)/shard_map/all_to_all | solution.py:117
  289.6 4.4 %copy.123 = bf16[8,256,640]{2,1,0:T(8,128)(2,1)} copy(bf16[8,256,640]{1,2,0:T(8,128)(2,1)} %bitcast.68) | data formatting | bytes 5242880 | tf_op jit(solution)/shard_map/all_to_all | solution.py:117
  294.0 4.7 %convolution_bitcast_fusion = f32[256,4,128]{2,0,1:T(8,128)S(1)} fusion(bf16[2048,8,128]{0,2,1:T(8,128)(2,1)} %bitcast.65, bf16[4,256,2048]{1,2,0:T(8,128)(2,1)} %copy-done.10), kind=kOutput, calls=%fused_computation.28 | convolution fusion | flops 536870912 | bytes 8912896 | tf_op jit(solution)/shard_map/hqk,khd->qhd/dot_general | solution.py:135
  302.9 7.9 %fusion.30 = f32[1024,640]{1,0:T(8,128)} fusion(bf16[2048,1024]{0,1:T(8,128)(2,1)} %constant_dynamic-update-slice_fusion.4, bf16[2048,640]{1,0:T(8,128)(2,1)} %bitcast.85), kind=kOutput, calls=%fused_computation.59 | convolution fusion | flops 2684354560 | bytes 9437184 | tf_op jit(solution)/shard_map/th,td->hd/dot_general | solution.py:155
  (119 shorter events, 55.3 us)
Async XLA Ops:
  7.2 12.6 %copy-start.21 = (s32[256]{0:T(256)S(1)}, s32[256]{0:T(256)}, u32[]{:S(2)}) copy-start(s32[256]{0:T(256)} %param.9) | copy-start | bytes 3076
  7.2 22.2 %copy-start.18 = (bf16[256,1024]{1,0:T(8,128)(2,1)S(1)}, bf16[256,1024]{1,0:T(8,128)(2,1)}, u32[]{:S(2)}) copy-start(bf16[256,1024]{1,0:T(8,128)(2,1)} %param.6) | copy-start | bytes 1572868
  7.2 62.4 %all-gather.4.cloned.1.call-start = ((), (), s32[]{:S(2)}) async-start(), calls=%async_computation.3 | async-start | bytes 9437184 | tf_op jit(solution)/shard_map/all_gather | solution.py:91
  10.9 123.7 %all-gather.6.cloned.1.call-start = ((), (), s32[]{:S(2)}) async-start(), calls=%async_computation.4 | async-start | bytes 11796480 | tf_op jit(solution)/shard_map/all_gather | solution.py:107
  11.6 299.2 %reduce-scatter.5.cloned.1.call-start = ((), (), s32[]{:S(2)}) async-start(), calls=%async_computation.6 | async-start | bytes 4718592 | tf_op jit(solution)/shard_map/reduce_scatter | solution.py:150
  12.8 21.1 %collective-permute-start.10 = (bf16[256,1280]{0,1:T(8,128)(2,1)}, bf16[256,1280]{0,1:T(8,128)(2,1)}, u32[]{:S(2)}, u32[]{:S(2)}) collective-permute-start(bf16[256,1280]{0,1:T(8,128)(2,1)} %copy.99), channel_id=1, source_target_pairs={{0,1},{1,2},{2,3},{3,0},{4,5},{5,6},{6,7},{7,4},{8,9},{9,10},{10,1... | collective-permute-start | bytes 1966088 | tf_op jit(solution)/shard_map/ppermute | solution.py:29
  15.8 45.3 %collective-permute-start.11 = (bf16[256,1280]{0,1:T(8,128)(2,1)}, bf16[256,1280]{0,1:T(8,128)(2,1)}, u32[]{:S(2)}, u32[]{:S(2)}) collective-permute-start(bf16[256,1280]{0,1:T(8,128)(2,1)} %copy.99), channel_id=1, source_target_pairs={{0,2},{1,3},{2,0},{3,1},{4,6},{5,7},{6,4},{7,5},{8,10},{9,11},{10,... | collective-permute-start | bytes 1966088 | tf_op jit(solution)/shard_map/ppermute | solution.py:29
  18.4 43.8 %collective-permute-start.12 = (bf16[256,1280]{0,1:T(8,128)(2,1)}, bf16[256,1280]{0,1:T(8,128)(2,1)}, u32[]{:S(2)}, u32[]{:S(2)}) collective-permute-start(bf16[256,1280]{0,1:T(8,128)(2,1)} %copy.99), channel_id=1, source_target_pairs={{0,3},{1,0},{2,1},{3,2},{4,7},{5,4},{6,5},{7,6},{8,11},{9,8},{10,9... | collective-permute-start | bytes 1966088 | tf_op jit(solution)/shard_map/ppermute | solution.py:29
  63.4 71.1 %copy-start.5 = (bf16[256,5120]{0,1:T(8,128)(2,1)}, bf16[256,5120]{0,1:T(8,128)(2,1)S(1)}, u32[]{:S(2)}) copy-start(bf16[256,5120]{0,1:T(8,128)(2,1)S(1)} %constant_dynamic-update-slice_fusion) | copy-start | bytes 7864324
  141.7 11.8 %copy-start.14 = (bf16[256,1024]{0,1:T(8,128)(2,1)}, bf16[256,1024]{0,1:T(8,128)(2,1)S(1)}, u32[]{:S(2)}) copy-start(bf16[256,1024]{0,1:T(8,128)(2,1)S(1)} %copy.103) | copy-start | bytes 1572868
  161.8 150.2 %reduce-scatter.3.cloned.1.call-start = ((), (), s32[]{:S(2)}) async-start(), calls=%async_computation.5 | async-start | bytes 4718592 | tf_op jit(solution)/shard_map/reduce_scatter | solution.py:150
  162.1 15.9 %slice-start = ((s8[8388608]{0:T(1024)(128)(4,1)}), s8[4194304]{0:T(1024)(128)(4,1)S(1)}, s32[]{:S(2)}) async-start(s8[8388608]{0:T(1024)(128)(4,1)} %bitcast.59), calls=%async_computation.7 | async-start | bytes 8388608
  162.1 15.9 %slice-start.1 = ((s8[8388608]{0:T(1024)(128)(4,1)}), s8[4194304]{0:T(1024)(128)(4,1)S(1)}, s32[]{:S(2)}) async-start(s8[8388608]{0:T(1024)(128)(4,1)} %bitcast.59), calls=%async_computation.8 | async-start | bytes 8388608
  162.1 15.8 %copy-start.15 = (bf16[256,1024]{0,1:T(8,128)(2,1)S(1)}, bf16[256,1024]{0,1:T(8,128)(2,1)}, u32[]{:S(2)}) copy-start(bf16[256,1024]{0,1:T(8,128)(2,1)} %copy-done.14) | copy-start | bytes 1572868
  162.1 23.7 %collective-permute-start.3 = (bf16[256,1024]{0,1:T(8,128)(2,1)S(1)}, bf16[256,1024]{0,1:T(8,128)(2,1)S(1)}, u32[]{:S(2)}, u32[]{:S(2)}) collective-permute-start(bf16[256,1024]{0,1:T(8,128)(2,1)S(1)} %bitcast.69), channel_id=1, source_target_pairs={{0,4},{4,0},{8,12},{12,8},{16,20},{20,16},{24,28},{28,24},{1,5},{5... | collective-permute-start | bytes 1572872 | tf_op jit(solution)/shard_map/ppermute | solution.py:65
  162.4 23.5 %collective-permute-start.4 = (bf16[256,1024]{0,1:T(8,128)(2,1)S(1)}, bf16[256,1024]{0,1:T(8,128)(2,1)S(1)}, u32[]{:S(2)}, u32[]{:S(2)}) collective-permute-start(bf16[256,1024]{0,1:T(8,128)(2,1)S(1)} %bitcast.70), channel_id=1, source_target_pairs={{0,8},{4,12},{8,16},{12,20},{16,24},{20,28},{24,0},{28,4},{1,9},{5... | collective-permute-start | bytes 1572872 | tf_op jit(solution)/shard_map/ppermute | solution.py:62
  173.5 35.7 %collective-permute-start.2 = (bf16[256,1280]{1,0:T(8,128)(2,1)}, bf16[256,1280]{1,0:T(8,128)(2,1)}, u32[]{:S(2)}, u32[]{:S(2)}) collective-permute-start(bf16[256,1280]{1,0:T(8,128)(2,1)} %get-tuple-element.31), channel_id=1, source_target_pairs={{0,3},{1,0},{2,1},{3,2},{4,7},{5,4},{6,5},{7,6},{8,11},{9,8},{10,9... | collective-permute-start | bytes 1966088 | tf_op jit(solution)/shard_map/ppermute | solution.py:81
  176.8 56.6 %collective-permute-start.1 = (bf16[256,1280]{1,0:T(8,128)(2,1)}, bf16[256,1280]{1,0:T(8,128)(2,1)}, u32[]{:S(2)}, u32[]{:S(2)}) collective-permute-start(bf16[256,1280]{1,0:T(8,128)(2,1)} %get-tuple-element.32), channel_id=1, source_target_pairs={{0,2},{1,3},{2,0},{3,1},{4,6},{5,7},{6,4},{7,5},{8,10},{9,11},{10,... | collective-permute-start | bytes 1966088 | tf_op jit(solution)/shard_map/ppermute | solution.py:81
  176.8 56.6 %collective-permute-start = (bf16[256,1280]{1,0:T(8,128)(2,1)}, bf16[256,1280]{1,0:T(8,128)(2,1)}, u32[]{:S(2)}, u32[]{:S(2)}) collective-permute-start(bf16[256,1280]{1,0:T(8,128)(2,1)} %get-tuple-element.30), channel_id=1, source_target_pairs={{0,1},{1,2},{2,3},{3,0},{4,5},{5,6},{6,7},{7,4},{8,9},{9,10},{10,1... | collective-permute-start | bytes 1966088 | tf_op jit(solution)/shard_map/ppermute | solution.py:81
  185.8 22.9 %collective-permute-start.6 = (bf16[256,1024]{0,1:T(8,128)(2,1)S(1)}, bf16[256,1024]{0,1:T(8,128)(2,1)}, u32[]{:S(2)}, u32[]{:S(2)}) collective-permute-start(bf16[256,1024]{0,1:T(8,128)(2,1)S(1)} %bitcast.73), channel_id=1, source_target_pairs={{0,16},{4,20},{8,24},{12,28},{16,0},{20,4},{24,8},{28,12},{1,17},{... | collective-permute-start | bytes 1572872 | tf_op jit(solution)/shard_map/ppermute | solution.py:62
  187.8 20.9 %collective-permute-start.8 = (bf16[256,1024]{0,1:T(8,128)(2,1)S(1)}, bf16[256,1024]{0,1:T(8,128)(2,1)}, u32[]{:S(2)}, u32[]{:S(2)}) collective-permute-start(bf16[256,1024]{0,1:T(8,128)(2,1)S(1)} %bitcast.74), channel_id=1, source_target_pairs={{0,24},{4,28},{8,0},{12,4},{16,8},{20,12},{24,16},{28,20},{1,25},{... | collective-permute-start | bytes 1572872 | tf_op jit(solution)/shard_map/ppermute | solution.py:62
  208.7 27.6 %collective-permute-start.5 = (bf16[256,1024]{0,1:T(8,128)(2,1)}, bf16[256,1024]{0,1:T(8,128)(2,1)S(1)}, u32[]{:S(2)}, u32[]{:S(2)}) collective-permute-start(bf16[256,1024]{0,1:T(8,128)(2,1)} %copy-done.19), channel_id=1, source_target_pairs={{0,4},{4,0},{8,12},{12,8},{16,20},{20,16},{24,28},{28,24},{1,5},{5... | collective-permute-start | bytes 1572872 | tf_op jit(solution)/shard_map/ppermute | solution.py:65
  208.7 30.5 %collective-permute-start.7 = (bf16[256,1024]{0,1:T(8,128)(2,1)}, bf16[256,1024]{0,1:T(8,128)(2,1)S(1)}, u32[]{:S(2)}, u32[]{:S(2)}) collective-permute-start(bf16[256,1024]{0,1:T(8,128)(2,1)} %collective-permute-done.6), channel_id=1, source_target_pairs={{0,4},{4,0},{8,12},{12,8},{16,20},{20,16},{24,28},{28,24},{1,5},{5... | collective-permute-start | bytes 1572872 | tf_op jit(solution)/shard_map/ppermute | solution.py:65
  209.2 32.8 %collective-permute-start.9 = (bf16[256,1024]{0,1:T(8,128)(2,1)}, bf16[256,1024]{0,1:T(8,128)(2,1)S(1)}, u32[]{:S(2)}, u32[]{:S(2)}) collective-permute-start(bf16[256,1024]{0,1:T(8,128)(2,1)} %collective-permute-done.8), channel_id=1, source_target_pairs={{0,4},{4,0},{8,12},{12,8},{16,20},{20,16},{24,28},{28,24},{1,5},{5... | collective-permute-start | bytes 1572872 | tf_op jit(solution)/shard_map/ppermute | solution.py:65
  (17 other events, 74.8 us)
Sparse Core Ops, SparseCore 0:
  11.0 58.5 all-gather.3
  71.5 62.9 all-gather.5
  161.9 72.8 reduce-scatter.4
  243.1 60.5 reduce-scatter.2

commit v11 on v10

--- a/solution.py
+++ b/solution.py
@@ -104,7 +104,7 @@
     )
     attended_heads = attended.astype(jnp.bfloat16)
     attended_flat = attended_heads.reshape(local_tokens, local_heads * HEAD_DIM)
-    weight_full = lax.all_gather(out_weight, "seq", axis=1, tiled=True)
+    weight_full = pair_gather(out_weight, "seq", 1)
     partial_sum = jnp.dot(attended_flat, weight_full, preferred_element_type=jnp.float32).astype(
         jnp.bfloat16
     )
@@ -113,7 +113,7 @@
     grad_attended = jnp.einsum(
         "td,hd->th", cotangent_full, weight_full, preferred_element_type=jnp.float32
     ).astype(jnp.bfloat16)
-    all_attended = pair_gather(attended_flat, "seq", 0)
+    all_attended = lax.all_gather(attended_flat, "seq", axis=0, tiled=True)
     cotangent_cols = lax.all_to_all(cotangent_full, "seq", 1, 0, tiled=True)
     grad_heads = split_heads(grad_attended)
     row_delta = jnp.sum(

time: 324 us -> 348 us (1.074)
  blocking collectives: 55.7 us -> 113 us
  waiting for transfers between devices: 98.9 us -> 62.2 us
  local copies, waits for them, and re-layouts: 44.9 us -> 52.6 us
  matrix products: 59.2 us -> 52.6 us
  starting transfers between devices: 15.1 us -> 20.5 us
    all_gather x1, blocking collectives: 9.09 us -> 74.1 us  [shards(): all_pos = lax.all_gather(positions, 'seq', axis=0, tiled=True)]
    all_gather x1, waiting for transfers between devices: 26 us -> 0.01 us  [shards(): all_attended = lax.all_gather(attended_flat, 'seq', axis=0, tiled=True)]
    ppermute x3, waiting for transfers between devices: 28.3 us -> 6.4 us  [shift_pieces(): pieces.append(lax.ppermute(block, axis, route))]
    ppermute x3, waiting for transfers between devices: 24.1 us -> 40.8 us  [permute_sum_scatter(): total = total + lax.ppermute(piece, axis, route).astype(jnp.float32)]
    reduce_scatter x2, waiting for transfers between devices: 0.02 us -> 14.9 us  [shards(): lax.psum_scatter(both_parts, 'seq', scatter_dimension=0, tiled=True)]
    ppermute x3, waiting for transfers between devices: 13.5 us -> 0.01 us  [pair_gather(): piece = lax.ppermute(block, axis, route)]
    all_to_all x1, blocking collectives: 46.6 us -> 39.2 us  [shards(): cotangent_cols = lax.all_to_all(cotangent_full, 'seq', 1, 0, tiled=True)]
    all_gather x1, waiting for transfers between devices: 6.21 us -> 0.02 us  [shards(): all_packed = lax.all_gather(packed, 'seq', axis=0, tiled=True)]
  transfers between devices with their start and end apart: 17 -> 17, of which waited for: 6 -> 4; matrix products, arithmetic and copies ran while one was open for 31% -> 23% of each run, Pallas kernels for 0% -> 0%
where the time goes in v11:
time: 348 us; the launch traced here: 347 us
  blocking collectives  113 us (32%)
  waiting for transfers between devices  62.2 us (18%)
  local copies, waits for them, and re-layouts  52.6 us (15%)
  matrix products  52.6 us (15%)
  other arithmetic  31.6 us (9%)
  starting transfers between devices  20.5 us (6%)
  between operations  14.3 us (4%)
    all_gather x1, blocking collectives, shards(): all_pos = lax.all_gather(positions, 'seq', axis=0, tiled=True)  74.1 us
    ppermute x3, waiting for transfers between devices, permute_sum_scatter(): total = total + lax.ppermute(piece, axis, route).astype(jnp.float32)  40.8 us
    all_to_all x1, blocking collectives, shards(): cotangent_cols = lax.all_to_all(cotangent_full, 'seq', 1, 0, tiled=True)  39.2 us
    unnamed x47, local copies, waits for them, and re-layouts  19.7 us
    reduce_scatter x2, waiting for transfers between devices, shards(): lax.psum_scatter(both_parts, 'seq', scatter_dimension=0, tiled=True)  14.9 us
    convert_element_type x1, other arithmetic, shards(): weights = probs.astype(jnp.bfloat16)  13.1 us
    dynamic_update_slice x8, local copies, waits for them, and re-layouts, pair_gather(): full = lax.dynamic_update_slice(full, part, start)  11.3 us
    dot_general x2, matrix products, shards(): jnp.einsum('qhd,khd->hqk', half_grads, value_heads[:, heads], preferred_e...  9.83 us
  transfers between devices with their start and end apart: 17, of which 4 were waited for; matrix products, arithmetic and copies ran while one was open for 23% of the time, Pallas kernels for 0%

profile of v11, /device:TPU:0, one launch (start us, length us, event | category | flops | bytes accessed | tf_op | source)
XLA Modules:
  0.0 347.2 jit_solution(14789964835539013769)
XLA Ops:
  10.9 3.0 collective-permute-start.1
  19.5 2.6 collective-permute-start.11
  22.1 74.1 %all-gather = s32[8,1,256]{2,1,0:T(1,128)S(1)} all-gather(s32[1,1,256]{2,1,0:T(1,128)S(1)} %bitcast.82), channel_id=1, replica_groups=mesh['seq'=8,'fsdp'=4] {'seq'}, dimensions={0}, use_global_device_ids=true | all-gather | bytes 9216 | tf_op jit(solution)/shard_map/all_gather | solution.py:94
  99.4 3.7 %collective-permute-start.12 = (bf16[256,1280]{0,1:T(8,128)(2,1)}, bf16[256,1280]{0,1:T(8,128)(2,1)}, u32[]{:S(2)}, u32[]{:S(2)}) collective-permute-start(bf16[256,1280]{0,1:T(8,128)(2,1)} %copy.99), channel_id=1, source_target_pairs={{0,3},{1,0},{2,1},{3,2},{4,7},{5,4},{6,5},{7,6},{8,11},{9,8},{10,9... | collective-permute-start | bytes 1966088 | tf_op jit(solution)/shard_map/ppermute | solution.py:29
  111.3 6.4 %collective-permute-done.12 = bf16[256,1280]{0,1:T(8,128)(2,1)} collective-permute-done((bf16[256,1280]{0,1:T(8,128)(2,1)}, bf16[256,1280]{0,1:T(8,128)(2,1)}, u32[]{:S(2)}, u32[]{:S(2)}) %collective-permute-start.12) | collective-permute-done | bytes 655392 | tf_op jit(solution)/shard_map/ppermute | solution.py:29
  128.3 3.9 %copy-done = bf16[1024,5120]{1,0:T(8,128)(2,1)} copy-done((bf16[1024,5120]{1,0:T(8,128)(2,1)}, bf16[1024,5120]{1,0:T(8,128)(2,1)S(1)}, u32[]{:S(2)}) %copy-start) | copy-done | bytes 10485784
  132.2 3.7 %convolution_convert_fusion.3 = bf16[256,1024]{1,0:T(8,128)(2,1)} fusion(bf16[256,5120]{0,1:T(8,128)(2,1)S(1)} %constant_dynamic-update-slice_fusion, bf16[1024,5120]{1,0:T(8,128)(2,1)S(1)} %constant_dynamic-update-slice_fusion.4), kind=kOutput, calls=%fused_computation.26 | convolution fusion | flops 2684616704 | bytes 13631488 | tf_op jit(solution)/shard_map/td,hd->th/dot_general | solution.py:113
  137.2 5.5 %fusion.26 = (bf16[2048,1024]{0,1:T(8,128)(2,1)S(1)}, bf16[2048,1024]{0,1:T(8,128)(2,1)}) fusion(bf16[2048,2048]{0,1:T(8,128)(2,1)} %all-gather.4.cloned.1.call-done), kind=kLoop, calls=%fused_computation.55 | loop fusion | bytes 16777216 | tf_op jit(solution)/shard_map/slice | solution.py:92
  142.8 7.5 %fusion = (f32[8,256]{1,0:T(8,128)S(1)}, f32[8,2048,256]{2,1,0:T(8,128)}) fusion(pred[256,2048]{0,1:T(8,128)(4,1)S(1)} %broadcast_compare_fusion, bf16[2048,8,128]{0,2,1:T(8,128)(2,1)S(1)} %bitcast.62, bf16[256,8,128]{0,2,1:T(8,128)(2,1)S(1)} %bitcast.69), kind=kOutput, calls=%fused_computation.3 | convolution fusion | flops 1086322688 | bytes 22028288 | tf_op jit(solution)/shard_map/qhd,khd->hqk/dot_general | solution.py:17
  150.3 9.2 %exponential_reduce_fusion = f32[8,256]{1,0:T(8,128)S(1)} fusion(f32[8,2048,256]{2,1,0:T(8,128)} %get-tuple-element.40, f32[8,256]{1,0:T(8,128)S(1)} %get-tuple-element.39, pred[256,2048]{0,1:T(8,128)(4,1)S(1)} %broadcast_compare_fusion), kind=kLoop, calls=%fused_computation.2 | loop fusion | flops 16775168 | bytes 17317888 | tf_op jit(solution)/shard_map/reduce_sum | solution.py:99
  159.5 13.1 %fusion.25 = (bf16[8,256,2048]{1,2,0:T(8,128)(2,1)S(1)}, f32[8,256,2048]{1,2,0:T(8,128)}) fusion(f32[8,256]{1,0:T(8,128)S(1)} %log_add_fusion, f32[8,2048,256]{2,1,0:T(8,128)} %get-tuple-element.40, pred[256,2048]{0,1:T(8,128)(4,1)S(1)} %broadcast_compare_fusion), kind=kLoop, calls=%fused_computation.54 | loop fusion | flops 16777216 | bytes 42475520 | tf_op jit(solution)/shard_map/convert_element_type | solution.py:101
  172.6 2.6 multiply_reduce_fusion
  176.3 5.5 %fusion.1 = bf16[4,256,2048]{1,2,0:T(8,128)(2,1)S(1)} fusion(f32[8,256,2048]{1,2,0:T(8,128)} %get-tuple-element.27, f32[4,256]{1,0:T(4,128)S(1)} %get-tuple-element.37, bf16[256,8,128]{0,2,1:T(8,128)(2,1)S(1)} %bitcast.75, bf16[2048,8,128]{0,2,1:T(8,128)(2,1)} %bitcast.59), kind=kOutput, calls=%fused_computation.5 | convolution fusion | flops 543162368 | bytes 15208448 | tf_op jit(solution)/shard_map/qhd,khd->hqk/dot_general | solution.py:128
  187.8 7.2 %convolution_convert_fusion = bf16[256,5120]{1,0:T(8,128)(2,1)S(1)} fusion(bf16[256,1024]{0,1:T(8,128)(2,1)S(1)} %bitcast.68, bf16[1024,5120]{1,0:T(8,128)(2,1)} %copy-done), kind=kOutput, calls=%fused_computation.8 | convolution fusion | flops 2685665280 | bytes 13631488 | tf_op jit(solution)/shard_map/dot_general | solution.py:108
  196.2 4.3 %collective-permute-start.9 = (bf16[256,1280]{1,0:T(8,128)(2,1)}, bf16[256,1280]{1,0:T(8,128)(2,1)}, u32[]{:S(2)}, u32[]{:S(2)}) collective-permute-start(bf16[256,1280]{1,0:T(8,128)(2,1)} %get-tuple-element.31), channel_id=1, source_target_pairs={{0,3},{1,0},{2,1},{3,2},{4,7},{5,4},{6,5},{7,6},{8,11},{9,8},{10,9... | collective-permute-start | bytes 1966088 | tf_op jit(solution)/shard_map/ppermute | solution.py:81
  201.1 3.9 %fusion.18 = bf16[2048,4,128]{2,0,1:T(8,128)(2,1)S(1)} fusion(bf16[256,8,128]{0,2,1:T(8,128)(2,1)S(1)} %bitcast.77, bf16[8,256,2048]{1,2,0:T(8,128)(2,1)} %copy-done.1), kind=kOutput, calls=%fused_computation.22 | convolution fusion | flops 537919488 | bytes 6815744 | tf_op jit(solution)/shard_map/hqk,qhd->khd/dot_general | solution.py:142
  205.0 4.3 %fusion.2 = bf16[4,256,2048]{1,2,0:T(8,128)(2,1)S(1)} fusion(f32[8,256,2048]{1,2,0:T(8,128)} %get-tuple-element.27, f32[4,256]{1,0:T(4,128)S(1)} %get-tuple-element.38, bf16[256,8,128]{0,2,1:T(8,128)(2,1)S(1)} %bitcast.78, bf16[2048,8,128]{0,2,1:T(8,128)(2,1)S(1)} %bitcast.61), kind=kOutput, calls=%fused_computation.7 | convolution fusion | flops 543162368 | bytes 15208448 | tf_op jit(solution)/shard_map/qhd,khd->hqk/dot_general | solution.py:128
  216.0 38.6 %collective-permute-done.8 = bf16[256,1280]{1,0:T(8,128)(2,1)} collective-permute-done((bf16[256,1280]{1,0:T(8,128)(2,1)}, bf16[256,1280]{1,0:T(8,128)(2,1)}, u32[]{:S(2)}, u32[]{:S(2)}) %collective-permute-start.8) | collective-permute-done | bytes 655392 | tf_op jit(solution)/shard_map/ppermute | solution.py:81
  254.6 2.8 convert_add_fusion
  259.2 39.2 %all_to_all.19 = bf16[256,8,640]{0,2,1:T(8,128)(2,1)} all-to-all(bf16[256,8,640]{0,2,1:T(8,128)(2,1)S(1)} %bitcast.65), channel_id=1, replica_groups=mesh['seq'=8,'fsdp'=4] {'seq'}, dimensions={1} | all-to-all | bytes 5242880 | tf_op jit(solution)/shard_map/all_to_all | solution.py:117
  298.4 4.4 %copy.123 = bf16[8,256,640]{2,1,0:T(8,128)(2,1)} copy(bf16[8,256,640]{1,2,0:T(8,128)(2,1)} %bitcast.66) | data formatting | bytes 5242880 | tf_op jit(solution)/shard_map/all_to_all | solution.py:117
  302.8 4.5 %convolution_bitcast_fusion = f32[256,4,128]{2,0,1:T(8,128)S(1)} fusion(bf16[2048,8,128]{0,2,1:T(8,128)(2,1)} %bitcast.63, bf16[4,256,2048]{1,2,0:T(8,128)(2,1)} %copy-done.12), kind=kOutput, calls=%fused_computation.28 | convolution fusion | flops 536870912 | bytes 8912896 | tf_op jit(solution)/shard_map/hqk,khd->qhd/dot_general | solution.py:135
  313.3 8.0 %fusion.30 = f32[1024,640]{1,0:T(8,128)} fusion(bf16[2048,1024]{0,1:T(8,128)(2,1)} %all-gather.6.cloned.1.call-done, bf16[2048,640]{1,0:T(8,128)(2,1)} %bitcast.79), kind=kOutput, calls=%fused_computation.59 | convolution fusion | flops 2684354560 | bytes 9437184 | tf_op jit(solution)/shard_map/th,td->hd/dot_general | solution.py:155
  321.2 14.9 %reduce-scatter.3.cloned.1.call-done = bf16[256,8,128]{2,0,1:T(8,128)(2,1)} async-done(((bf16[2048,8,128]{2,0,1:T(8,128)(2,1)}), bf16[256,8,128]{2,0,1:T(8,128)(2,1)}) %reduce-scatter.3.cloned.1.call-update) | async-done | bytes 524304 | tf_op jit(solution)/shard_map/reduce_scatter | solution.py:150
  (110 shorter events, 59.9 us)
Async XLA Ops:
  7.2 14.9 %copy-start.19 = (s32[256]{0:T(256)S(1)}, s32[256]{0:T(256)}, u32[]{:S(2)}) copy-start(s32[256]{0:T(256)} %param.9) | copy-start | bytes 3076
  7.2 130.0 %all-gather.4.cloned.1.call-start = ((), (), s32[]{:S(2)}) async-start(), calls=%async_computation.3 | async-start | bytes 9437184 | tf_op jit(solution)/shard_map/all_gather | solution.py:91
  10.8 246.6 %all-gather.6.cloned.1.call-start = ((), (), s32[]{:S(2)}) async-start(), calls=%async_computation.4 | async-start | bytes 4718592 | tf_op jit(solution)/shard_map/all_gather | solution.py:116
  10.9 86.7 %collective-permute-start.1 = (bf16[1024,640]{1,0:T(8,128)(2,1)}, bf16[1024,640]{1,0:T(8,128)(2,1)}, u32[]{:S(2)}, u32[]{:S(2)}) collective-permute-start(bf16[1024,640]{1,0:T(8,128)(2,1)} %param.10), channel_id=1, source_target_pairs={{0,8},{4,12},{8,16},{12,20},{16,24},{20,28},{24,0},{28,4},{1,9},{5... | collective-permute-start | bytes 3932168 | tf_op jit(solution)/shard_map/ppermute | solution.py:62
  15.0 81.3 %collective-permute-start.10 = (bf16[256,1280]{0,1:T(8,128)(2,1)}, bf16[256,1280]{0,1:T(8,128)(2,1)S(1)}, u32[]{:S(2)}, u32[]{:S(2)}) collective-permute-start(bf16[256,1280]{0,1:T(8,128)(2,1)} %copy.99), channel_id=1, source_target_pairs={{0,1},{1,2},{2,3},{3,0},{4,5},{5,6},{6,7},{7,4},{8,9},{9,10},{10,1... | collective-permute-start | bytes 1966088 | tf_op jit(solution)/shard_map/ppermute | solution.py:29
  16.6 91.8 %collective-permute-start.3 = (bf16[1024,640]{1,0:T(8,128)(2,1)}, bf16[1024,640]{1,0:T(8,128)(2,1)}, u32[]{:S(2)}, u32[]{:S(2)}) collective-permute-start(bf16[1024,640]{1,0:T(8,128)(2,1)} %param.10), channel_id=1, source_target_pairs={{0,16},{4,20},{8,24},{12,28},{16,0},{20,4},{24,8},{28,12},{1,17},{... | collective-permute-start | bytes 3932168 | tf_op jit(solution)/shard_map/ppermute | solution.py:62
  18.1 91.5 %collective-permute-start.5 = (bf16[1024,640]{1,0:T(8,128)(2,1)}, bf16[1024,640]{1,0:T(8,128)(2,1)}, u32[]{:S(2)}, u32[]{:S(2)}) collective-permute-start(bf16[1024,640]{1,0:T(8,128)(2,1)} %param.10), channel_id=1, source_target_pairs={{0,24},{4,28},{8,0},{12,4},{16,8},{20,12},{24,16},{28,20},{1,25},{... | collective-permute-start | bytes 3932168 | tf_op jit(solution)/shard_map/ppermute | solution.py:62
  19.5 79.8 %collective-permute-start.11 = (bf16[256,1280]{0,1:T(8,128)(2,1)}, bf16[256,1280]{0,1:T(8,128)(2,1)}, u32[]{:S(2)}, u32[]{:S(2)}) collective-permute-start(bf16[256,1280]{0,1:T(8,128)(2,1)} %copy.99), channel_id=1, source_target_pairs={{0,2},{1,3},{2,0},{3,1},{4,6},{5,7},{6,4},{7,5},{8,10},{9,11},{10,... | collective-permute-start | bytes 1966088 | tf_op jit(solution)/shard_map/ppermute | solution.py:29
  96.3 22.5 %collective-permute-start = (bf16[1024,640]{1,0:T(8,128)(2,1)}, bf16[1024,640]{1,0:T(8,128)(2,1)}, u32[]{:S(2)}, u32[]{:S(2)}) collective-permute-start(bf16[1024,640]{1,0:T(8,128)(2,1)} %param.10), channel_id=1, source_target_pairs={{0,4},{4,0},{8,12},{12,8},{16,20},{20,16},{24,28},{28,24},{1,5},{5... | collective-permute-start | bytes 3932168 | tf_op jit(solution)/shard_map/ppermute | solution.py:65
  97.6 25.4 %collective-permute-start.2 = (bf16[1024,640]{1,0:T(8,128)(2,1)}, bf16[1024,640]{1,0:T(8,128)(2,1)}, u32[]{:S(2)}, u32[]{:S(2)}) collective-permute-start(bf16[1024,640]{1,0:T(8,128)(2,1)} %collective-permute-done.1), channel_id=1, source_target_pairs={{0,4},{4,0},{8,12},{12,8},{16,20},{20,16},{24,28},{28,24},{1,5},{5... | collective-permute-start | bytes 3932168 | tf_op jit(solution)/shard_map/ppermute | solution.py:65
  99.4 18.3 %collective-permute-start.12 = (bf16[256,1280]{0,1:T(8,128)(2,1)}, bf16[256,1280]{0,1:T(8,128)(2,1)}, u32[]{:S(2)}, u32[]{:S(2)}) collective-permute-start(bf16[256,1280]{0,1:T(8,128)(2,1)} %copy.99), channel_id=1, source_target_pairs={{0,3},{1,0},{2,1},{3,2},{4,7},{5,4},{6,5},{7,6},{8,11},{9,8},{10,9... | collective-permute-start | bytes 1966088 | tf_op jit(solution)/shard_map/ppermute | solution.py:29
  108.3 17.8 %collective-permute-start.4 = (bf16[1024,640]{1,0:T(8,128)(2,1)}, bf16[1024,640]{1,0:T(8,128)(2,1)S(1)}, u32[]{:S(2)}, u32[]{:S(2)}) collective-permute-start(bf16[1024,640]{1,0:T(8,128)(2,1)} %collective-permute-done.3), channel_id=1, source_target_pairs={{0,4},{4,0},{8,12},{12,8},{16,20},{20,16},{24,28},{28,24},{1,5},{5... | collective-permute-start | bytes 3932168 | tf_op jit(solution)/shard_map/ppermute | solution.py:65
  109.6 18.4 %collective-permute-start.6 = (bf16[1024,640]{1,0:T(8,128)(2,1)}, bf16[1024,640]{1,0:T(8,128)(2,1)S(1)}, u32[]{:S(2)}, u32[]{:S(2)}) collective-permute-start(bf16[1024,640]{1,0:T(8,128)(2,1)} %collective-permute-done.5), channel_id=1, source_target_pairs={{0,4},{4,0},{8,12},{12,8},{16,20},{20,16},{24,28},{28,24},{1,5},{5... | collective-permute-start | bytes 3932168 | tf_op jit(solution)/shard_map/ppermute | solution.py:65
  118.8 9.5 %copy-start.7 = (bf16[256,5120]{0,1:T(8,128)(2,1)}, bf16[256,5120]{0,1:T(8,128)(2,1)S(1)}, u32[]{:S(2)}) copy-start(bf16[256,5120]{0,1:T(8,128)(2,1)S(1)} %constant_dynamic-update-slice_fusion) | copy-start | bytes 7864324
  137.2 45.9 %copy-start.15 = (bf16[256,1024]{0,1:T(8,128)(2,1)}, bf16[256,1024]{0,1:T(8,128)(2,1)S(1)}, u32[]{:S(2)}) copy-start(bf16[256,1024]{0,1:T(8,128)(2,1)S(1)} %copy.103) | copy-start | bytes 1572868
  142.7 7.5 %copy-start.5 = (bf16[2048,1024]{0,1:T(8,128)(2,1)}, bf16[2048,1024]{0,1:T(8,128)(2,1)S(1)}, u32[]{:S(2)}) copy-start(bf16[2048,1024]{0,1:T(8,128)(2,1)S(1)} %get-tuple-element.28) | copy-start | bytes 12582916
  159.5 13.1 %copy-start.3 = (bf16[2048,1024]{0,1:T(8,128)(2,1)S(1)}, bf16[2048,1024]{0,1:T(8,128)(2,1)}, u32[]{:S(2)}) copy-start(bf16[2048,1024]{0,1:T(8,128)(2,1)} %get-tuple-element.29) | copy-start | bytes 12582916
  176.0 136.1 %reduce-scatter.5.cloned.1.call-start = ((), (), s32[]{:S(2)}) async-start(), calls=%async_computation.6 | async-start | bytes 4718592 | tf_op jit(solution)/shard_map/reduce_scatter | solution.py:150
  176.3 6.8 %copy-start.2 = (bf16[8,256,2048]{1,2,0:T(8,128)(2,1)S(1)}, bf16[8,256,2048]{1,2,0:T(8,128)(2,1)}, u32[]{:S(2)}) copy-start(bf16[8,256,2048]{1,2,0:T(8,128)(2,1)} %copy-done.1) | copy-start | bytes 25165828
  186.7 149.4 %reduce-scatter.3.cloned.1.call-start = ((), (), s32[]{:S(2)}) async-start(), calls=%async_computation.5 | async-start | bytes 4718592 | tf_op jit(solution)/shard_map/reduce_scatter | solution.py:150
  187.8 13.3 %copy-start.16 = (bf16[256,1024]{0,1:T(8,128)(2,1)S(1)}, bf16[256,1024]{0,1:T(8,128)(2,1)}, u32[]{:S(2)}) copy-start(bf16[256,1024]{0,1:T(8,128)(2,1)} %copy-done.15) | copy-start | bytes 1572868
  196.2 19.7 %collective-permute-start.9 = (bf16[256,1280]{1,0:T(8,128)(2,1)}, bf16[256,1280]{1,0:T(8,128)(2,1)}, u32[]{:S(2)}, u32[]{:S(2)}) collective-permute-start(bf16[256,1280]{1,0:T(8,128)(2,1)} %get-tuple-element.31), channel_id=1, source_target_pairs={{0,3},{1,0},{2,1},{3,2},{4,7},{5,4},{6,5},{7,6},{8,11},{9,8},{10,9... | collective-permute-start | bytes 1966088 | tf_op jit(solution)/shard_map/ppermute | solution.py:81
  200.5 54.1 %collective-permute-start.8 = (bf16[256,1280]{1,0:T(8,128)(2,1)}, bf16[256,1280]{1,0:T(8,128)(2,1)}, u32[]{:S(2)}, u32[]{:S(2)}) collective-permute-start(bf16[256,1280]{1,0:T(8,128)(2,1)} %get-tuple-element.32), channel_id=1, source_target_pairs={{0,2},{1,3},{2,0},{3,1},{4,6},{5,7},{6,4},{7,5},{8,10},{9,11},{10,... | collective-permute-start | bytes 1966088 | tf_op jit(solution)/shard_map/ppermute | solution.py:81
  200.5 54.1 %collective-permute-start.7 = (bf16[256,1280]{1,0:T(8,128)(2,1)S(1)}, bf16[256,1280]{1,0:T(8,128)(2,1)}, u32[]{:S(2)}, u32[]{:S(2)}) collective-permute-start(bf16[256,1280]{1,0:T(8,128)(2,1)S(1)} %get-tuple-element.30), channel_id=1, source_target_pairs={{0,1},{1,2},{2,3},{3,0},{4,5},{5,6},{6,7},{7,4},{8,9},{9,10},{10,1... | collective-permute-start | bytes 1966088 | tf_op jit(solution)/shard_map/ppermute | solution.py:81
  (13 other events, 47.3 us)
Sparse Core Ops, SparseCore 0:
  11.0 98.3 all-gather.3
  176.1 39.8 all-gather.5
  219.4 55.4 reduce-scatter.4
  278.1 57.9 reduce-scatter.2

commit v12 on v8

--- a/solution.py
+++ b/solution.py
@@ -82,11 +82,12 @@
     partial_sum = jnp.dot(attended_flat, weight_full, preferred_element_type=jnp.float32).astype(
         jnp.bfloat16
     )
-    attn_output = permute_sum_scatter(partial_sum, "fsdp", 1)
     cotangent_full = permute_gather(cotangent, "fsdp", 1)
     grad_attended = jnp.einsum(
         "td,hd->th", cotangent_full, weight_full, preferred_element_type=jnp.float32
     ).astype(jnp.bfloat16)
+    partial_sum, grad_attended = lax.optimization_barrier((partial_sum, grad_attended))
+    attn_output = permute_sum_scatter(partial_sum, "fsdp", 1)
     all_attended = lax.all_gather(attended_flat, "seq", axis=0, tiled=True)
     cotangent_cols = lax.all_to_all(cotangent_full, "seq", 1, 0, tiled=True)
     grad_heads = split_heads(grad_attended)
@@ -118,9 +119,7 @@
         )
         both_parts = jnp.concatenate([key_part, value_part], axis=1).astype(jnp.bfloat16)
         if half == 0:
-            attn_output, all_attended, both_parts = lax.optimization_barrier(
-                (attn_output, all_attended, both_parts)
-            )
+            all_attended, both_parts = lax.optimization_barrier((all_attended, both_parts))
         both_sums = lax.psum_scatter(both_parts, "seq", scatter_dimension=0, tiled=True).astype(
             jnp.float32
         )

time: 318 us -> 347 us (1.091)
  waiting for transfers between devices: 117 us -> 173 us
  blocking collectives: 44.5 us -> 10.4 us
  starting transfers between devices: 11.6 us -> 27.3 us
  matrix products: 63.7 us -> 55.7 us
    all_to_all x0 -> x1, waiting for transfers between devices: none -> 43.4 us  [shards(): cotangent_cols = lax.all_to_all(cotangent_full, 'seq', 1, 0, tiled=True)]
    all_gather x1, waiting for transfers between devices: 6.21 us -> 46.8 us  [shards(): all_packed = lax.all_gather(packed, 'seq', axis=0, tiled=True)]
    all_to_all x1 -> x0, blocking collectives: 35.4 us -> none  [shards(): cotangent_cols = lax.all_to_all(cotangent_full, 'seq', 1, 0, tiled=True)]
    all_gather x1, waiting for transfers between devices: 25.9 us -> 0.01 us  [shards(): weight_full = lax.all_gather(out_weight, 'seq', axis=1, tiled=True)]
    ppermute x3, starting transfers between devices: 4.42 us -> 16.8 us  [permute_sum_scatter(): total = total + lax.ppermute(piece, axis, route).astype(jnp.float32)]
    reduce_scatter x2, waiting for transfers between devices: 11.8 us -> 0.02 us  [shards(): lax.psum_scatter(both_parts, 'seq', scatter_dimension=0, tiled=True)]
    ppermute x3, waiting for transfers between devices: 28.3 us -> 37.9 us  [shift_pieces(): pieces.append(lax.ppermute(block, axis, route))]
    all_to_all x0 -> x1, starting transfers between devices: none -> 4.4 us  [shards(): cotangent_cols = lax.all_to_all(cotangent_full, 'seq', 1, 0, tiled=True)]
  transfers between devices with their start and end apart: 11 -> 12, of which waited for: 7 -> 6; matrix products, arithmetic and copies ran while one was open for 33% -> 32% of each run, Pallas kernels for 0% -> 0%
where the time goes in v12:
time: 347 us; the launch traced here: 345 us
  waiting for transfers between devices  173 us (50%)
  matrix products  55.7 us (16%)
  other arithmetic  34.7 us (10%)
  local copies, waits for them, and re-layouts  30.4 us (9%)
  starting transfers between devices  27.3 us (8%)
  between operations  14.2 us (4%)
  blocking collectives  10.4 us (3%)
    all_gather x1, waiting for transfers between devices, shards(): all_packed = lax.all_gather(packed, 'seq', axis=0, tiled=True)  46.8 us
    ppermute x3, waiting for transfers between devices, permute_sum_scatter(): total = total + lax.ppermute(piece, axis, route).astype(jnp.float32)  43.7 us
    all_to_all x1, waiting for transfers between devices, shards(): cotangent_cols = lax.all_to_all(cotangent_full, 'seq', 1, 0, tiled=True)  43.4 us
    ppermute x3, waiting for transfers between devices, shift_pieces(): pieces.append(lax.ppermute(block, axis, route))  37.9 us
    ppermute x3, starting transfers between devices, permute_sum_scatter(): total = total + lax.ppermute(piece, axis, route).astype(jnp.float32)  16.8 us
    convert_element_type x1, other arithmetic, shards(): weights = probs.astype(jnp.bfloat16)  13.8 us
    dot_general x2, matrix products, shards(): jnp.einsum('qhd,khd->hqk', half_grads, value_heads[:, heads], preferred_e...  11 us
    all_gather x1, blocking collectives, shards(): all_pos = lax.all_gather(positions, 'seq', axis=0, tiled=True)  10.4 us
  transfers between devices with their start and end apart: 12, of which 6 were waited for; matrix products, arithmetic and copies ran while one was open for 32% of the time, Pallas kernels for 0%

profile of v12, /device:TPU:0, one launch (start us, length us, event | category | flops | bytes accessed | tf_op | source)
XLA Modules:
  0.0 345.3 jit_solution(961239113615317251)
XLA Ops:
  11.9 10.4 %all-gather = s32[8,1,256]{2,1,0:T(1,128)S(1)} all-gather(s32[1,1,256]{2,1,0:T(1,128)S(1)} %bitcast.82), channel_id=1, replica_groups=mesh['seq'=8,'fsdp'=4] {'seq'}, dimensions={0}, use_global_device_ids=true | all-gather | bytes 9216 | tf_op jit(solution)/shard_map/all_gather | solution.py:68
  22.7 46.8 %all-gather.5.cloned.1.call-done = bf16[2048,2048]{0,1:T(8,128)(2,1)} async-done(((bf16[256,2048]{0,1:T(8,128)(2,1)}), bf16[2048,2048]{0,1:T(8,128)(2,1)}) %all-gather.5.cloned.1.call-update) | async-done | bytes 8388624 | tf_op jit(solution)/shard_map/all_gather | solution.py:65
  69.6 5.2 %fusion.26 = (bf16[2048,1024]{0,1:T(8,128)(2,1)S(1)}, bf16[2048,1024]{0,1:T(8,128)(2,1)}) fusion(bf16[2048,2048]{0,1:T(8,128)(2,1)} %all-gather.5.cloned.1.call-done), kind=kLoop, calls=%fused_computation.47 | loop fusion | bytes 16777216 | tf_op jit(solution)/shard_map/slice | solution.py:66
  74.8 8.1 %fusion = (f32[8,256]{1,0:T(8,128)S(1)}, f32[8,2048,256]{2,1,0:T(8,128)}) fusion(pred[256,2048]{0,1:T(8,128)(4,1)S(1)} %broadcast_compare_fusion, bf16[2048,8,128]{0,2,1:T(8,128)(2,1)S(1)} %bitcast.64, bf16[256,8,128]{0,2,1:T(8,128)(2,1)S(1)} %bitcast.69), kind=kOutput, calls=%fused_computation.3 | convolution fusion | flops 1086322688 | bytes 22028288 | tf_op jit(solution)/shard_map/qhd,khd->hqk/dot_general | solution.py:17
  82.9 9.2 %exponential_reduce_fusion = f32[8,256]{1,0:T(8,128)S(1)} fusion(f32[8,2048,256]{2,1,0:T(8,128)} %get-tuple-element.47, f32[8,256]{1,0:T(8,128)S(1)} %get-tuple-element.46, pred[256,2048]{0,1:T(8,128)(4,1)S(1)} %broadcast_compare_fusion), kind=kLoop, calls=%fused_computation.2 | loop fusion | flops 16775168 | bytes 17317888 | tf_op jit(solution)/shard_map/reduce_sum | solution.py:73
  92.1 13.8 %fusion.25 = (bf16[8,256,2048]{1,2,0:T(8,128)(2,1)S(1)}, f32[8,256,2048]{1,2,0:T(8,128)}) fusion(f32[8,256]{1,0:T(8,128)S(1)} %log_add_fusion, f32[8,2048,256]{2,1,0:T(8,128)} %get-tuple-element.47, pred[256,2048]{0,1:T(8,128)(4,1)S(1)} %broadcast_compare_fusion), kind=kLoop, calls=%fused_computation.46 | loop fusion | flops 16777216 | bytes 42475520 | tf_op jit(solution)/shard_map/convert_element_type | solution.py:75
  106.0 2.6 convolution_convert_fusion.4
  118.0 11.3 %collective-permute-done = bf16[256,1280]{0,1:T(8,128)(2,1)S(1)} collective-permute-done((bf16[256,1280]{0,1:T(8,128)(2,1)S(1)}, bf16[256,1280]{0,1:T(8,128)(2,1)S(1)}, u32[]{:S(2)}, u32[]{:S(2)}) %collective-permute-start) | collective-permute-done | bytes 655392 | tf_op jit(solution)/shard_map/ppermute | solution.py:29
  130.2 26.6 %collective-permute-done.1 = bf16[256,1280]{0,1:T(8,128)(2,1)S(1)} collective-permute-done((bf16[256,1280]{0,1:T(8,128)(2,1)S(1)}, bf16[256,1280]{0,1:T(8,128)(2,1)S(1)}, u32[]{:S(2)}, u32[]{:S(2)}) %collective-permute-start.1) | collective-permute-done | bytes 655392 | tf_op jit(solution)/shard_map/ppermute | solution.py:29
  158.6 7.5 %convolution_convert_fusion = bf16[256,5120]{1,0:T(8,128)(2,1)S(1)} fusion(bf16[256,1024]{0,1:T(8,128)(2,1)S(1)} %bitcast.68, bf16[1024,5120]{1,0:T(8,128)(2,1)} %all-gather.7.cloned.1.call-done), kind=kOutput, calls=%fused_computation.8 | convolution fusion | flops 2685665280 | bytes 13631488 | tf_op jit(solution)/shard_map/dot_general | solution.py:82
  166.1 5.6 %convolution_convert_fusion.3 = bf16[256,1024]{1,0:T(8,128)(2,1)} fusion(bf16[256,5120]{0,1:T(8,128)(2,1)} %constant_dynamic-update-slice_fusion, bf16[1024,5120]{1,0:T(8,128)(2,1)S(1)} %copy-done.4), kind=kOutput, calls=%fused_computation.26 | convolution fusion | flops 2684616704 | bytes 13631488 | tf_op jit(solution)/shard_map/td,hd->th/dot_general | solution.py:86
  175.2 5.6 %fusion.1 = bf16[4,256,2048]{1,2,0:T(8,128)(2,1)S(1)} fusion(f32[8,256,2048]{1,2,0:T(8,128)} %get-tuple-element.34, f32[4,256]{1,0:T(4,128)S(1)} %get-tuple-element.45, bf16[256,8,128]{0,2,1:T(8,128)(2,1)} %bitcast.76, bf16[2048,8,128]{0,2,1:T(8,128)(2,1)} %bitcast.61), kind=kOutput, calls=%fused_computation.5 | convolution fusion | flops 543162368 | bytes 15208448 | tf_op jit(solution)/shard_map/qhd,khd->hqk/dot_general | solution.py:103
  186.4 5.4 %fusion.2 = bf16[4,256,2048]{1,2,0:T(8,128)(2,1)S(1)} fusion(f32[8,256,2048]{1,2,0:T(8,128)} %get-tuple-element.34, f32[4,256]{1,0:T(4,128)S(1)} %get-tuple-element.44, bf16[256,8,128]{0,2,1:T(8,128)(2,1)} %bitcast.77, bf16[2048,8,128]{0,2,1:T(8,128)(2,1)} %bitcast.62), kind=kOutput, calls=%fused_computation.7 | convolution fusion | flops 543162368 | bytes 15208448 | tf_op jit(solution)/shard_map/qhd,khd->hqk/dot_general | solution.py:103
  193.4 3.7 %fusion.18 = bf16[2048,4,128]{0,2,1:T(8,128)(2,1)S(1)} fusion(bf16[256,8,128]{0,2,1:T(8,128)(2,1)S(1)} %bitcast.79, bf16[8,256,2048]{1,2,0:T(8,128)(2,1)} %copy-done), kind=kOutput, calls=%fused_computation.22 | convolution fusion | flops 537919488 | bytes 6815744 | tf_op jit(solution)/shard_map/hqk,qhd->khd/dot_general | solution.py:117
  199.6 4.4 %all-to-all-start = ((bf16[256,8,640]{0,2,1:T(8,128)(2,1)}), bf16[256,8,640]{0,2,1:T(8,128)(2,1)}, u32[]{:S(2)}, u32[]{:S(2)}) async-start(bf16[256,8,640]{0,2,1:T(8,128)(2,1)} %bitcast.20), calls=%async_computation.2 | async-start | bytes 5242880 | tf_op jit(solution)/shard_map/all_to_all | solution.py:92
  204.0 43.4 %all-to-all-done = bf16[256,8,640]{0,2,1:T(8,128)(2,1)} async-done(((bf16[256,8,640]{0,2,1:T(8,128)(2,1)}), bf16[256,8,640]{0,2,1:T(8,128)(2,1)}, u32[]{:S(2)}, u32[]{:S(2)}) %all-to-all-start) | async-done | bytes 2621472 | tf_op jit(solution)/shard_map/all_to_all | solution.py:92
  247.5 4.4 %copy.109 = bf16[8,256,640]{2,1,0:T(8,128)(2,1)} copy(bf16[8,256,640]{1,2,0:T(8,128)(2,1)} %bitcast.21) | data formatting | bytes 5242880 | tf_op jit(solution)/shard_map/all_to_all | solution.py:92
  253.2 16.2 %collective-permute-start.5 = (bf16[256,1280]{1,0:T(8,128)(2,1)}, bf16[256,1280]{1,0:T(8,128)(2,1)}, u32[]{:S(2)}, u32[]{:S(2)}) collective-permute-start(bf16[256,1280]{1,0:T(8,128)(2,1)} %get-tuple-element.38), channel_id=1, source_target_pairs={{0,3},{1,0},{2,1},{3,2},{4,7},{5,4},{6,5},{7,6},{8,11},{9,8},{10,9... | collective-permute-start | bytes 1966088 | tf_op jit(solution)/shard_map/ppermute | solution.py:55
  270.0 3.9 %convolution_bitcast_fusion = f32[256,4,128]{0,2,1:T(8,128)S(1)} fusion(bf16[2048,8,128]{0,2,1:T(8,128)(2,1)} %bitcast.65, bf16[4,256,2048]{1,2,0:T(8,128)(2,1)} %copy-done.8), kind=kOutput, calls=%fused_computation.28 | convolution fusion | flops 536870912 | bytes 8912896 | tf_op jit(solution)/shard_map/hqk,khd->qhd/dot_general | solution.py:110
  276.7 2.5 copy.110
  279.2 5.7 %collective-permute-done.5 = bf16[256,1280]{1,0:T(8,128)(2,1)} collective-permute-done((bf16[256,1280]{1,0:T(8,128)(2,1)}, bf16[256,1280]{1,0:T(8,128)(2,1)}, u32[]{:S(2)}, u32[]{:S(2)}) %collective-permute-start.5) | collective-permute-done | bytes 655392 | tf_op jit(solution)/shard_map/ppermute | solution.py:55
  284.9 38.0 %collective-permute-done.4 = bf16[256,1280]{1,0:T(8,128)(2,1)} collective-permute-done((bf16[256,1280]{1,0:T(8,128)(2,1)}, bf16[256,1280]{1,0:T(8,128)(2,1)}, u32[]{:S(2)}, u32[]{:S(2)}) %collective-permute-start.4) | collective-permute-done | bytes 655392 | tf_op jit(solution)/shard_map/ppermute | solution.py:55
  322.9 2.9 convert_add_fusion
  325.7 8.0 %fusion.30 = f32[1024,640]{1,0:T(8,128)} fusion(bf16[2048,1024]{0,1:T(8,128)(2,1)} %all-gather.9.cloned.1.call-done, bf16[2048,640]{1,0:T(8,128)(2,1)} %bitcast.75), kind=kOutput, calls=%fused_computation.51 | convolution fusion | flops 2684354560 | bytes 9437184 | tf_op jit(solution)/shard_map/th,td->hd/dot_general | solution.py:128
  (86 shorter events, 39.8 us)
Async XLA Ops:
  7.2 4.7 %copy-start.15 = (s32[256]{0:T(256)S(1)}, s32[256]{0:T(256)}, u32[]{:S(2)}) copy-start(s32[256]{0:T(256)} %param.9) | copy-start | bytes 3076
  7.2 62.4 %all-gather.5.cloned.1.call-start = ((), (), s32[]{:S(2)}) async-start(), calls=%async_computation.3 | async-start | bytes 9437184 | tf_op jit(solution)/shard_map/all_gather | solution.py:65
  10.8 147.7 %all-gather.7.cloned.1.call-start = ((), (), s32[]{:S(2)}) async-start(), calls=%async_computation.4 | async-start | bytes 11796480 | tf_op jit(solution)/shard_map/all_gather | solution.py:81
  11.6 188.0 %all-gather.9.cloned.1.call-start = ((), (), s32[]{:S(2)}) async-start(), calls=%async_computation.5 | async-start | bytes 4718592 | tf_op jit(solution)/shard_map/all_gather | solution.py:91
  11.9 62.9 %copy-start.6 = (bf16[256,1024]{0,1:T(8,128)(2,1)}, bf16[256,1024]{0,1:T(8,128)(2,1)S(1)}, u32[]{:S(2)}) copy-start(bf16[256,1024]{0,1:T(8,128)(2,1)S(1)} %copy.86) | copy-start | bytes 1572868
  74.8 8.2 %copy-start.2 = (bf16[2048,1024]{0,1:T(8,128)(2,1)}, bf16[2048,1024]{0,1:T(8,128)(2,1)S(1)}, u32[]{:S(2)}) copy-start(bf16[2048,1024]{0,1:T(8,128)(2,1)S(1)} %get-tuple-element.35) | copy-start | bytes 12582916
  92.1 13.8 %copy-start.1 = (bf16[2048,1024]{0,1:T(8,128)(2,1)S(1)}, bf16[2048,1024]{0,1:T(8,128)(2,1)}, u32[]{:S(2)}) copy-start(bf16[2048,1024]{0,1:T(8,128)(2,1)} %get-tuple-element.36) | copy-start | bytes 12582916
  109.4 224.2 %reduce-scatter.5.cloned.1.call-start = ((), (), s32[]{:S(2)}) async-start(), calls=%async_computation.7 | async-start | bytes 4718592 | tf_op jit(solution)/shard_map/reduce_scatter | solution.py:123
  109.7 48.8 %copy-start.5 = (bf16[8,128,256]{2,1,0:T(8,128)(2,1)S(1)}, bf16[8,128,256]{2,1,0:T(8,128)(2,1)}, u32[]{:S(2)}) copy-start(bf16[8,128,256]{2,1,0:T(8,128)(2,1)} %convolution_convert_fusion.4) | copy-start | bytes 1572868
  109.7 19.6 %collective-permute-start = (bf16[256,1280]{0,1:T(8,128)(2,1)S(1)}, bf16[256,1280]{0,1:T(8,128)(2,1)S(1)}, u32[]{:S(2)}, u32[]{:S(2)}) collective-permute-start(bf16[256,1280]{0,1:T(8,128)(2,1)S(1)} %copy.90), channel_id=1, source_target_pairs={{0,1},{1,2},{2,3},{3,0},{4,5},{5,6},{6,7},{7,4},{8,9},{9,10},{10,1... | collective-permute-start | bytes 1966088 | tf_op jit(solution)/shard_map/ppermute | solution.py:29
  111.6 45.2 %collective-permute-start.1 = (bf16[256,1280]{0,1:T(8,128)(2,1)S(1)}, bf16[256,1280]{0,1:T(8,128)(2,1)S(1)}, u32[]{:S(2)}, u32[]{:S(2)}) collective-permute-start(bf16[256,1280]{0,1:T(8,128)(2,1)S(1)} %copy.90), channel_id=1, source_target_pairs={{0,2},{1,3},{2,0},{3,1},{4,6},{5,7},{6,4},{7,5},{8,10},{9,11},{10,... | collective-permute-start | bytes 1966088 | tf_op jit(solution)/shard_map/ppermute | solution.py:29
  114.0 43.6 %collective-permute-start.2 = (bf16[256,1280]{0,1:T(8,128)(2,1)S(1)}, bf16[256,1280]{0,1:T(8,128)(2,1)S(1)}, u32[]{:S(2)}, u32[]{:S(2)}) collective-permute-start(bf16[256,1280]{0,1:T(8,128)(2,1)S(1)} %copy.90), channel_id=1, source_target_pairs={{0,3},{1,0},{2,1},{3,2},{4,7},{5,4},{6,5},{7,6},{8,11},{9,8},{10,9... | collective-permute-start | bytes 1966088 | tf_op jit(solution)/shard_map/ppermute | solution.py:29
  158.5 7.6 %copy-start.4 = (bf16[1024,5120]{1,0:T(8,128)(2,1)S(1)}, bf16[1024,5120]{1,0:T(8,128)(2,1)}, u32[]{:S(2)}) copy-start(bf16[1024,5120]{1,0:T(8,128)(2,1)} %all-gather.7.cloned.1.call-done) | copy-start | bytes 31457284
  173.8 8.5 %slice-start = ((s8[8388608]{0:T(1024)(128)(4,1)}), s8[4194304]{0:T(1024)(128)(4,1)S(1)}, s32[]{:S(2)}) async-start(s8[8388608]{0:T(1024)(128)(4,1)} %bitcast.59), calls=%async_computation.8 | async-start | bytes 8388608
  175.1 5.6 %copy-start.7 = (bf16[256,1024]{0,1:T(8,128)(2,1)S(1)}, bf16[256,1024]{0,1:T(8,128)(2,1)}, u32[]{:S(2)}) copy-start(bf16[256,1024]{0,1:T(8,128)(2,1)} %copy-done.6) | copy-start | bytes 1572868
  175.2 7.1 %slice-start.1 = ((s8[8388608]{0:T(1024)(128)(4,1)}), s8[4194304]{0:T(1024)(128)(4,1)S(1)}, s32[]{:S(2)}) async-start(s8[8388608]{0:T(1024)(128)(4,1)} %bitcast.59), calls=%async_computation.9 | async-start | bytes 8388608
  186.2 148.7 %reduce-scatter.3.cloned.1.call-start = ((), (), s32[]{:S(2)}) async-start(), calls=%async_computation.6 | async-start | bytes 4718592 | tf_op jit(solution)/shard_map/reduce_scatter | solution.py:123
  191.9 5.3 %copy-start.9 = (bf16[4,256,2048]{1,2,0:T(8,128)(2,1)}, bf16[4,256,2048]{1,2,0:T(8,128)(2,1)S(1)}, u32[]{:S(2)}) copy-start(bf16[4,256,2048]{1,2,0:T(8,128)(2,1)S(1)} %fusion.2) | copy-start | bytes 12582916
  199.6 47.9 %all-to-all-start = ((bf16[256,8,640]{0,2,1:T(8,128)(2,1)}), bf16[256,8,640]{0,2,1:T(8,128)(2,1)}, u32[]{:S(2)}, u32[]{:S(2)}) async-start(bf16[256,8,640]{0,2,1:T(8,128)(2,1)} %bitcast.20), calls=%async_computation.2 | async-start | bytes 5242880 | tf_op jit(solution)/shard_map/all_to_all | solution.py:92
  253.2 31.7 %collective-permute-start.5 = (bf16[256,1280]{1,0:T(8,128)(2,1)}, bf16[256,1280]{1,0:T(8,128)(2,1)}, u32[]{:S(2)}, u32[]{:S(2)}) collective-permute-start(bf16[256,1280]{1,0:T(8,128)(2,1)} %get-tuple-element.38), channel_id=1, source_target_pairs={{0,3},{1,0},{2,1},{3,2},{4,7},{5,4},{6,5},{7,6},{8,11},{9,8},{10,9... | collective-permute-start | bytes 1966088 | tf_op jit(solution)/shard_map/ppermute | solution.py:55
  269.4 53.4 %collective-permute-start.4 = (bf16[256,1280]{1,0:T(8,128)(2,1)}, bf16[256,1280]{1,0:T(8,128)(2,1)}, u32[]{:S(2)}, u32[]{:S(2)}) collective-permute-start(bf16[256,1280]{1,0:T(8,128)(2,1)} %get-tuple-element.39), channel_id=1, source_target_pairs={{0,2},{1,3},{2,0},{3,1},{4,6},{5,7},{6,4},{7,5},{8,10},{9,11},{10,... | collective-permute-start | bytes 1966088 | tf_op jit(solution)/shard_map/ppermute | solution.py:55
  269.4 4.5 %copy-start.3 = (bf16[2048,1024]{0,1:T(8,128)(2,1)S(1)}, bf16[2048,1024]{0,1:T(8,128)(2,1)}, u32[]{:S(2)}) copy-start(bf16[2048,1024]{0,1:T(8,128)(2,1)} %copy-done.2) | copy-start | bytes 12582916
  269.4 5.4 %copy-start.10 = (bf16[4,256,2048]{1,2,0:T(8,128)(2,1)S(1)}, bf16[4,256,2048]{1,2,0:T(8,128)(2,1)}, u32[]{:S(2)}) copy-start(bf16[4,256,2048]{1,2,0:T(8,128)(2,1)} %copy-done.9) | copy-start | bytes 12582916
  269.4 53.4 %collective-permute-start.3 = (bf16[256,1280]{1,0:T(8,128)(2,1)}, bf16[256,1280]{1,0:T(8,128)(2,1)}, u32[]{:S(2)}, u32[]{:S(2)}) collective-permute-start(bf16[256,1280]{1,0:T(8,128)(2,1)} %get-tuple-element.37), channel_id=1, source_target_pairs={{0,1},{1,2},{2,3},{3,0},{4,5},{5,6},{6,7},{7,4},{8,9},{9,10},{10,1... | collective-permute-start | bytes 1966088 | tf_op jit(solution)/shard_map/ppermute | solution.py:55
  (6 other events, 17.5 us)
Sparse Core Ops, SparseCore 0:
  11.0 58.5 all-gather.4
  71.5 62.9 all-gather.6
  137.0 37.3 all-gather.8
  186.3 85.9 reduce-scatter.4
  275.5 51.0 reduce-scatter.2

commit v13 on v4

--- a/solution.py
+++ b/solution.py
@@ -60,8 +60,11 @@
     local_tokens = query_states.shape[0]
     query_heads = split_heads(query_states)
     local_heads = query_heads.shape[1]
-    all_keys = lax.all_gather(key_states, "seq", axis=0, tiled=True)
-    all_values = lax.all_gather(value_states, "seq", axis=0, tiled=True)
+    model_cols = key_states.shape[1]
+    packed = jnp.concatenate([key_states, value_states], axis=1)
+    all_packed = lax.all_gather(packed, "seq", axis=0, tiled=True)
+    all_keys = all_packed[:, :model_cols]
+    all_values = all_packed[:, model_cols:]
     all_pos = lax.all_gather(positions, "seq", axis=0, tiled=True)
     key_heads = split_heads(all_keys)
     value_heads = split_heads(all_values)

time: 339 us -> 322 us (0.950)
  waiting for transfers between devices: 127 us -> 108 us
  other arithmetic: 16.9 us -> 22 us
  matrix products: 79 us -> 74.4 us
    all_gather x1, waiting for transfers between devices: 52.7 us -> 34 us  [shards(): weight_full = lax.all_gather(out_weight, 'seq', axis=1, tiled=True)]
    slice x0 -> x1, local copies, waits for them, and re-layouts: none -> 7.26 us  [shards(): all_keys = all_packed[:, :model_cols]]
    all_gather x1 -> x0, local copies, waits for them, and re-layouts: 6.88 us -> none  [shards(): all_values = lax.all_gather(value_states, 'seq', axis=0, tiled=True)]
    all_gather x2 -> x1, waiting for transfers between devices: 5.45 us -> 0.02 us  [shards(): all_packed = lax.all_gather(packed, 'seq', axis=0, tiled=True)]
    reduce_sum x1, other arithmetic: 4.49 us -> 9.2 us  [shards(): jnp.sum(jnp.exp(scores - row_max[:, :, None]), axis=2)]
    dot_general x1, matrix products: 8.12 us -> 4.35 us  [shards(): jnp.einsum('hqk,qhd->khd', grad_scores, query_heads, preferred_element_ty...]
    unnamed x23 -> x32, local copies, waits for them, and re-layouts: 13.5 us -> 14 us
  transfers between devices with their start and end apart: 11 -> 10, of which waited for: 6 -> 5; matrix products, arithmetic and copies ran while one was open for 30% -> 30% of each run, Pallas kernels for 0% -> 0%
where the time goes in v13:
time: 322 us
  waiting for transfers between devices  108 us (34%)
  matrix products  74.4 us (23%)
  blocking collectives  55.3 us (17%)
  local copies, waits for them, and re-layouts  36.7 us (11%)
  other arithmetic  22 us (7%)
  between operations  14 us (4%)
  starting transfers between devices  10.9 us (3%)
    all_to_all x1, blocking collectives, shards(): cotangent_cols = lax.all_to_all(cotangent_full, 'seq', 1, 0, tiled=True)  46.2 us
    ppermute x3, waiting for transfers between devices, shift_pieces(): pieces.append(lax.ppermute(block, axis, route))  42.6 us
    all_gather x1, waiting for transfers between devices, shards(): weight_full = lax.all_gather(out_weight, 'seq', axis=1, tiled=True)  34 us
    ppermute x3, waiting for transfers between devices, permute_sum_scatter(): total = total + lax.ppermute(piece, axis, route).astype(jnp.float32)  20.1 us
    unnamed x32, local copies, waits for them, and re-layouts  14 us
    dot_general x1, matrix products, shards(): jnp.einsum('hqk,khd->qhd', weights, value_heads, preferred_element_type=j...  12.1 us
    dot_general x1, matrix products, shards(): jnp.einsum('hqk,qhd->khd', weights, grad_heads, preferred_element_type=jn...  11.5 us
    reduce_scatter x1, waiting for transfers between devices, shards(): lax.psum_scatter(both_parts, 'seq', scatter_dimension=0, tiled=True)  10.7 us
  transfers between devices with their start and end apart: 10, of which 5 were waited for; matrix products, arithmetic and copies ran while one was open for 30% of the time, Pallas kernels for 0%

profile of v13, /device:TPU:0, one launch (start us, length us, event | category | flops | bytes accessed | tf_op | source)
XLA Modules:
  0.0 321.5 jit_solution(13154463750303641087)
XLA Ops:
  12.8 5.1 %collective-permute-start.5 = (bf16[256,1280]{0,1:T(8,128)(2,1)}, bf16[256,1280]{0,1:T(8,128)(2,1)}, u32[]{:S(2)}, u32[]{:S(2)}) collective-permute-start(bf16[256,1280]{0,1:T(8,128)(2,1)} %copy.70), channel_id=1, source_target_pairs={{0,3},{1,0},{2,1},{3,2},{4,7},{5,4},{6,5},{7,6},{8,11},{9,8},{10,9... | collective-permute-start | bytes 1966088 | tf_op jit(solution)/shard_map/ppermute | solution.py:29
  18.9 9.1 %all-gather = s32[8,1,256]{2,1,0:T(1,128)S(1)} all-gather(s32[1,1,256]{2,1,0:T(1,128)S(1)} %bitcast.80), channel_id=1, replica_groups=mesh['seq'=8,'fsdp'=4] {'seq'}, dimensions={0}, use_global_device_ids=true | all-gather | bytes 9216 | tf_op jit(solution)/shard_map/all_gather | solution.py:68
  30.4 30.8 %collective-permute-done.3 = bf16[256,1280]{0,1:T(8,128)(2,1)} collective-permute-done((bf16[256,1280]{0,1:T(8,128)(2,1)}, bf16[256,1280]{0,1:T(8,128)(2,1)}, u32[]{:S(2)}, u32[]{:S(2)}) %collective-permute-start.3) | collective-permute-done | bytes 655392 | tf_op jit(solution)/shard_map/ppermute | solution.py:29
  62.4 11.8 %collective-permute-done.4 = bf16[256,1280]{0,1:T(8,128)(2,1)} collective-permute-done((bf16[256,1280]{0,1:T(8,128)(2,1)}, bf16[256,1280]{0,1:T(8,128)(2,1)}, u32[]{:S(2)}, u32[]{:S(2)}) %collective-permute-start.4) | collective-permute-done | bytes 655392 | tf_op jit(solution)/shard_map/ppermute | solution.py:29
  76.5 7.3 %fusion.9 = (bf16[2048,1024]{0,1:T(8,128)(2,1)S(1)}, bf16[2048,1024]{0,1:T(8,128)(2,1)}) fusion(bf16[2048,2048]{0,1:T(8,128)(2,1)} %all-gather.5.cloned.1.call-done), kind=kLoop, calls=%fused_computation.31 | loop fusion | bytes 16777216 | tf_op jit(solution)/shard_map/slice | solution.py:66
  83.8 7.5 %fusion.1 = (f32[8,256]{1,0:T(8,128)S(1)}, f32[8,2048,256]{2,1,0:T(8,128)}) fusion(pred[256,2048]{0,1:T(8,128)(4,1)S(1)} %copy-done.6, bf16[2048,8,128]{0,2,1:T(8,128)(2,1)S(1)} %bitcast.65, bf16[256,1024]{1,0:T(8,128)(2,1)S(1)} %copy-done), kind=kOutput, calls=%fused_computation.5 | convolution fusion | flops 1086322688 | bytes 22028288 | tf_op jit(solution)/shard_map/qhd,khd->hqk/dot_general | solution.py:17
  91.3 9.2 %exponential_reduce_fusion = f32[8,256]{1,0:T(8,128)S(1)} fusion(f32[8,2048,256]{2,1,0:T(8,128)} %get-tuple-element.35, f32[8,256]{1,0:T(8,128)S(1)} %get-tuple-element.34, pred[256,2048]{0,1:T(8,128)(4,1)} %broadcast_compare_fusion), kind=kLoop, calls=%fused_computation.3 | loop fusion | flops 16775168 | bytes 17317888 | tf_op jit(solution)/shard_map/reduce_sum | solution.py:73
  100.5 34.0 %all-gather.7.cloned.1.call-done = bf16[1024,5120]{1,0:T(8,128)(2,1)} async-done(((bf16[1024,640]{1,0:T(8,128)(2,1)}), bf16[1024,5120]{1,0:T(8,128)(2,1)}) %all-gather.7.cloned.1.call-update) | async-done | bytes 10485776 | tf_op jit(solution)/shard_map/all_gather | solution.py:81
  134.6 7.7 %convolution_convert_fusion.1 = bf16[256,1024]{1,0:T(8,128)(2,1)} fusion(bf16[256,5120]{0,1:T(8,128)(2,1)S(1)} %constant_dynamic-update-slice_fusion, bf16[1024,5120]{1,0:T(8,128)(2,1)} %all-gather.7.cloned.1.call-done), kind=kOutput, calls=%fused_computation.12 | convolution fusion | flops 2684616704 | bytes 13631488 | tf_op jit(solution)/shard_map/td,hd->th/dot_general | solution.py:87
  143.5 12.1 %multiply_reduce_fusion = (f32[256,8]{0,1:T(8,128)S(1)}, bf16[8,128,256]{2,1,0:T(8,128)(2,1)}) fusion(bf16[256,1024]{0,1:T(8,128)(2,1)S(1)} %copy.74, bf16[2048,8,128]{0,2,1:T(8,128)(2,1)} %bitcast.72, f32[8,2048,256]{2,1,0:T(8,128)} %get-tuple-element.35, f32[8,256]{1,0:T(8,128)S(1)} %log_add_fusion, pred[256,2048]{0,1:T(8,128)(4,1)} %broadcast_compare_fusion), kind=kOutput, calls=%fused_computation.16 | convolution fusion | flops 1091827712 | bytes 22560768 | tf_op jit(solution)/shard_map/hqk,khd->qhd/dot_general | solution.py:76
  156.0 7.2 %convolution_convert_fusion = bf16[256,5120]{1,0:T(8,128)(2,1)S(1)} fusion(bf16[256,1024]{0,1:T(8,128)(2,1)} %bitcast.75, bf16[1024,5120]{1,0:T(8,128)(2,1)} %all-gather.7.cloned.1.call-done), kind=kOutput, calls=%fused_computation.7 | convolution fusion | flops 2685665280 | bytes 13631488 | tf_op jit(solution)/shard_map/dot_general | solution.py:82
  167.1 2.3 collective-permute-start.2
  170.1 11.5 %convert_bitcast_fusion = bf16[2048,8,128]{2,0,1:T(8,128)(2,1)} fusion(bf16[256,8,128]{0,2,1:T(8,128)(2,1)S(1)} %bitcast.78, f32[8,2048,256]{2,1,0:T(8,128)} %get-tuple-element.35, f32[8,256]{1,0:T(8,128)S(1)} %log_add_fusion, pred[256,2048]{0,1:T(8,128)(4,1)S(1)} %copy-done.7), kind=kOutput, calls=%fused_computation.8 | convolution fusion | flops 1092616192 | bytes 22028288 | tf_op jit(solution)/shard_map/hqk,qhd->khd/dot_general | solution.py:109
  181.6 10.1 %multiply_convert_fusion = bf16[8,256,2048]{1,2,0:T(8,128)(2,1)S(1)} fusion(f32[8,2048,256]{2,1,0:T(8,128)} %get-tuple-element.35, f32[8,256]{1,0:T(8,128)S(1)} %bitcast.81, f32[8,256]{1,0:T(8,128)S(1)} %log_add_fusion, pred[256,2048]{0,1:T(8,128)(4,1)S(1)} %copy-done.7, bf16[256,8,128]{0,2,1:T(8,128)(2,1)} %bitcast.77, bf16[2048,8,128]{0,2,1:T(8,128)(2,1)} %bitcast.73), kind=kOutput, calls=%fused_computation.1 | convolution fusion | flops 1098907648 | bytes 30425088 | tf_op jit(solution)/shard_map/qhd,khd->hqk/dot_general | solution.py:99
  191.7 3.2 copy-done.2
  194.9 4.3 %convert_bitcast_fusion.1 = bf16[2048,8,128]{2,0,1:T(8,128)(2,1)} fusion(bf16[8,256,2048]{1,2,0:T(8,128)(2,1)S(1)} %multiply_convert_fusion, bf16[256,1024]{1,0:T(8,128)(2,1)S(1)} %copy-done), kind=kOutput, calls=%fused_computation.9 | convolution fusion | flops 1075838976 | bytes 13107200 | tf_op jit(solution)/shard_map/hqk,qhd->khd/dot_general | solution.py:106
  199.3 7.4 %pad_maximum_fusion = bf16[2048,16,128]{2,0,1:T(8,128)(2,1)} fusion(bf16[2048,8,128]{2,0,1:T(8,128)(2,1)} %convert_bitcast_fusion, bf16[2048,8,128]{2,0,1:T(8,128)(2,1)} %convert_bitcast_fusion.1), kind=kLoop, calls=%fused_computation.6 | loop fusion | flops 4194304 | bytes 16777216 | tf_op jit(solution)/shard_map/concatenate | solution.py:112
  206.7 20.1 %collective-permute-done.1 = bf16[256,1280]{1,0:T(8,128)(2,1)} collective-permute-done((bf16[256,1280]{1,0:T(8,128)(2,1)S(1)}, bf16[256,1280]{1,0:T(8,128)(2,1)}, u32[]{:S(2)}, u32[]{:S(2)}) %collective-permute-start.1) | collective-permute-done | bytes 655392 | tf_op jit(solution)/shard_map/ppermute | solution.py:55
  226.8 2.8 convert_add_fusion
  231.4 46.2 %all_to_all.19 = bf16[256,8,640]{0,2,1:T(8,128)(2,1)} all-to-all(bf16[256,8,640]{0,2,1:T(8,128)(2,1)S(1)} %bitcast.67), channel_id=1, replica_groups=mesh['seq'=8,'fsdp'=4] {'seq'}, dimensions={1} | all-to-all | bytes 5242880 | tf_op jit(solution)/shard_map/all_to_all | solution.py:91
  277.6 4.4 %copy.84 = bf16[8,256,640]{2,1,0:T(8,128)(2,1)} copy(bf16[8,256,640]{1,2,0:T(8,128)(2,1)} %bitcast.68) | data formatting | bytes 5242880 | tf_op jit(solution)/shard_map/all_to_all | solution.py:91
  282.0 6.0 %convolution_multiply_fusion = f32[8,128,256]{2,1,0:T(8,128)S(1)} fusion(bf16[2048,8,128]{0,2,1:T(8,128)(2,1)} %bitcast.66, bf16[8,256,2048]{1,2,0:T(8,128)(2,1)} %copy-done.2), kind=kOutput, calls=%fused_computation.10 | convolution fusion | flops 1074003968 | bytes 13631488 | tf_op jit(solution)/shard_map/hqk,khd->qhd/dot_general | solution.py:103
  289.4 7.9 %fusion.10 = f32[1024,640]{1,0:T(8,128)} fusion(bf16[2048,1024]{0,1:T(8,128)(2,1)} %all-gather.9.cloned.1.call-done, bf16[2048,640]{1,0:T(8,128)(2,1)} %bitcast.76), kind=kOutput, calls=%fused_computation.32 | convolution fusion | flops 2684354560 | bytes 9437184 | tf_op jit(solution)/shard_map/th,td->hd/dot_general | solution.py:92
  297.3 10.7 %reduce-scatter.2.cloned.1.call-done = bf16[256,16,128]{2,0,1:T(8,128)(2,1)} async-done(((bf16[2048,16,128]{2,0,1:T(8,128)(2,1)}), bf16[256,16,128]{2,0,1:T(8,128)(2,1)}) %reduce-scatter.2.cloned.1.call-update) | async-done | bytes 1048592 | tf_op jit(solution)/shard_map/reduce_scatter | solution.py:114
  (63 shorter events, 28.6 us)
Async XLA Ops:
  7.2 76.6 %copy-start = (bf16[256,1024]{1,0:T(8,128)(2,1)S(1)}, bf16[256,1024]{1,0:T(8,128)(2,1)}, u32[]{:S(2)}) copy-start(bf16[256,1024]{1,0:T(8,128)(2,1)} %param.6) | copy-start | bytes 1572868
  7.2 4.5 %copy-start.9 = (bf16[256,1280]{1,0:T(8,128)(2,1)S(1)}, bf16[256,1280]{1,0:T(8,128)(2,1)}, u32[]{:S(2)}) copy-start(bf16[256,1280]{1,0:T(8,128)(2,1)} %param.11) | copy-start | bytes 1966084
  7.2 11.7 %copy-start.12 = (s32[256]{0:T(256)S(1)}, s32[256]{0:T(256)}, u32[]{:S(2)}) copy-start(s32[256]{0:T(256)} %param.9) | copy-start | bytes 3076
  7.2 69.3 %all-gather.5.cloned.1.call-start = ((), (), s32[]{:S(2)}) async-start(), calls=%async_computation.2 | async-start | bytes 9437184 | tf_op jit(solution)/shard_map/all_gather | solution.py:65
  10.9 123.7 %all-gather.7.cloned.1.call-start = ((), (), s32[]{:S(2)}) async-start(), calls=%async_computation.3 | async-start | bytes 11796480 | tf_op jit(solution)/shard_map/all_gather | solution.py:81
  11.6 277.7 %all-gather.9.cloned.1.call-start = ((), (), s32[]{:S(2)}) async-start(), calls=%async_computation.5 | async-start | bytes 4718592 | tf_op jit(solution)/shard_map/all_gather | solution.py:90
  12.8 62.5 %collective-permute-start.5 = (bf16[256,1280]{0,1:T(8,128)(2,1)}, bf16[256,1280]{0,1:T(8,128)(2,1)}, u32[]{:S(2)}, u32[]{:S(2)}) collective-permute-start(bf16[256,1280]{0,1:T(8,128)(2,1)} %copy.70), channel_id=1, source_target_pairs={{0,3},{1,0},{2,1},{3,2},{4,7},{5,4},{6,5},{7,6},{8,11},{9,8},{10,9... | collective-permute-start | bytes 1966088 | tf_op jit(solution)/shard_map/ppermute | solution.py:29
  17.9 56.3 %collective-permute-start.4 = (bf16[256,1280]{0,1:T(8,128)(2,1)}, bf16[256,1280]{0,1:T(8,128)(2,1)}, u32[]{:S(2)}, u32[]{:S(2)}) collective-permute-start(bf16[256,1280]{0,1:T(8,128)(2,1)} %copy.70), channel_id=1, source_target_pairs={{0,2},{1,3},{2,0},{3,1},{4,6},{5,7},{6,4},{7,5},{8,10},{9,11},{10,... | collective-permute-start | bytes 1966088 | tf_op jit(solution)/shard_map/ppermute | solution.py:29
  17.9 43.4 %collective-permute-start.3 = (bf16[256,1280]{0,1:T(8,128)(2,1)}, bf16[256,1280]{0,1:T(8,128)(2,1)}, u32[]{:S(2)}, u32[]{:S(2)}) collective-permute-start(bf16[256,1280]{0,1:T(8,128)(2,1)} %copy.70), channel_id=1, source_target_pairs={{0,1},{1,2},{2,3},{3,0},{4,5},{5,6},{6,7},{7,4},{8,9},{9,10},{10,1... | collective-permute-start | bytes 1966088 | tf_op jit(solution)/shard_map/ppermute | solution.py:29
  76.5 58.1 %copy-start.4 = (bf16[256,5120]{0,1:T(8,128)(2,1)}, bf16[256,5120]{0,1:T(8,128)(2,1)S(1)}, u32[]{:S(2)}) copy-start(bf16[256,5120]{0,1:T(8,128)(2,1)S(1)} %constant_dynamic-update-slice_fusion) | copy-start | bytes 7864324
  76.5 7.3 %copy-start.6 = (pred[256,2048]{0,1:T(8,128)(4,1)S(1)}, pred[256,2048]{0,1:T(8,128)(4,1)}, u32[]{:S(2)}) copy-start(pred[256,2048]{0,1:T(8,128)(4,1)} %broadcast_compare_fusion) | copy-start | bytes 1572868
  83.8 7.5 %copy-start.1 = (bf16[2048,1024]{0,1:T(8,128)(2,1)}, bf16[2048,1024]{0,1:T(8,128)(2,1)S(1)}, u32[]{:S(2)}) copy-start(bf16[2048,1024]{0,1:T(8,128)(2,1)S(1)} %get-tuple-element.29) | copy-start | bytes 12582916
  143.5 12.1 %copy-start.10 = (bf16[256,1024]{0,1:T(8,128)(2,1)}, bf16[256,1024]{0,1:T(8,128)(2,1)S(1)}, u32[]{:S(2)}) copy-start(bf16[256,1024]{0,1:T(8,128)(2,1)S(1)} %copy.74) | copy-start | bytes 1572868
  155.7 152.3 %reduce-scatter.2.cloned.1.call-start = ((), (), s32[]{:S(2)}) async-start(), calls=%async_computation.4 | async-start | bytes 9437184 | tf_op jit(solution)/shard_map/reduce_scatter | solution.py:114
  156.0 14.1 %copy-start.7 = (pred[256,2048]{0,1:T(8,128)(4,1)S(1)}, pred[256,2048]{0,1:T(8,128)(4,1)}, u32[]{:S(2)}) copy-start(pred[256,2048]{0,1:T(8,128)(4,1)} %broadcast_compare_fusion) | copy-start | bytes 1572868
  156.0 14.1 %copy-start.11 = (bf16[256,1024]{0,1:T(8,128)(2,1)S(1)}, bf16[256,1024]{0,1:T(8,128)(2,1)}, u32[]{:S(2)}) copy-start(bf16[256,1024]{0,1:T(8,128)(2,1)} %copy-done.10) | copy-start | bytes 1572868
  163.2 1.5 copy-start.3
  165.6 41.1 %collective-permute-start = (bf16[256,1280]{1,0:T(8,128)(2,1)}, bf16[256,1280]{1,0:T(8,128)(2,1)S(1)}, u32[]{:S(2)}, u32[]{:S(2)}) collective-permute-start(bf16[256,1280]{1,0:T(8,128)(2,1)} %get-tuple-element.31), channel_id=1, source_target_pairs={{0,1},{1,2},{2,3},{3,0},{4,5},{5,6},{6,7},{7,4},{8,9},{9,10},{10,1... | collective-permute-start | bytes 1966088 | tf_op jit(solution)/shard_map/ppermute | solution.py:55
  167.1 39.6 %collective-permute-start.2 = (bf16[256,1280]{1,0:T(8,128)(2,1)S(1)}, bf16[256,1280]{1,0:T(8,128)(2,1)}, u32[]{:S(2)}, u32[]{:S(2)}) collective-permute-start(bf16[256,1280]{1,0:T(8,128)(2,1)S(1)} %get-tuple-element.32), channel_id=1, source_target_pairs={{0,3},{1,0},{2,1},{3,2},{4,7},{5,4},{6,5},{7,6},{8,11},{9,8},{10,9... | collective-permute-start | bytes 1966088 | tf_op jit(solution)/shard_map/ppermute | solution.py:55
  169.5 57.3 %collective-permute-start.1 = (bf16[256,1280]{1,0:T(8,128)(2,1)S(1)}, bf16[256,1280]{1,0:T(8,128)(2,1)}, u32[]{:S(2)}, u32[]{:S(2)}) collective-permute-start(bf16[256,1280]{1,0:T(8,128)(2,1)S(1)} %get-tuple-element.33), channel_id=1, source_target_pairs={{0,2},{1,3},{2,0},{3,1},{4,6},{5,7},{6,4},{7,5},{8,10},{9,11},{10,... | collective-permute-start | bytes 1966088 | tf_op jit(solution)/shard_map/ppermute | solution.py:55
  191.7 3.2 %copy-start.2 = (bf16[8,256,2048]{1,2,0:T(8,128)(2,1)}, bf16[8,256,2048]{1,2,0:T(8,128)(2,1)S(1)}, u32[]{:S(2)}) copy-start(bf16[8,256,2048]{1,2,0:T(8,128)(2,1)S(1)} %multiply_convert_fusion) | copy-start | bytes 25165828
  229.6 1.7 copy-start.5
  308.0 5.0 %copy-start.8 = (bf16[256,16,128]{2,0,1:T(8,128)(2,1)S(1)}, bf16[256,16,128]{2,0,1:T(8,128)(2,1)}, u32[]{:S(2)}) copy-start(bf16[256,16,128]{2,0,1:T(8,128)(2,1)} %reduce-scatter.2.cloned.1.call-done) | copy-start | bytes 3145732
Sparse Core Ops, SparseCore 0:
  11.0 58.5 all-gather.4
  71.5 62.9 all-gather.6
  155.8 37.3 all-gather.8
  229.8 78.1 reduce-scatter.1
